TPU v7x, 32 devices: a whole 2x2x4 slice. The times are simulated.
32 devices in a mesh: grp: 4 (over z), mem: 8 (over y, x, core).
Axes of the slice: x: 2, y: 2, z: 4, core: 2. Of those that a mesh axis runs over, the one named last changes fastest.
Arguments:
- design: bfloat16 [8192, 1024], P(('grp', 'mem'))
- active_blocks: int32 [32, 8], P(('grp', 'mem')), may hold values from 0 to 31, as said below
- ridge: float32 [4096], replicated, may hold values from 0.5 to 2
Outputs:
- factored: float32 [8, 128, 128, 128], P('mem', 'grp')
Inputs may be any that keep to these rules, and one draw needn't show every extreme that they name: active_blocks[d, a] % 8 == a for every device d and position a, so a device's blocks are distinct.
All inputs are finite; a program needn't handle non-finite values.
Results may differ from a plain program's by a relative error of at most 0.0003.
Values sent between devices are 32-bit elements; how exact they have to be, the bound alone decides.
No kernel may reach another device: no remote copies, remote signals or barrier semaphores. Data moves between devices by JAX's collectives and lax.ppermute only.
A program may use at most 64 MiB of HBM per device.

v0:
```python
import jax
import jax.numpy as jnp
from jax import lax
from jax.sharding import PartitionSpec as P

NB = 32
BLK = 128
ACT = 8


def panel_solve(column):
    count = column.shape[0]
    chol = jnp.linalg.cholesky(column[0])
    stacked = jnp.transpose(column, (2, 0, 1)).reshape(BLK, count * BLK)
    solved = lax.linalg.triangular_solve(chol, stacked, left_side=True, lower=True)
    lower_col = jnp.transpose(solved.reshape(BLK, count, BLK), (1, 2, 0))
    return lower_col.at[0].set(chol)


def apply_step(tiles, lower_col, step, tile_rows, tile_cols):
    left_tiles = jnp.take(lower_col, jnp.maximum(tile_rows - step, 0), axis=0)
    right_tiles = jnp.take(lower_col, jnp.maximum(tile_cols - step, 0), axis=0)
    update = jnp.einsum("tpr,tqr->tpq", left_tiles, right_tiles, precision=lax.Precision.HIGHEST)
    trailing = ((tile_rows > step) & (tile_cols > step))[:, None, None]
    on_column = ((tile_cols == step) & (tile_rows >= step))[:, None, None]
    on_row = ((tile_rows == step) & (tile_cols > step))[:, None, None]
    tiles = jnp.where(trailing, tiles - update, tiles)
    tiles = jnp.where(on_column, left_tiles, tiles)
    tiles = jnp.where(on_row, jnp.transpose(right_tiles, (0, 2, 1)), tiles)
    return tiles


def column_picker(step, tile_rows, tile_cols):
    wanted = step + jnp.arange(NB - step, dtype=jnp.int32)
    inside = (tile_cols == step) & (tile_rows >= step)
    return ((tile_rows[None, :] == wanted[:, None]) & inside[None, :]).astype(jnp.float32)


def on_device(design, active_blocks, ridge):
    n_mem = lax.axis_size("mem")
    n_grp = lax.axis_size("grp")
    member = lax.axis_index("mem")
    group = lax.axis_index("grp")
    classes = n_mem // 8
    per_pos = ACT // classes
    per_row = NB // ACT
    slot_count = NB // classes * per_row
    owned_count = slot_count // n_grp
    row_count = design.shape[0]
    residue = member // 8
    position = member % 8
    everyone = lax.all_gather(active_blocks, "mem", axis=0, tiled=True)
    blocks = design.reshape(row_count, ACT, BLK)
    left = blocks.reshape(row_count, per_pos, classes, BLK)
    outgoing = jnp.einsum("ncqk,nbl->qbckl", left, blocks, preferred_element_type=jnp.float32)
    outgoing = outgoing.reshape(n_mem, per_pos, BLK, BLK)
    received = lax.all_to_all(outgoing, "mem", split_axis=0, concat_axis=0, tiled=True)
    row_ids = jnp.take(everyone.reshape(n_mem, per_pos, classes), residue, axis=2)
    col_ids = jnp.take(everyone, position, axis=1)
    targets = row_ids // classes * per_row + (col_ids // 8)[:, None]
    onehot = (
        targets.reshape(-1)[None, :] == jnp.arange(slot_count, dtype=jnp.int32)[:, None]
    ).astype(jnp.float32)
    sums = jnp.dot(
        onehot,
        received.reshape(n_mem * per_pos, BLK * BLK),
        precision=lax.Precision.HIGHEST,
        preferred_element_type=jnp.float32,
    )
    sums = sums.reshape(slot_count, BLK, BLK)
    owned = lax.psum_scatter(sums, "grp", scatter_dimension=0, tiled=True)
    slots = group * owned_count + jnp.arange(owned_count, dtype=jnp.int32)
    tile_rows = slots // per_row * classes + residue
    tile_cols = slots % per_row * 8 + position
    ridge_blocks = jnp.take(ridge.reshape(NB, BLK), tile_rows, axis=0)
    same = (tile_rows == tile_cols).astype(jnp.float32)
    extra = jnp.eye(BLK, dtype=jnp.float32)[None] * ridge_blocks[:, None, :] * same[:, None, None]
    divisor = jnp.float32(row_count * n_grp * n_mem // 16)
    tiles = owned / divisor + extra
    picker = column_picker(0, tile_rows, tile_cols)
    partial_value = jnp.einsum("it,tpq->ipq", picker, tiles, precision=lax.Precision.HIGHEST)
    column = lax.psum(partial_value, ("grp", "mem"))
    lower_col = panel_solve(column)
    tiles = apply_step(tiles, lower_col, 0, tile_rows, tile_cols)
    return tiles[None]


def solution(mesh):
    in_specs = (P(("grp", "mem"), None), P(("grp", "mem"), None), P())
    out_specs = P("mem", "grp", None, None)
    return jax.shard_map(
        on_device, mesh=mesh, in_specs=in_specs, out_specs=out_specs, check_vma=False
    )
```

profile of v0, /device:TPU:0, one launch (start us, length us, event | category | flops | bytes accessed | tf_op | source)
XLA Modules:
  0.0 429.8 jit_solution(17097673286191930407)
XLA Ops:
  6.5 0.0 copy-start
  6.5 1.1 copy.49
  7.7 3.8 convolution_bitcast_fusion
  11.4 0.0 copy-start.4
  11.4 5.3 %all-to-all-start = ((f32[8,8,128,128]{2,3,1,0:T(8,128)}), f32[8,8,128,128]{2,3,1,0:T(8,128)}, u32[]{:S(2)}, u32[]{:S(2)}) async-start(f32[8,8,128,128]{2,3,1,0:T(8,128)} %convolution_bitcast_fusion), calls=%async_computation | async-start | bytes 8388608 | tf_op jit(solution)/shard_map/all_to_all | solution.py:57
  16.7 0.0 reduce-scatter.2.cloned.1.call-start
  16.8 0.0 copy-done.4
  16.8 52.0 %all-gather = s32[8,1,8]{2,1,0:T(1,128)S(1)} all-gather(s32[1,1,8]{2,1,0:T(1,128)S(1)} %bitcast.80), channel_id=1, replica_groups=mesh['grp'=4,'mem'=8] {'mem'}, dimensions={0}, use_global_device_ids=true | all-gather | bytes 288 | tf_op jit(solution)/shard_map/all_gather | solution.py:52
  68.9 0.3 fusion.29
  69.2 0.1 bitcast_add_fusion.1
  69.3 0.1 add.248
  69.3 0.0 all-to-all-done
  69.4 5.4 %copy.30 = f32[8,8,128,128]{3,2,1,0:T(8,128)} copy(f32[8,8,128,128]{2,3,1,0:T(8,128)} %all-to-all-done) | data formatting | bytes 8388608 | tf_op jit(solution)/shard_map/all_to_all | solution.py:57
  74.7 11.4 %fusion = f32[128,128,128]{2,0,1:T(8,128)} fusion(s32[64]{0:T(128)S(1)} %add.248, f32[8,8,128,128]{3,2,1,0:T(8,128)} %copy.30), kind=kOutput, calls=%fused_computation.4 | convolution fusion | flops 1610620928 | bytes 12583168 | tf_op jit(solution)/shard_map/dot_general | solution.py:64
  86.2 0.0 reduce-scatter.2.cloned.1.call-update
  86.2 0.2 all-reduce.2.cloned.1.call-start
  86.4 0.0 copy-done
  86.5 0.6 gather_fusion
  87.1 0.1 broadcast_select_fusion.1
  87.2 143.8 %reduce-scatter.2.cloned.1.call-done = f32[32,128,128]{2,0,1:T(8,128)} async-done(((f32[128,128,128]{2,0,1:T(8,128)}), f32[32,128,128]{2,0,1:T(8,128)}) %reduce-scatter.2.cloned.1.call-update) | async-done | bytes 2097168 | tf_op jit(solution)/shard_map/reduce_scatter | solution.py:71
  231.0 3.0 fusion.11
  234.0 1.9 copy.32
  235.8 0.0 all-reduce.2.cloned.1.call-update
  235.9 135.0 %all-reduce.2.cloned.1.call-done = f32[32,128,128]{1,2,0:T(8,128)} async-done(((f32[32,128,128]{1,2,0:T(8,128)}), f32[32,128,128]{1,2,0:T(8,128)}) %all-reduce.2.cloned.1.call-update) | async-done | bytes 2097168 | tf_op jit(solution)/shard_map/psum | solution.py:82
  370.9 0.8 slice_bitcast_fusion
  371.7 0.1 copy.34
  371.8 0.9 fusion.19
  372.7 11.7 %cholesky.14 = f32[128,128]{1,0:T(8,128)S(1)} custom-call(f32[128,128]{1,0:T(8,128)S(1)} %fusion.19), custom_call_target="Cholesky" | custom-call | tf_op jit(solution)/shard_map/jit(cholesky)/cholesky | solution.py:13
  384.4 0.6 compare_reduce_fusion
  385.1 0.6 select_bitcast_fusion
  385.7 9.8 %custom-call.6 = f32[1,128,128]{1,2,0:T(8,128)S(1)} custom-call(f32[1,128,128]{2,1,0:T(8,128)S(1)} %select_bitcast_fusion), custom_call_target="InvertDiagBlocksLowerTriangular" | custom-call | tf_op jit(solution)/shard_map/triangular_solve | solution.py:15
  395.5 2.9 copy.33
  398.4 3.4 fusion.6
  401.8 0.6 bitcast_dynamic-update-slice_fusion
  402.4 2.0 gather_fusion.1
  404.4 3.1 copy.36
  407.5 2.0 gather_fusion.2
  409.5 0.0 copy-start.2
  409.5 2.0 broadcast_select_fusion
  411.6 0.2 copy-done.2
  411.8 1.3 copy_select_fusion
  413.1 0.0 copy-start.1
  413.1 0.0 copy-start.3
  413.1 4.5 %fusion.8 = f32[32,128,128]{2,1,0:T(8,128)S(1)} fusion(f32[32,128,128]{1,0,2:T(8,128)S(1)} %broadcast_select_fusion, f32[32,128,128]{2,0,1:T(8,128)S(1)} %copy_select_fusion), kind=kOutput, calls=%fused_computation.14 | convolution fusion | flops 805306368 | bytes 6291456 | tf_op jit(solution)/shard_map/tpr,tqr->tpq/dot_general | solution.py:23
  417.7 0.0 copy-done.1
  417.7 0.0 copy-done.3
  417.7 2.7 fusion.5
  420.4 2.5 copy.41
  (10 shorter events, 0.1 us)
Async XLA Ops:
  6.5 79.9 %copy-start = (f32[4096]{0:T(1024)S(1)}, f32[4096]{0:T(1024)}, u32[]{:S(2)}) copy-start(f32[4096]{0:T(1024)} %param.9) | copy-start | bytes 49156
  11.4 5.4 %copy-start.4 = (s32[1,8]{1,0:T(1,128)S(1)}, s32[1,8]{1,0:T(1,128)}, u32[]{:S(2)}) copy-start(s32[1,8]{1,0:T(1,128)} %param.8) | copy-start | bytes 100
  11.4 57.9 %all-to-all-start = ((f32[8,8,128,128]{2,3,1,0:T(8,128)}), f32[8,8,128,128]{2,3,1,0:T(8,128)}, u32[]{:S(2)}, u32[]{:S(2)}) async-start(f32[8,8,128,128]{2,3,1,0:T(8,128)} %convolution_bitcast_fusion), calls=%async_computation | async-start | bytes 8388608 | tf_op jit(solution)/shard_map/all_to_all | solution.py:57
  16.7 214.2 %reduce-scatter.2.cloned.1.call-start = ((), (), s32[]{:S(2)}) async-start(), calls=%async_computation.2 | async-start | bytes 10485760 | tf_op jit(solution)/shard_map/reduce_scatter | solution.py:71
  86.2 284.7 %all-reduce.2.cloned.1.call-start = ((), (), s32[]{:S(2)}) async-start(), calls=%async_computation.3 | async-start | bytes 4194304 | tf_op jit(solution)/shard_map/psum | solution.py:82
  409.5 2.2 copy-start.2
  413.1 4.6 %copy-start.1 = (f32[32,128,128]{1,0,2:T(8,128)S(1)}, f32[32,128,128]{1,0,2:T(8,128)}, u32[]{:S(2)}) copy-start(f32[32,128,128]{1,0,2:T(8,128)} %copy.36) | copy-start | bytes 6291460
  413.1 4.6 %copy-start.3 = (f32[32,128,128]{2,0,1:T(8,128)S(1)}, f32[32,128,128]{2,0,1:T(8,128)}, u32[]{:S(2)}) copy-start(f32[32,128,128]{2,0,1:T(8,128)} %reduce-scatter.2.cloned.1.call-done) | copy-start | bytes 6291460
Sparse Core Ops, SparseCore 0:
  86.3 144.6 reduce-scatter.1
  236.3 134.5 all-reduce.1
where the time goes:
time: 430 us
  waiting for transfers between devices  279 us (65%)
  blocking collectives  52 us (12%)
  other arithmetic  30.9 us (7%)
  matrix products  26.1 us (6%)
  local copies, waits for them, and re-layouts  22.7 us (5%)
  between operations  13.7 us (3%)
  starting transfers between devices  5.56 us (1%)
    reduce_scatter x1, waiting for transfers between devices, on_device(): owned = lax.psum_scatter(sums, 'grp', scatter_dimension=0, tiled=True)  144 us
    psum x1, waiting for transfers between devices, on_device(): column = lax.psum(partial_value, ('grp', 'mem'))  135 us
    all_gather x1, blocking collectives, on_device(): everyone = lax.all_gather(active_blocks, 'mem', axis=0, tiled=True)  52 us
    another operation x3, other arithmetic, panel_solve(): chol = jnp.linalg.cholesky(column[0])  12.4 us
    dot_general x1, matrix products, on_device(): jnp.dot(onehot, received.reshape(n_mem * per_pos, BLK * BLK), precision=l...  11.4 us
    another operation x2, other arithmetic, panel_solve(): lax.linalg.triangular_solve(chol, stacked, left_side=True, lower=True)  10.4 us
  transfers between devices with their start and end apart: 3, of which 2 were waited for; matrix products, arithmetic and copies ran while one was open for 0% of the time, Pallas kernels for 0%

commit v1 on v0

--- a/solution.py
+++ b/solution.py
@@ -6,6 +6,7 @@
 NB = 32
 BLK = 128
 ACT = 8
+HI = lax.Precision.HIGHEST
 
 
 def panel_solve(column):
@@ -20,7 +21,7 @@
 def apply_step(tiles, lower_col, step, tile_rows, tile_cols):
     left_tiles = jnp.take(lower_col, jnp.maximum(tile_rows - step, 0), axis=0)
     right_tiles = jnp.take(lower_col, jnp.maximum(tile_cols - step, 0), axis=0)
-    update = jnp.einsum("tpr,tqr->tpq", left_tiles, right_tiles, precision=lax.Precision.HIGHEST)
+    update = jnp.einsum("tpr,tqr->tpq", left_tiles, right_tiles, precision=HI)
     trailing = ((tile_rows > step) & (tile_cols > step))[:, None, None]
     on_column = ((tile_cols == step) & (tile_rows >= step))[:, None, None]
     on_row = ((tile_rows == step) & (tile_cols > step))[:, None, None]
@@ -36,7 +37,7 @@
     return ((tile_rows[None, :] == wanted[:, None]) & inside[None, :]).astype(jnp.float32)
 
 
-def on_device(design, active_blocks, ridge):
+def on_device_general(design, active_blocks, ridge):
     n_mem = lax.axis_size("mem")
     n_grp = lax.axis_size("grp")
     member = lax.axis_index("mem")
@@ -64,7 +65,7 @@
     sums = jnp.dot(
         onehot,
         received.reshape(n_mem * per_pos, BLK * BLK),
-        precision=lax.Precision.HIGHEST,
+        precision=HI,
         preferred_element_type=jnp.float32,
     )
     sums = sums.reshape(slot_count, BLK, BLK)
@@ -78,16 +79,93 @@
     divisor = jnp.float32(row_count * n_grp * n_mem // 16)
     tiles = owned / divisor + extra
     picker = column_picker(0, tile_rows, tile_cols)
-    partial_value = jnp.einsum("it,tpq->ipq", picker, tiles, precision=lax.Precision.HIGHEST)
+    partial_value = jnp.einsum("it,tpq->ipq", picker, tiles, precision=HI)
     column = lax.psum(partial_value, ("grp", "mem"))
     lower_col = panel_solve(column)
     tiles = apply_step(tiles, lower_col, 0, tile_rows, tile_cols)
     return tiles[None]
 
 
+def on_device_fast(design, active_blocks, ridge):
+    n_mem = lax.axis_size("mem")
+    n_grp = lax.axis_size("grp")
+    member = lax.axis_index("mem")
+    group = lax.axis_index("grp")
+    per_row = NB // ACT
+    row_count = design.shape[0]
+    divisor = jnp.float32(row_count * n_grp * n_mem // 16)
+    eye = jnp.eye(BLK, dtype=jnp.float32)
+    ridge_blocks = ridge.reshape(NB, BLK)
+
+    everyone = lax.all_gather(active_blocks, "mem", axis=0, tiled=True)
+    blocks = design.reshape(row_count, ACT, BLK)
+    outgoing = jnp.einsum("nak,nbl->bakl", blocks, blocks, preferred_element_type=jnp.float32)
+
+    mine00 = jnp.where(active_blocks[0, 0] == 0, outgoing[0, 0], 0.0)
+    gram00 = lax.psum(mine00, ("grp", "mem"))
+    a00 = gram00 / divisor + eye * ridge_blocks[0][None, :]
+    chol = jnp.linalg.cholesky(a00)
+    chol_inv = lax.linalg.triangular_solve(chol, eye, left_side=True, lower=True)
+
+    received = lax.all_to_all(outgoing, "mem", split_axis=0, concat_axis=0, tiled=True)
+    received = received.reshape(n_mem, ACT, BLK, BLK)
+
+    row_grp = everyone // 8
+    col_grp = jnp.take(everyone, member, axis=1) // 8
+    grp_ids = jnp.arange(n_grp, dtype=jnp.int32)
+    q_ids = jnp.arange(per_row, dtype=jnp.int32)
+    mask = (
+        (row_grp[:, :, None, None] == grp_ids[None, None, :, None])
+        & (col_grp[:, None, None, None] == q_ids[None, None, None, :])
+    ).astype(jnp.float32)
+    main = jnp.einsum("sagq,sakl->gaqkl", mask, received, precision=HI)
+    main = main.reshape(n_grp, ACT * per_row, BLK, BLK)
+    col_mask = (
+        (col_grp[:, None] == grp_ids[None, :]) & (everyone[:, 0:1] == 0)
+    ).astype(jnp.float32)
+    col_part = jnp.einsum("sg,slk->gkl", col_mask, received[:, 0], precision=HI)
+    send = jnp.concatenate([main, col_part[:, None]], axis=1)
+    send = send.reshape(n_grp * (ACT * per_row + 1), BLK, BLK)
+    got = lax.psum_scatter(send, "grp", scatter_dimension=0, tiled=True)
+    owned = got[: ACT * per_row]
+    col_tile = got[ACT * per_row] / divisor
+
+    t = jnp.arange(ACT * per_row, dtype=jnp.int32)
+    tile_rows = group * 8 + t // per_row
+    tile_cols = (t % per_row) * 8 + member
+    same = (tile_rows == tile_cols).astype(jnp.float32)
+    diag = eye[None] * jnp.take(ridge_blocks, tile_rows, axis=0)[:, None, :] * same[:, None, None]
+    tiles = owned / divisor + diag
+
+    col_rows = lax.all_gather(col_tile, "mem", axis=0, tiled=False)
+    col_cols = lax.all_gather(col_tile, "grp", axis=0, tiled=False)
+    p_rows = jnp.einsum("ipr,qr->ipq", col_rows, chol_inv, precision=HI)
+    p_cols = jnp.einsum("ipr,qr->ipq", col_cols, chol_inv, precision=HI)
+    row_ids = group * 8 + jnp.arange(8, dtype=jnp.int32)
+    col_ids = jnp.arange(per_row, dtype=jnp.int32) * 8 + member
+    p_rows = jnp.where((row_ids == 0)[:, None, None], chol[None], p_rows)
+    p_cols = jnp.where((col_ids == 0)[:, None, None], chol[None], p_cols)
+
+    update = jnp.einsum("apr,qsr->aqps", p_rows, p_cols, precision=HI)
+    update = update.reshape(ACT * per_row, BLK, BLK)
+    left_tiles = jnp.repeat(p_rows, per_row, axis=0)
+    right_tiles = jnp.tile(p_cols, (ACT, 1, 1))
+    trailing = ((tile_rows > 0) & (tile_cols > 0))[:, None, None]
+    on_column = (tile_cols == 0)[:, None, None]
+    on_row = ((tile_rows == 0) & (tile_cols > 0))[:, None, None]
+    tiles = jnp.where(trailing, tiles - update, tiles)
+    tiles = jnp.where(on_column, left_tiles, tiles)
+    tiles = jnp.where(on_row, jnp.transpose(right_tiles, (0, 2, 1)), tiles)
+    return tiles[None]
+
+
 def solution(mesh):
+    n_mem = mesh.shape["mem"]
+    n_grp = mesh.shape["grp"]
+    fast = n_mem == 8 and n_grp * 8 == NB
+    body = on_device_fast if fast else on_device_general
     in_specs = (P(("grp", "mem"), None), P(("grp", "mem"), None), P())
     out_specs = P("mem", "grp", None, None)
     return jax.shard_map(
-        on_device, mesh=mesh, in_specs=in_specs, out_specs=out_specs, check_vma=False
+        body, mesh=mesh, in_specs=in_specs, out_specs=out_specs, check_vma=False
     )

time: 430 us -> 330 us (0.77)
  waiting for transfers between devices: 279 us -> 167 us
  blocking collectives: 52 us -> 75.8 us
  local copies, waits for them, and re-layouts: 22.7 us -> 8.48 us
  other arithmetic: 30.9 us -> 35.7 us
  matrix products: 26.1 us -> 21.5 us
    reduce_scatter x1, waiting for transfers between devices: 144 us -> 0.03 us  [on_device_fast(): got = lax.psum_scatter(send, 'grp', scatter_dimension=0, tiled=True)]
    psum x1, waiting for transfers between devices: 135 us -> 167 us  [on_device_fast(): gram00 = lax.psum(mine00, ('grp', 'mem'))]
    all_gather x1 -> x3, blocking collectives: 52 us -> 75.8 us  [the longest x1 50.7 us: on_device_fast(): everyone = lax.all_gather(active_blocks, 'mem', axis=0, tiled=True)]
    gather x4 -> x1, local copies, waits for them, and re-layouts: 7.69 us -> 0.57 us  [on_device_fast(): jnp.take(ridge_blocks, tile_rows, axis=0)[:, None, :]]
    all_to_all x1 -> x0, local copies, waits for them, and re-layouts: 5.35 us -> none  [on_device(): lax.all_to_all(outgoing, 'mem', split_axis=0, concat_axis=0, tiled=True)]
    dot_general x4 -> x6, matrix products: 22.7 us -> 21.2 us  [the longest x1 14 us: on_device_fast(): main = jnp.einsum('sagq,sakl->gaqkl', mask, received, precision=HI)]
  transfers between devices with their start and end apart: 3 -> 3, of which waited for: 2 -> 1; matrix products, arithmetic and copies ran while one was open for 0% -> 15% of each run, Pallas kernels for 0% -> 0%
where the time goes in v1:
time: 330 us; the launch traced here: 329 us
  waiting for transfers between devices  167 us (51%)
  blocking collectives  75.8 us (23%)
  other arithmetic  35.7 us (11%)
  matrix products  21.5 us (7%)
  between operations  15.1 us (5%)
  local copies, waits for them, and re-layouts  8.48 us (3%)
  starting transfers between devices  5.37 us (2%)
    psum x1, waiting for transfers between devices, on_device_fast(): gram00 = lax.psum(mine00, ('grp', 'mem'))  167 us
    all_gather x1, blocking collectives, on_device_fast(): everyone = lax.all_gather(active_blocks, 'mem', axis=0, tiled=True)  50.7 us
    all_gather x1, blocking collectives, on_device_fast(): col_cols = lax.all_gather(col_tile, 'grp', axis=0, tiled=False)  15.1 us
    dot_general x1, matrix products, on_device_fast(): main = jnp.einsum('sagq,sakl->gaqkl', mask, received, precision=HI)  14 us
    another operation x3, other arithmetic, on_device_fast(): chol = jnp.linalg.cholesky(a00)  12.4 us
    another operation x2, other arithmetic, on_device_fast(): lax.linalg.triangular_solve(chol, eye, left_side=True, lower=True)  10.5 us
    all_gather x1, blocking collectives, on_device_fast(): col_rows = lax.all_gather(col_tile, 'mem', axis=0, tiled=False)  10 us
  transfers between devices with their start and end apart: 3, of which 1 were waited for; matrix products, arithmetic and copies ran while one was open for 15% of the time, Pallas kernels for 0%

profile of v1, /device:TPU:0, one launch (start us, length us, event | category | flops | bytes accessed | tf_op | source)
XLA Modules:
  0.0 329.3 jit_solution(12028579138386191531)
XLA Ops:
  7.4 1.1 copy.56
  8.5 3.8 %convolution_bitcast_fusion.1 = f32[8,8,128,128]{3,2,1,0:T(8,128)} fusion(bf16[256,8,128,1]{2,1,0,3:T(8,128)(2,1)S(1)} %bitcast.82, bf16[256,1024]{1,0:T(8,128)(2,1)} %param.3), kind=kOutput, calls=%fused_computation.5 | convolution fusion | flops 536870912 | bytes 5242880 | tf_op jit(solution)/shard_map/nak,nbl->bakl/dot_general | solution.py:102
  12.3 0.0 copy-start.1
  12.3 5.3 %all-to-all-start = ((f32[8,8,128,128]{3,2,1,0:T(8,128)}), f32[8,8,128,128]{3,2,1,0:T(8,128)}, u32[]{:S(2)}, u32[]{:S(2)}) async-start(f32[8,8,128,128]{3,2,1,0:T(8,128)} %convolution_bitcast_fusion.1), calls=%async_computation | async-start | bytes 8388608 | tf_op jit(solution)/shard_map/all_to_all | solution.py:110
  17.6 0.0 all-reduce.2.cloned.1.call-start
  17.6 0.0 copy-done.1
  17.7 1.5 fusion.10
  19.1 0.0 all-reduce.2.cloned.1.call-update
  19.2 0.0 reduce-scatter.2.cloned.1.call-start
  19.2 50.7 %all-gather = s32[8,1,8]{2,1,0:T(1,128)S(1)} all-gather(s32[1,1,8]{2,1,0:T(1,128)S(1)} %bitcast.87), channel_id=1, replica_groups=mesh['grp'=4,'mem'=8] {'mem'}, dimensions={0}, use_global_device_ids=true | all-gather | bytes 288 | tf_op jit(solution)/shard_map/all_gather | solution.py:100
  69.9 0.1 copy.39
  70.0 0.3 fusion.19
  70.3 0.1 fusion.21
  70.5 0.0 all-to-all-done
  70.5 1.1 slice_bitcast_fusion
  71.6 0.7 convolution_bitcast_fusion.3
  72.2 0.1 copy.43
  72.4 14.0 %convolution_bitcast_fusion = f32[4,8,4,128,128]{4,2,0,3,1:T(4,128)S(1)} fusion(f32[8,8,128,128,1]{3,2,1,0,4:T(8,128)} %bitcast.6, pred[8,4]{0,1:T(4,128)(4,1)S(1)} %iota_compare_fusion.4, pred[8,8,4]{0,2,1:T(4,128)(4,1)S(1)} %iota_compare_fusion.3), kind=kOutput, calls=%fused_computation.2 | convolution fusion | flops 201327616 | bytes 12583200 | tf_op jit(solution)/shard_map/sagq,sakl->gaqkl/dot_general | solution.py:121
  86.4 2.7 copy.41
  89.1 3.9 %pad_maximum_fusion = f32[4,33,128,128]{3,2,1,0:T(8,128)} fusion(f32[4,1,128,128]{3,2,1,0:T(8,128)S(1)} %copy.43, f32[4,32,128,128]{3,2,1,0:T(8,128)S(1)} %bitcast.80), kind=kLoop, calls=%fused_computation.1 | loop fusion | flops 2162688 | bytes 17301504 | tf_op jit(solution)/shard_map/concatenate | solution.py:127
  93.0 0.0 copy-start
  93.0 0.0 reduce-scatter.2.cloned.1.call-update
  93.1 0.7 copy-done
  93.8 0.6 gather_fusion
  94.4 0.1 broadcast_select_fusion
  94.5 167.3 %all-reduce.2.cloned.1.call-done = f32[128,128]{1,0:T(8,128)} async-done(((f32[128,128]{1,0:T(8,128)}), f32[128,128]{1,0:T(8,128)}) %all-reduce.2.cloned.1.call-update) | async-done | bytes 65552 | tf_op jit(solution)/shard_map/psum | solution.py:105
  261.8 0.9 select_add_fusion
  262.7 0.1 copy.38
  262.8 0.9 fusion.12
  263.7 11.7 %cholesky.23 = f32[128,128]{1,0:T(8,128)S(1)} custom-call(f32[128,128]{1,0:T(8,128)S(1)} %fusion.12), custom_call_target="Cholesky" | custom-call | tf_op jit(solution)/shard_map/jit(cholesky)/cholesky | solution.py:107
  275.4 0.6 compare_reduce_fusion
  276.1 0.7 select_bitcast_fusion
  276.7 9.8 %custom-call.6 = f32[1,128,128]{1,2,0:T(8,128)S(1)} custom-call(f32[1,128,128]{2,1,0:T(8,128)S(1)} %get-tuple-element.16), custom_call_target="InvertDiagBlocksLowerTriangular" | custom-call | tf_op jit(solution)/shard_map/triangular_solve | solution.py:108
  286.5 0.2 convolution_bitcast_fusion.4
  286.8 0.0 reduce-scatter.2.cloned.1.call-done
  286.8 0.8 slice_multiply_fusion.1
  287.7 15.1 %all_gather.12 = f32[4,128,128]{2,1,0:T(8,128)S(1)} all-gather(f32[1,128,128]{2,1,0:T(8,128)S(1)} %slice_multiply_fusion.1), channel_id=1, replica_groups=mesh['grp'=4,'mem'=8] {'grp'}, dimensions={0}, use_global_device_ids=true | all-gather | bytes 327680 | tf_op jit(solution)/shard_map/all_gather | solution.py:141
  302.8 10.0 %all_gather.13 = f32[8,128,128]{2,1,0:T(8,128)S(1)} all-gather(f32[1,128,128]{2,1,0:T(8,128)S(1)} %slice_multiply_fusion.1), channel_id=1, replica_groups=mesh['grp'=4,'mem'=8] {'mem'}, dimensions={0}, use_global_device_ids=true | all-gather | bytes 589824 | tf_op jit(solution)/shard_map/all_gather | solution.py:140
  312.8 0.4 convolution_select_fusion.1
  313.2 0.1 copy.44
  313.3 0.6 convolution_select_fusion
  313.9 1.8 convolution_bitcast_fusion.2
  315.7 1.9 copy.45
  317.6 4.3 %fusion.3 = f32[1,32,128,128]{3,2,1,0:T(8,128)} fusion(f32[33,128,128]{2,1,0:T(8,128)} %reduce-scatter.2.cloned.1.call-done, f32[8,4,128,128]{3,2,1,0:T(8,128)} %copy.45, f32[32]{0:T(128)S(1)} %get-tuple-element.18, f32[32,128]{1,0:T(8,128)S(1)} %broadcast_select_fusion, f32[128,128]{1,0:T(8,128)S(1)} %fusion.13, ...), kind=kLoop, calls=%fused_computation.8 | loop fusion | flops 4194304 | bytes 7160032 | tf_op jit(solution)/shard_map/broadcast_in_dim | solution.py:159
  (14 shorter events, 0.1 us)
Async XLA Ops:
  12.3 5.3 %copy-start.1 = (s32[1,8]{1,0:T(1,128)S(1)}, s32[1,8]{1,0:T(1,128)}, u32[]{:S(2)}) copy-start(s32[1,8]{1,0:T(1,128)} %param.4) | copy-start | bytes 100
  12.3 58.2 %all-to-all-start = ((f32[8,8,128,128]{3,2,1,0:T(8,128)}), f32[8,8,128,128]{3,2,1,0:T(8,128)}, u32[]{:S(2)}, u32[]{:S(2)}) async-start(f32[8,8,128,128]{3,2,1,0:T(8,128)} %convolution_bitcast_fusion.1), calls=%async_computation | async-start | bytes 8388608 | tf_op jit(solution)/shard_map/all_to_all | solution.py:110
  17.6 244.3 %all-reduce.2.cloned.1.call-start = ((), (), s32[]{:S(2)}) async-start(), calls=%async_computation.2 | async-start | bytes 131072 | tf_op jit(solution)/shard_map/psum | solution.py:105
  19.2 267.6 %reduce-scatter.2.cloned.1.call-start = ((), (), s32[]{:S(2)}) async-start(), calls=%async_computation.3 | async-start | bytes 10813440 | tf_op jit(solution)/shard_map/reduce_scatter | solution.py:129
  93.0 0.7 copy-start
Sparse Core Ops, SparseCore 0:
  24.0 237.8 all-reduce.1
Sparse Core Ops, SparseCore 1:
  93.1 149.5 reduce-scatter.1

commit v2 on v1

--- a/solution.py
+++ b/solution.py
@@ -92,6 +92,8 @@
     member = lax.axis_index("mem")
     group = lax.axis_index("grp")
     per_row = NB // ACT
+    chunks = 4
+    per_chunk = ACT // chunks
     row_count = design.shape[0]
     divisor = jnp.float32(row_count * n_grp * n_mem // 16)
     eye = jnp.eye(BLK, dtype=jnp.float32)
@@ -101,34 +103,64 @@
     blocks = design.reshape(row_count, ACT, BLK)
     outgoing = jnp.einsum("nak,nbl->bakl", blocks, blocks, preferred_element_type=jnp.float32)
 
-    mine00 = jnp.where(active_blocks[0, 0] == 0, outgoing[0, 0], 0.0)
-    gram00 = lax.psum(mine00, ("grp", "mem"))
-    a00 = gram00 / divisor + eye * ridge_blocks[0][None, :]
+    row_grp = everyone // 8
+    col_grp = jnp.take(everyone, member, axis=1) // 8
+    zero_on = everyone[:, 0] == 0
+    grp_ids = jnp.arange(n_grp, dtype=jnp.int32)
+    q_ids = jnp.arange(per_row, dtype=jnp.int32)
+    pos_ids = jnp.arange(per_chunk, dtype=jnp.int32)
+
+    owned_parts = []
+    prev = None
+    for k in range(chunks):
+        piece = outgoing[:, k * per_chunk:(k + 1) * per_chunk]
+        if prev is not None:
+            piece, prev = lax.optimization_barrier((piece, prev))
+        got_piece = lax.all_to_all(piece, "mem", split_axis=0, concat_axis=0, tiled=True)
+        got_piece = got_piece.reshape(n_mem, per_chunk, BLK, BLK)
+        prev = got_piece
+        rg = row_grp[:, k * per_chunk:(k + 1) * per_chunk]
+        sel = (
+            (pos_ids[None, :, None, None, None] == pos_ids[None, None, None, None, :])
+            & (rg[None, None, None, :, :] == grp_ids[:, None, None, None, None])
+            & (col_grp[None, None, None, :, None] == q_ids[None, None, :, None, None])
+        )
+        sel = sel.reshape(n_grp, per_chunk * per_row, n_mem * per_chunk)
+        if k == 0:
+            first = pos_ids == 0
+            col_sel = (
+                (col_grp[None, :, None] == grp_ids[:, None, None])
+                & zero_on[None, :, None]
+                & first[None, None, :]
+            ).reshape(n_grp, 1, n_mem * per_chunk)
+            a00_sel = (
+                zero_on[None, :, None] & first[None, None, :] & (member == 0)
+            ).reshape(1, 1, n_mem * per_chunk)
+            a00_sel = jnp.broadcast_to(a00_sel, (n_grp, 1, n_mem * per_chunk))
+            sel = jnp.concatenate([sel, col_sel, a00_sel], axis=1)
+        width = sel.shape[1]
+        send = jnp.dot(
+            sel.reshape(n_grp * width, n_mem * per_chunk).astype(jnp.float32),
+            got_piece.reshape(n_mem * per_chunk, BLK * BLK),
+            precision=HI,
+            preferred_element_type=jnp.float32,
+        ).reshape(n_grp * width, BLK, BLK)
+        got = lax.psum_scatter(send, "grp", scatter_dimension=0, tiled=True)
+        owned_parts.append(got[: per_chunk * per_row])
+        if k == 0:
+            col_tile = jnp.transpose(got[per_chunk * per_row]) / divisor
+            a00 = got[per_chunk * per_row + 1] / divisor + eye * ridge_blocks[0][None, :]
+    owned = jnp.concatenate(owned_parts, axis=0)
+
+    col_tile, a00, prev = lax.optimization_barrier((col_tile, a00, prev))
+    pair = jnp.broadcast_to(jnp.stack([col_tile, a00])[None], (n_mem, 2, BLK, BLK))
+    pairs = lax.all_to_all(pair, "mem", split_axis=0, concat_axis=0, tiled=True)
+    col_rows = pairs[:, 0]
+    a00 = pairs[0, 1]
+    spread = jnp.broadcast_to(col_tile[None], (n_grp, BLK, BLK))
+    col_cols = lax.all_to_all(spread, "grp", split_axis=0, concat_axis=0, tiled=True)
     chol = jnp.linalg.cholesky(a00)
     chol_inv = lax.linalg.triangular_solve(chol, eye, left_side=True, lower=True)
-
-    received = lax.all_to_all(outgoing, "mem", split_axis=0, concat_axis=0, tiled=True)
-    received = received.reshape(n_mem, ACT, BLK, BLK)
-
-    row_grp = everyone // 8
-    col_grp = jnp.take(everyone, member, axis=1) // 8
-    grp_ids = jnp.arange(n_grp, dtype=jnp.int32)
-    q_ids = jnp.arange(per_row, dtype=jnp.int32)
-    mask = (
-        (row_grp[:, :, None, None] == grp_ids[None, None, :, None])
-        & (col_grp[:, None, None, None] == q_ids[None, None, None, :])
-    ).astype(jnp.float32)
-    main = jnp.einsum("sagq,sakl->gaqkl", mask, received, precision=HI)
-    main = main.reshape(n_grp, ACT * per_row, BLK, BLK)
-    col_mask = (
-        (col_grp[:, None] == grp_ids[None, :]) & (everyone[:, 0:1] == 0)
-    ).astype(jnp.float32)
-    col_part = jnp.einsum("sg,slk->gkl", col_mask, received[:, 0], precision=HI)
-    send = jnp.concatenate([main, col_part[:, None]], axis=1)
-    send = send.reshape(n_grp * (ACT * per_row + 1), BLK, BLK)
-    got = lax.psum_scatter(send, "grp", scatter_dimension=0, tiled=True)
-    owned = got[: ACT * per_row]
-    col_tile = got[ACT * per_row] / divisor
 
     t = jnp.arange(ACT * per_row, dtype=jnp.int32)
     tile_rows = group * 8 + t // per_row
@@ -137,8 +169,6 @@
     diag = eye[None] * jnp.take(ridge_blocks, tile_rows, axis=0)[:, None, :] * same[:, None, None]
     tiles = owned / divisor + diag
 
-    col_rows = lax.all_gather(col_tile, "mem", axis=0, tiled=False)
-    col_cols = lax.all_gather(col_tile, "grp", axis=0, tiled=False)
     p_rows = jnp.einsum("ipr,qr->ipq", col_rows, chol_inv, precision=HI)
     p_cols = jnp.einsum("ipr,qr->ipq", col_cols, chol_inv, precision=HI)
     row_ids = group * 8 + jnp.arange(8, dtype=jnp.int32)

time: 330 us -> 247 us (0.75)
  blocking collectives: 75.8 us -> 18.3 us
  waiting for transfers between devices: 167 us -> 127 us
  starting transfers between devices: 5.37 us -> 24.8 us
  local copies, waits for them, and re-layouts: 8.48 us -> 21.4 us
  matrix products: 21.5 us -> 12.5 us
  other arithmetic: 35.7 us -> 29.2 us
    psum x1 -> x0, waiting for transfers between devices: 167 us -> none  [on_device_fast(): gram00 = lax.psum(mine00, ('grp', 'mem'))]
    reduce_scatter x1 -> x4, waiting for transfers between devices: 0.03 us -> 67.1 us  [on_device_fast(): got = lax.psum_scatter(send, 'grp', scatter_dimension=0, tiled=True)]
    all_to_all x1 -> x6, waiting for transfers between devices: 0.01 us -> 59.6 us  [the longest x4 45.1 us: on_device_fast(): lax.all_to_all(piece, 'mem', split_axis=0, concat_axis=0, tiled=True)]
    all_gather x1, blocking collectives: 50.7 us -> 18.3 us  [on_device_fast(): everyone = lax.all_gather(active_blocks, 'mem', axis=0, tiled=True)]
    all_gather x2 -> x0, blocking collectives: 25.1 us -> none  [the longest x1 15.1 us: on_device_fast(): col_cols = lax.all_gather(col_tile, 'grp', axis=0, tiled=False)]
    all_to_all x1 -> x6, starting transfers between devices: 5.29 us -> 24.4 us  [the longest x4 16 us: on_device_fast(): lax.all_to_all(piece, 'mem', split_axis=0, concat_axis=0, tiled=True)]
    dot_general x0 -> x4, local copies, waits for them, and re-layouts: none -> 7.81 us  [on_device_fast(): jnp.dot(sel.reshape(n_grp * width, n_mem * per_chunk).astype(jnp.float32)...]
    dot_general x2 -> x4, matrix products: 14.7 us -> 7.31 us  [on_device_fast(): jnp.dot(sel.reshape(n_grp * width, n_mem * per_chunk).astype(jnp.float32)...]
  transfers between devices with their start and end apart: 3 -> 10, of which waited for: 1 -> 6; matrix products, arithmetic and copies ran while one was open for 15% -> 18% of each run, Pallas kernels for 0% -> 0%
where the time goes in v2:
time: 247 us; the launch traced here: 246 us
  waiting for transfers between devices  127 us (51%)
  other arithmetic  29.2 us (12%)
  starting transfers between devices  24.8 us (10%)
  local copies, waits for them, and re-layouts  21.4 us (9%)
  blocking collectives  18.3 us (7%)
  between operations  13.6 us (6%)
  matrix products  12.5 us (5%)
    reduce_scatter x4, waiting for transfers between devices, on_device_fast(): got = lax.psum_scatter(send, 'grp', scatter_dimension=0, tiled=True)  67.1 us
    all_to_all x4, waiting for transfers between devices, on_device_fast(): lax.all_to_all(piece, 'mem', split_axis=0, concat_axis=0, tiled=True)  45.1 us
    all_gather x1, blocking collectives, on_device_fast(): everyone = lax.all_gather(active_blocks, 'mem', axis=0, tiled=True)  18.3 us
    all_to_all x4, starting transfers between devices, on_device_fast(): lax.all_to_all(piece, 'mem', split_axis=0, concat_axis=0, tiled=True)  16 us
    all_to_all x1, waiting for transfers between devices, on_device_fast(): pairs = lax.all_to_all(pair, 'mem', split_axis=0, concat_axis=0, tiled=True)  14.5 us
    another operation x3, other arithmetic, on_device_fast(): chol = jnp.linalg.cholesky(a00)  12.4 us
    another operation x2, other arithmetic, on_device_fast(): lax.linalg.triangular_solve(chol, eye, left_side=True, lower=True)  10.4 us
    dot_general x4, local copies, waits for them, and re-layouts, on_device_fast(): jnp.dot(sel.reshape(n_grp * width, n_mem * per_chunk).astype(jnp.float32)...  7.81 us
  transfers between devices with their start and end apart: 10, of which 6 were waited for; matrix products, arithmetic and copies ran while one was open for 18% of the time, Pallas kernels for 0%

profile of v2, /device:TPU:0, one launch (start us, length us, event | category | flops | bytes accessed | tf_op | source)
XLA Modules:
  0.0 246.5 jit_solution(2653108719217321697)
XLA Ops:
  6.5 1.1 copy.143
  7.7 1.8 convolution_bitcast_fusion
  9.5 2.1 fusion.34
  11.6 5.3 %all-to-all-start = ((f32[8,2,128,128]{2,3,1,0:T(8,128)}), f32[8,2,128,128]{2,3,1,0:T(8,128)S(1)}, u32[]{:S(2)}, u32[]{:S(2)}) async-start(f32[8,2,128,128]{2,3,1,0:T(8,128)} %get-tuple-element.28), calls=%async_computation | async-start | bytes 2097152 | tf_op jit(solution)/shard_map/all_to_all | solution.py:119
  16.9 18.3 %all-gather = s32[8,1,8]{2,1,0:T(1,128)S(1)} all-gather(s32[1,1,8]{2,1,0:T(1,128)S(1)} %bitcast.154), channel_id=1, replica_groups=mesh['grp'=4,'mem'=8] {'mem'}, dimensions={0}, use_global_device_ids=true | all-gather | bytes 288 | tf_op jit(solution)/shard_map/all_gather | solution.py:102
  35.4 0.3 fusion.26
  36.9 0.2 copy.105
  37.7 0.2 copy.110
  38.0 1.3 copy.113
  39.3 2.8 %fusion.13 = f32[40,128,128]{2,0,1:T(8,128)S(1)} fusion(pred[40,16,1]{0,1,2:T(8,128)(4,1)S(1)} %reshape.503, f32[2,8,128,128]{3,2,1,0:T(8,128)} %bitcast.142), kind=kOutput, calls=%fused_computation.25 | convolution fusion | flops 125829120 | bytes 3670656 | tf_op jit(solution)/shard_map/dot_general | solution.py:142
  42.2 2.2 copy.115
  44.4 3.6 %all-to-all-start.1 = ((f32[8,2,128,128]{2,3,1,0:T(8,128)}), f32[8,2,128,128]{2,3,1,0:T(8,128)S(1)}, u32[]{:S(2)}, u32[]{:S(2)}) async-start(f32[8,2,128,128]{2,3,1,0:T(8,128)} %get-tuple-element.10), calls=%async_computation.2 | async-start | bytes 2097152 | tf_op jit(solution)/shard_map/all_to_all | solution.py:119
  48.0 0.3 broadcast_and_fusion.2
  48.4 14.9 %all-to-all-done.1 = f32[8,2,128,128]{2,3,1,0:T(8,128)S(1)} async-done(((f32[8,2,128,128]{2,3,1,0:T(8,128)}), f32[8,2,128,128]{2,3,1,0:T(8,128)S(1)}, u32[]{:S(2)}, u32[]{:S(2)}) %all-to-all-start.1) | async-done | bytes 1048608 | tf_op jit(solution)/shard_map/all_to_all | solution.py:119
  63.3 0.3 copy.121
  63.6 1.5 fusion.10
  65.1 1.9 copy.123
  67.0 3.6 %all-to-all-start.2 = ((f32[8,2,128,128]{2,3,1,0:T(8,128)}), f32[8,2,128,128]{2,3,1,0:T(8,128)S(1)}, u32[]{:S(2)}, u32[]{:S(2)}) async-start(f32[8,2,128,128]{2,3,1,0:T(8,128)} %get-tuple-element.11), calls=%async_computation.3 | async-start | bytes 2097152 | tf_op jit(solution)/shard_map/all_to_all | solution.py:119
  70.7 15.2 %all-to-all-done.2 = f32[8,2,128,128]{2,3,1,0:T(8,128)S(1)} async-done(((f32[8,2,128,128]{2,3,1,0:T(8,128)}), f32[8,2,128,128]{2,3,1,0:T(8,128)S(1)}, u32[]{:S(2)}, u32[]{:S(2)}) %all-to-all-start.2) | async-done | bytes 1048608 | tf_op jit(solution)/shard_map/all_to_all | solution.py:119
  85.9 0.3 copy.124
  86.3 1.5 fusion.7
  87.8 1.9 copy.126
  89.7 3.6 %all-to-all-start.3 = ((f32[8,2,128,128]{2,3,1,0:T(8,128)}), f32[8,2,128,128]{2,3,1,0:T(8,128)S(1)}, u32[]{:S(2)}, u32[]{:S(2)}) async-start(f32[8,2,128,128]{2,3,1,0:T(8,128)} %get-tuple-element.12), calls=%async_computation.4 | async-start | bytes 2097152 | tf_op jit(solution)/shard_map/all_to_all | solution.py:119
  93.3 0.2 reduce-scatter.11.cloned.1.call-start
  93.6 15.0 %all-to-all-done.3 = f32[8,2,128,128]{2,3,1,0:T(8,128)S(1)} async-done(((f32[8,2,128,128]{2,3,1,0:T(8,128)}), f32[8,2,128,128]{2,3,1,0:T(8,128)S(1)}, u32[]{:S(2)}, u32[]{:S(2)}) %all-to-all-start.3) | async-done | bytes 1048608 | tf_op jit(solution)/shard_map/all_to_all | solution.py:119
  108.6 0.3 copy.127
  108.9 1.5 fusion.4
  110.4 1.9 copy.129
  112.4 0.9 fusion.20
  113.5 1.1 broadcast_in_dim.76
  114.6 3.6 %all-to-all-start.4 = ((f32[8,2,128,128]{2,3,1,0:T(8,128)}), f32[8,2,128,128]{2,3,1,0:T(8,128)S(1)}, u32[]{:S(2)}, u32[]{:S(2)}) async-start(f32[8,2,128,128]{2,3,1,0:T(8,128)} %broadcast_in_dim.76), calls=%async_computation.5 | async-start | bytes 2097152 | tf_op jit(solution)/shard_map/all_to_all | solution.py:157
  118.3 0.6 gather_fusion
  119.0 14.5 %all-to-all-done.4 = f32[8,2,128,128]{2,3,1,0:T(8,128)S(1)} async-done(((f32[8,2,128,128]{2,3,1,0:T(8,128)}), f32[8,2,128,128]{2,3,1,0:T(8,128)S(1)}, u32[]{:S(2)}, u32[]{:S(2)}) %all-to-all-start.4) | async-done | bytes 1048608 | tf_op jit(solution)/shard_map/all_to_all | solution.py:157
  133.5 0.7 broadcast_in_dim.84
  134.2 4.9 %all-to-all-start.5 = ((f32[4,128,128]{2,1,0:T(8,128)}), f32[4,128,128]{2,1,0:T(8,128)S(1)}, u32[]{:S(2)}, u32[]{:S(2)}) async-start(f32[4,128,128]{2,1,0:T(8,128)} %broadcast_in_dim.84), calls=%async_computation.6 | async-start | bytes 524288 | tf_op jit(solution)/shard_map/all_to_all | solution.py:161
  139.2 11.7 %cholesky.23 = f32[128,128]{1,0:T(8,128)S(1)} custom-call(f32[128,128]{1,0:T(8,128)S(1)} %fusion.22), custom_call_target="Cholesky" | custom-call | tf_op jit(solution)/shard_map/jit(cholesky)/cholesky | solution.py:162
  151.0 0.6 compare_reduce_fusion
  151.6 0.6 select_bitcast_fusion
  152.2 9.8 %custom-call.6 = f32[1,128,128]{1,2,0:T(8,128)S(1)} custom-call(f32[1,128,128]{2,1,0:T(8,128)S(1)} %get-tuple-element.26), custom_call_target="InvertDiagBlocksLowerTriangular" | custom-call | tf_op jit(solution)/shard_map/triangular_solve | solution.py:163
  162.0 0.2 convolution_bitcast_fusion.2
  162.2 1.0 convolution_select_fusion
  163.4 0.4 convolution_select_fusion.1
  163.8 1.8 convolution_bitcast_fusion.1
  165.6 0.2 copy.131
  165.9 22.1 %reduce-scatter.9.cloned.1.call-done = f32[8,128,128]{1,2,0:T(8,128)} async-done(((f32[32,128,128]{1,2,0:T(8,128)}), f32[8,128,128]{1,2,0:T(8,128)}) %reduce-scatter.9.cloned.1.call-update) | async-done | bytes 524304 | tf_op jit(solution)/shard_map/reduce_scatter | solution.py:148
  188.0 45.0 %reduce-scatter.11.cloned.1.call-done = f32[8,128,128]{1,2,0:T(8,128)} async-done(((f32[32,128,128]{1,2,0:T(8,128)}), f32[8,128,128]{1,2,0:T(8,128)}) %reduce-scatter.11.cloned.1.call-update) | async-done | bytes 524304 | tf_op jit(solution)/shard_map/reduce_scatter | solution.py:148
  233.0 4.1 %fusion.2 = f32[1,32,128,128]{2,3,1,0:T(8,128)} fusion(f32[8,128,128]{1,2,0:T(8,128)} %reduce-scatter.11.cloned.1.call-done, f32[8,128,128]{1,2,0:T(8,128)} %reduce-scatter.9.cloned.1.call-done, f32[8,128,128]{1,2,0:T(8,128)} %reduce-scatter.7.cloned.1.call-done, f32[8,128,128]{1,2,0:T(8,128)S(1)} %slice-done, f32[8,4,128,128]{2,3,1,0:T(8,128)S(1)} %copy.131, ...), kind=kLoop, calls=%fused_computation.5 | loop fusion | flops 5767168 | bytes 7160032 | tf_op jit(solution)/shard_map/broadcast_in_dim | solution.py:189
  237.1 2.9 %copy.132 = f32[1,32,128,128]{3,2,1,0:T(8,128)} copy(f32[1,32,128,128]{2,3,1,0:T(8,128)} %fusion.2) | data formatting | bytes 4194304 | tf_op jit(solution)/shard_map/broadcast_in_dim | solution.py:189
  (70 shorter events, 3.3 us)
Async XLA Ops:
  11.6 5.4 %copy-start.1 = (s32[1,8]{1,0:T(1,128)S(1)}, s32[1,8]{1,0:T(1,128)}, u32[]{:S(2)}) copy-start(s32[1,8]{1,0:T(1,128)} %param.4) | copy-start | bytes 100
  11.6 26.4 %all-to-all-start = ((f32[8,2,128,128]{2,3,1,0:T(8,128)}), f32[8,2,128,128]{2,3,1,0:T(8,128)S(1)}, u32[]{:S(2)}, u32[]{:S(2)}) async-start(f32[8,2,128,128]{2,3,1,0:T(8,128)} %get-tuple-element.28), calls=%async_computation | async-start | bytes 2097152 | tf_op jit(solution)/shard_map/all_to_all | solution.py:119
  16.9 95.5 %reduce-scatter.5.cloned.1.call-start = ((), (), s32[]{:S(2)}) async-start(), calls=%async_computation.10 | async-start | bytes 3276800 | tf_op jit(solution)/shard_map/reduce_scatter | solution.py:148
  44.4 18.9 %all-to-all-start.1 = ((f32[8,2,128,128]{2,3,1,0:T(8,128)}), f32[8,2,128,128]{2,3,1,0:T(8,128)S(1)}, u32[]{:S(2)}, u32[]{:S(2)}) async-start(f32[8,2,128,128]{2,3,1,0:T(8,128)} %get-tuple-element.10), calls=%async_computation.2 | async-start | bytes 2097152 | tf_op jit(solution)/shard_map/all_to_all | solution.py:119
  47.9 117.9 %reduce-scatter.7.cloned.1.call-start = ((), (), s32[]{:S(2)}) async-start(), calls=%async_computation.11 | async-start | bytes 2621440 | tf_op jit(solution)/shard_map/reduce_scatter | solution.py:148
  67.0 18.9 %all-to-all-start.2 = ((f32[8,2,128,128]{2,3,1,0:T(8,128)}), f32[8,2,128,128]{2,3,1,0:T(8,128)S(1)}, u32[]{:S(2)}, u32[]{:S(2)}) async-start(f32[8,2,128,128]{2,3,1,0:T(8,128)} %get-tuple-element.11), calls=%async_computation.3 | async-start | bytes 2097152 | tf_op jit(solution)/shard_map/all_to_all | solution.py:119
  70.6 117.4 %reduce-scatter.9.cloned.1.call-start = ((), (), s32[]{:S(2)}) async-start(), calls=%async_computation.12 | async-start | bytes 2621440 | tf_op jit(solution)/shard_map/reduce_scatter | solution.py:148
  89.7 18.9 %all-to-all-start.3 = ((f32[8,2,128,128]{2,3,1,0:T(8,128)}), f32[8,2,128,128]{2,3,1,0:T(8,128)S(1)}, u32[]{:S(2)}, u32[]{:S(2)}) async-start(f32[8,2,128,128]{2,3,1,0:T(8,128)} %get-tuple-element.12), calls=%async_computation.4 | async-start | bytes 2097152 | tf_op jit(solution)/shard_map/all_to_all | solution.py:119
  93.3 139.7 %reduce-scatter.11.cloned.1.call-start = ((), (), s32[]{:S(2)}) async-start(), calls=%async_computation.13 | async-start | bytes 2621440 | tf_op jit(solution)/shard_map/reduce_scatter | solution.py:148
  112.3 1.1 slice-start.1
  113.3 5.0 %copy-start = (f32[4096]{0:T(1024)S(1)}, f32[4096]{0:T(1024)}, u32[]{:S(2)}) copy-start(f32[4096]{0:T(1024)} %param.5) | copy-start | bytes 49156
  114.6 18.9 %all-to-all-start.4 = ((f32[8,2,128,128]{2,3,1,0:T(8,128)}), f32[8,2,128,128]{2,3,1,0:T(8,128)S(1)}, u32[]{:S(2)}, u32[]{:S(2)}) async-start(f32[8,2,128,128]{2,3,1,0:T(8,128)} %broadcast_in_dim.76), calls=%async_computation.5 | async-start | bytes 2097152 | tf_op jit(solution)/shard_map/all_to_all | solution.py:157
  134.2 29.2 %all-to-all-start.5 = ((f32[4,128,128]{2,1,0:T(8,128)}), f32[4,128,128]{2,1,0:T(8,128)S(1)}, u32[]{:S(2)}, u32[]{:S(2)}) async-start(f32[4,128,128]{2,1,0:T(8,128)} %broadcast_in_dim.84), calls=%async_computation.6 | async-start | bytes 524288 | tf_op jit(solution)/shard_map/all_to_all | solution.py:161
  165.6 67.3 %slice-start = ((f32[10,128,128]{1,2,0:T(8,128)}), f32[8,128,128]{1,2,0:T(8,128)S(1)}, s32[]{:S(2)}) async-start(f32[10,128,128]{1,2,0:T(8,128)} %reduce-scatter.5.cloned.1.call-done), calls=%async_computation.14 | async-start | bytes 1048576 | tf_op jit(solution)/shard_map/slice | solution.py:149
Sparse Core Ops, SparseCore 0:
  44.5 51.5 reduce-scatter.4
  98.3 43.6 reduce-scatter.6
  144.4 43.5 reduce-scatter.8
  190.1 42.7 reduce-scatter.10

commit v3 on v2

--- a/solution.py
+++ b/solution.py
@@ -92,14 +92,16 @@
     member = lax.axis_index("mem")
     group = lax.axis_index("grp")
     per_row = NB // ACT
-    chunks = 4
-    per_chunk = ACT // chunks
+    sizes = (1, 2, 2, 3)
+    starts = (0, 1, 3, 5)
     row_count = design.shape[0]
     divisor = jnp.float32(row_count * n_grp * n_mem // 16)
     eye = jnp.eye(BLK, dtype=jnp.float32)
     ridge_blocks = ridge.reshape(NB, BLK)
 
-    everyone = lax.all_gather(active_blocks, "mem", axis=0, tiled=True)
+    ids_out = jnp.broadcast_to(active_blocks[None], (n_mem, 1, ACT))
+    everyone = lax.all_to_all(ids_out, "mem", split_axis=0, concat_axis=0, tiled=True)
+    everyone = everyone.reshape(n_mem, ACT)
     blocks = design.reshape(row_count, ACT, BLK)
     outgoing = jnp.einsum("nak,nbl->bakl", blocks, blocks, preferred_element_type=jnp.float32)
 
@@ -108,18 +110,20 @@
     zero_on = everyone[:, 0] == 0
     grp_ids = jnp.arange(n_grp, dtype=jnp.int32)
     q_ids = jnp.arange(per_row, dtype=jnp.int32)
-    pos_ids = jnp.arange(per_chunk, dtype=jnp.int32)
 
     owned_parts = []
     prev = None
-    for k in range(chunks):
-        piece = outgoing[:, k * per_chunk:(k + 1) * per_chunk]
+    for k in range(len(sizes)):
+        per_chunk = sizes[k]
+        lo = starts[k]
+        pos_ids = jnp.arange(per_chunk, dtype=jnp.int32)
+        piece = outgoing[:, lo:lo + per_chunk]
         if prev is not None:
             piece, prev = lax.optimization_barrier((piece, prev))
         got_piece = lax.all_to_all(piece, "mem", split_axis=0, concat_axis=0, tiled=True)
         got_piece = got_piece.reshape(n_mem, per_chunk, BLK, BLK)
         prev = got_piece
-        rg = row_grp[:, k * per_chunk:(k + 1) * per_chunk]
+        rg = row_grp[:, lo:lo + per_chunk]
         sel = (
             (pos_ids[None, :, None, None, None] == pos_ids[None, None, None, None, :])
             & (rg[None, None, None, :, :] == grp_ids[:, None, None, None, None])
@@ -133,11 +137,7 @@
                 & zero_on[None, :, None]
                 & first[None, None, :]
             ).reshape(n_grp, 1, n_mem * per_chunk)
-            a00_sel = (
-                zero_on[None, :, None] & first[None, None, :] & (member == 0)
-            ).reshape(1, 1, n_mem * per_chunk)
-            a00_sel = jnp.broadcast_to(a00_sel, (n_grp, 1, n_mem * per_chunk))
-            sel = jnp.concatenate([sel, col_sel, a00_sel], axis=1)
+            sel = jnp.concatenate([sel, col_sel], axis=1)
         width = sel.shape[1]
         send = jnp.dot(
             sel.reshape(n_grp * width, n_mem * per_chunk).astype(jnp.float32),
@@ -149,16 +149,15 @@
         owned_parts.append(got[: per_chunk * per_row])
         if k == 0:
             col_tile = jnp.transpose(got[per_chunk * per_row]) / divisor
-            a00 = got[per_chunk * per_row + 1] / divisor + eye * ridge_blocks[0][None, :]
     owned = jnp.concatenate(owned_parts, axis=0)
 
-    col_tile, a00, prev = lax.optimization_barrier((col_tile, a00, prev))
-    pair = jnp.broadcast_to(jnp.stack([col_tile, a00])[None], (n_mem, 2, BLK, BLK))
+    col_tile, prev = lax.optimization_barrier((col_tile, prev))
+    spread = jnp.broadcast_to(col_tile[None], (n_grp, BLK, BLK))
+    col_cols = lax.all_to_all(spread, "grp", split_axis=0, concat_axis=0, tiled=True)
+    pair = jnp.broadcast_to(jnp.stack([col_tile, col_cols[0]])[None], (n_mem, 2, BLK, BLK))
     pairs = lax.all_to_all(pair, "mem", split_axis=0, concat_axis=0, tiled=True)
     col_rows = pairs[:, 0]
-    a00 = pairs[0, 1]
-    spread = jnp.broadcast_to(col_tile[None], (n_grp, BLK, BLK))
-    col_cols = lax.all_to_all(spread, "grp", split_axis=0, concat_axis=0, tiled=True)
+    a00 = pairs[0, 1] + eye * ridge_blocks[0][None, :]
     chol = jnp.linalg.cholesky(a00)
     chol_inv = lax.linalg.triangular_solve(chol, eye, left_side=True, lower=True)
 

time: 247 us -> 235 us (0.951)
  blocking collectives: 18.3 us -> 0 us
  waiting for transfers between devices: 127 us -> 122 us
  local copies, waits for them, and re-layouts: 21.4 us -> 25.5 us
  starting transfers between devices: 24.8 us -> 28.8 us
  matrix products: 12.5 us -> 15.8 us
    reduce_scatter x4, waiting for transfers between devices: 67.1 us -> 33 us  [on_device_fast(): got = lax.psum_scatter(send, 'grp', scatter_dimension=0, tiled=True)]
    all_gather x1 -> x0, blocking collectives: 18.3 us -> none  [on_device_fast(): everyone = lax.all_gather(active_blocks, 'mem', axis=0, tiled=True)]
    all_to_all x1, waiting for transfers between devices: 0.01 us -> 15.6 us  [on_device_fast(): lax.all_to_all(spread, 'grp', split_axis=0, concat_axis=0, tiled=True)]
    all_to_all x4, waiting for transfers between devices: 45.1 us -> 58.9 us  [on_device_fast(): lax.all_to_all(piece, 'mem', split_axis=0, concat_axis=0, tiled=True)]
    slice x4 -> x9, local copies, waits for them, and re-layouts: 2.16 us -> 8.81 us  [the longest x3 7.7 us: on_device_fast(): piece = outgoing[:, lo:lo + per_chunk]]
    all_to_all x0 -> x1, starting transfers between devices: none -> 5.17 us  [on_device_fast(): lax.all_to_all(ids_out, 'mem', split_axis=0, concat_axis=0, tiled=True)]
    dot_general x4 -> x2, local copies, waits for them, and re-layouts: 7.81 us -> 3.96 us  [on_device_fast(): jnp.dot(sel.reshape(n_grp * width, n_mem * per_chunk).astype(jnp.float32)...]
    reduce_scatter x0 -> x2, local copies, waits for them, and re-layouts: none -> 3.24 us  [on_device_fast(): got = lax.psum_scatter(send, 'grp', scatter_dimension=0, tiled=True)]
  transfers between devices with their start and end apart: 10 -> 11, of which waited for: 6 -> 7; matrix products, arithmetic and copies ran while one was open for 18% -> 27% of each run, Pallas kernels for 0% -> 0%
where the time goes in v3:
time: 235 us; the launch traced here: 234 us
  waiting for transfers between devices  122 us (52%)
  starting transfers between devices  28.8 us (12%)
  other arithmetic  28 us (12%)
  local copies, waits for them, and re-layouts  25.5 us (11%)
  matrix products  15.8 us (7%)
  between operations  13.5 us (6%)
    all_to_all x4, waiting for transfers between devices, on_device_fast(): lax.all_to_all(piece, 'mem', split_axis=0, concat_axis=0, tiled=True)  58.9 us
    reduce_scatter x4, waiting for transfers between devices, on_device_fast(): got = lax.psum_scatter(send, 'grp', scatter_dimension=0, tiled=True)  33 us
    all_to_all x1, waiting for transfers between devices, on_device_fast(): lax.all_to_all(spread, 'grp', split_axis=0, concat_axis=0, tiled=True)  15.6 us
    all_to_all x4, starting transfers between devices, on_device_fast(): lax.all_to_all(piece, 'mem', split_axis=0, concat_axis=0, tiled=True)  14.9 us
    all_to_all x1, waiting for transfers between devices, on_device_fast(): pairs = lax.all_to_all(pair, 'mem', split_axis=0, concat_axis=0, tiled=True)  14.6 us
    another operation x3, other arithmetic, on_device_fast(): chol = jnp.linalg.cholesky(a00)  12.4 us
    another operation x2, other arithmetic, on_device_fast(): lax.linalg.triangular_solve(chol, eye, left_side=True, lower=True)  10.5 us
    dot_general x4, matrix products, on_device_fast(): jnp.dot(sel.reshape(n_grp * width, n_mem * per_chunk).astype(jnp.float32)...  9.07 us
  transfers between devices with their start and end apart: 11, of which 7 were waited for; matrix products, arithmetic and copies ran while one was open for 27% of the time, Pallas kernels for 0%

profile of v3, /device:TPU:0, one launch (start us, length us, event | category | flops | bytes accessed | tf_op | source)
XLA Modules:
  0.0 233.7 jit_solution(1649215507130295244)
XLA Ops:
  6.5 1.2 broadcast_in_dim.82
  7.8 5.2 %all-to-all-start = ((s32[8,1,8]{2,1,0:T(1,128)}), s32[8,1,8]{2,1,0:T(1,128)S(1)}, u32[]{:S(2)}, u32[]{:S(2)}) async-start(s32[8,1,8]{2,1,0:T(1,128)} %broadcast_in_dim.82), calls=%async_computation | async-start | bytes 8192 | tf_op jit(solution)/shard_map/all_to_all | solution.py:103
  13.0 1.1 copy.71
  14.1 3.7 %convolution_bitcast_fusion = f32[8,8,128,128]{2,3,1,0:T(8,128)} fusion(bf16[256,8,128,1]{2,1,0,3:T(8,128)(2,1)S(1)} %bitcast.138, bf16[256,1024]{1,0:T(8,128)(2,1)} %param.3), kind=kOutput, calls=%fused_computation.2 | convolution fusion | flops 536870912 | bytes 5242880 | tf_op jit(solution)/shard_map/nak,nbl->bakl/dot_general | solution.py:106
  17.8 1.9 slice.80
  19.7 4.2 %all-to-all-start.1 = ((f32[8,1,128,128]{2,3,1,0:T(8,128)}), f32[8,1,128,128]{2,3,1,0:T(8,128)S(1)}, u32[]{:S(2)}, u32[]{:S(2)}) async-start(f32[8,1,128,128]{2,3,1,0:T(8,128)} %slice.80), calls=%async_computation.1 | async-start | bytes 1048576 | tf_op jit(solution)/shard_map/all_to_all | solution.py:123
  24.1 0.3 fusion.25
  24.9 8.7 %all-to-all-done.1 = f32[8,1,128,128]{2,3,1,0:T(8,128)S(1)} async-done(((f32[8,1,128,128]{2,3,1,0:T(8,128)}), f32[8,1,128,128]{2,3,1,0:T(8,128)S(1)}, u32[]{:S(2)}, u32[]{:S(2)}) %all-to-all-start.1) | async-done | bytes 524320 | tf_op jit(solution)/shard_map/all_to_all | solution.py:123
  33.9 0.9 fusion.13
  34.8 1.4 copy.48
  36.2 3.1 %fusion.33 = (f32[8,2,128,128]{2,3,1,0:T(8,128)}, f32[8,2,128,128]{2,3,1,0:T(8,128)}) fusion(f32[8,8,128,128]{2,3,1,0:T(8,128)} %convolution_bitcast_fusion), kind=kLoop, calls=%fused_computation.105 | loop fusion | bytes 4194304 | tf_op jit(solution)/shard_map/slice | solution.py:120
  39.3 3.6 %all-to-all-start.2 = ((f32[8,2,128,128]{2,3,1,0:T(8,128)}), f32[8,2,128,128]{2,3,1,0:T(8,128)S(1)}, u32[]{:S(2)}, u32[]{:S(2)}) async-start(f32[8,2,128,128]{2,3,1,0:T(8,128)} %get-tuple-element.9), calls=%async_computation.3 | async-start | bytes 2097152 | tf_op jit(solution)/shard_map/all_to_all | solution.py:123
  43.2 0.2 broadcast_and_fusion.2
  43.5 14.7 %all-to-all-done.2 = f32[8,2,128,128]{2,3,1,0:T(8,128)S(1)} async-done(((f32[8,2,128,128]{2,3,1,0:T(8,128)}), f32[8,2,128,128]{2,3,1,0:T(8,128)S(1)}, u32[]{:S(2)}, u32[]{:S(2)}) %all-to-all-start.2) | async-done | bytes 1048608 | tf_op jit(solution)/shard_map/all_to_all | solution.py:123
  58.2 0.3 copy.52
  58.6 2.8 %fusion.10 = f32[32,128,128]{2,0,1:T(8,128)} fusion(pred[32,16,1]{0,1,2:T(8,128)(4,1)S(1)} %reshape.505, f32[2,8,128,128]{3,2,1,0:T(8,128)S(1)} %bitcast.135), kind=kOutput, calls=%fused_computation.21 | convolution fusion | flops 100663296 | bytes 3146240 | tf_op jit(solution)/shard_map/dot_general | solution.py:142
  61.4 3.6 %all-to-all-start.3 = ((f32[8,2,128,128]{2,3,1,0:T(8,128)}), f32[8,2,128,128]{2,3,1,0:T(8,128)S(1)}, u32[]{:S(2)}, u32[]{:S(2)}) async-start(f32[8,2,128,128]{2,3,1,0:T(8,128)} %get-tuple-element.10), calls=%async_computation.4 | async-start | bytes 2097152 | tf_op jit(solution)/shard_map/all_to_all | solution.py:123
  65.1 15.2 %all-to-all-done.3 = f32[8,2,128,128]{2,3,1,0:T(8,128)S(1)} async-done(((f32[8,2,128,128]{2,3,1,0:T(8,128)}), f32[8,2,128,128]{2,3,1,0:T(8,128)S(1)}, u32[]{:S(2)}, u32[]{:S(2)}) %all-to-all-start.3) | async-done | bytes 1048608 | tf_op jit(solution)/shard_map/all_to_all | solution.py:123
  80.3 0.3 copy.54
  80.7 2.8 %fusion.7 = f32[32,128,128]{2,0,1:T(8,128)} fusion(pred[32,16,1]{0,1,2:T(8,128)(4,1)S(1)} %reshape.506, f32[2,8,128,128]{3,2,1,0:T(8,128)S(1)} %bitcast.136), kind=kOutput, calls=%fused_computation.18 | convolution fusion | flops 100663296 | bytes 3146240 | tf_op jit(solution)/shard_map/dot_general | solution.py:142
  83.5 2.7 %slice.82 = f32[8,3,128,128]{2,3,1,0:T(8,128)} slice(f32[8,8,128,128]{2,3,1,0:T(8,128)} %convolution_bitcast_fusion), slice={[0:8], [5:8], [0:128], [0:128]} | slice | bytes 3145728 | tf_op jit(solution)/shard_map/slice | solution.py:120
  86.2 3.6 %all-to-all-start.4 = ((f32[8,3,128,128]{2,3,1,0:T(8,128)}), f32[8,3,128,128]{2,3,1,0:T(8,128)S(1)}, u32[]{:S(2)}, u32[]{:S(2)}) async-start(f32[8,3,128,128]{2,3,1,0:T(8,128)} %slice.82), calls=%async_computation.5 | async-start | bytes 3145728 | tf_op jit(solution)/shard_map/all_to_all | solution.py:123
  90.4 20.3 %all-to-all-done.4 = f32[8,3,128,128]{2,3,1,0:T(8,128)S(1)} async-done(((f32[8,3,128,128]{2,3,1,0:T(8,128)}), f32[8,3,128,128]{2,3,1,0:T(8,128)S(1)}, u32[]{:S(2)}, u32[]{:S(2)}) %all-to-all-start.4) | async-done | bytes 1572896 | tf_op jit(solution)/shard_map/all_to_all | solution.py:123
  110.8 0.5 copy.56
  111.2 2.5 %fusion.4 = f32[48,128,128]{2,0,1:T(8,128)S(1)} fusion(pred[48,24,1]{0,1,2:T(8,128)(4,1)S(1)} %reshape.507, f32[3,8,128,128]{3,2,1,0:T(8,128)S(1)} %bitcast.134), kind=kOutput, calls=%fused_computation.10 | convolution fusion | flops 226492416 | bytes 4719744 | tf_op jit(solution)/shard_map/dot_general | solution.py:142
  113.8 2.6 %copy.58 = f32[48,128,128]{2,1,0:T(8,128)} copy(f32[48,128,128]{2,0,1:T(8,128)S(1)} %fusion.4) | data formatting | bytes 6291456 | tf_op jit(solution)/shard_map/dot_general | solution.py:142
  116.4 0.8 slice.81
  117.4 0.7 broadcast_in_dim.85
  118.1 5.0 %all-to-all-start.5 = ((f32[4,128,128]{2,1,0:T(8,128)}), f32[4,128,128]{2,1,0:T(8,128)S(1)}, u32[]{:S(2)}, u32[]{:S(2)}) async-start(f32[4,128,128]{2,1,0:T(8,128)} %broadcast_in_dim.85), calls=%async_computation.6 | async-start | bytes 524288 | tf_op jit(solution)/shard_map/all_to_all | solution.py:156
  123.1 15.6 %all-to-all-done.5 = f32[4,128,128]{2,1,0:T(8,128)S(1)} async-done(((f32[4,128,128]{2,1,0:T(8,128)}), f32[4,128,128]{2,1,0:T(8,128)S(1)}, u32[]{:S(2)}, u32[]{:S(2)}) %all-to-all-start.5) | async-done | bytes 262176 | tf_op jit(solution)/shard_map/all_to_all | solution.py:156
  138.7 1.1 broadcast_in_dim.86
  139.8 3.6 %all-to-all-start.6 = ((f32[8,2,128,128]{3,2,1,0:T(8,128)}), f32[8,2,128,128]{3,2,1,0:T(8,128)S(1)}, u32[]{:S(2)}, u32[]{:S(2)}) async-start(f32[8,2,128,128]{3,2,1,0:T(8,128)} %broadcast_in_dim.86), calls=%async_computation.7 | async-start | bytes 2097152 | tf_op jit(solution)/shard_map/all_to_all | solution.py:158
  143.4 0.6 gather_fusion
  144.2 14.6 %all-to-all-done.6 = f32[8,2,128,128]{3,2,1,0:T(8,128)S(1)} async-done(((f32[8,2,128,128]{3,2,1,0:T(8,128)}), f32[8,2,128,128]{3,2,1,0:T(8,128)S(1)}, u32[]{:S(2)}, u32[]{:S(2)}) %all-to-all-start.6) | async-done | bytes 1048608 | tf_op jit(solution)/shard_map/all_to_all | solution.py:158
  158.9 11.7 %cholesky.23 = f32[128,128]{1,0:T(8,128)S(1)} custom-call(f32[128,128]{1,0:T(8,128)S(1)} %fusion.21), custom_call_target="Cholesky" | custom-call | tf_op jit(solution)/shard_map/jit(cholesky)/cholesky | solution.py:161
  170.6 0.7 compare_reduce_fusion
  171.3 0.6 select_bitcast_fusion
  171.9 9.8 %custom-call.6 = f32[1,128,128]{1,2,0:T(8,128)S(1)} custom-call(f32[1,128,128]{2,1,0:T(8,128)S(1)} %get-tuple-element.24), custom_call_target="InvertDiagBlocksLowerTriangular" | custom-call | tf_op jit(solution)/shard_map/triangular_solve | solution.py:162
  181.7 0.2 convolution_bitcast_fusion.2
  182.0 0.4 convolution_select_fusion.1
  182.4 0.9 copy.51
  183.2 0.6 convolution_select_fusion
  183.8 1.8 convolution_bitcast_fusion.1
  185.6 1.9 copy.61
  187.5 1.3 copy.59
  188.8 2.0 copy.60
  190.8 32.9 %reduce-scatter.11.cloned.1.call-done = f32[12,128,128]{2,1,0:T(8,128)} async-done(((f32[48,128,128]{2,1,0:T(8,128)}), f32[12,128,128]{2,1,0:T(8,128)}) %reduce-scatter.11.cloned.1.call-update) | async-done | bytes 786448 | tf_op jit(solution)/shard_map/reduce_scatter | solution.py:148
  223.7 3.5 %fusion.2 = f32[1,32,128,128]{3,2,1,0:T(8,128)} fusion(f32[12,128,128]{2,1,0:T(8,128)} %reduce-scatter.11.cloned.1.call-done, f32[8,128,128]{2,1,0:T(8,128)} %copy.60, f32[8,128,128]{2,1,0:T(8,128)S(1)} %copy.59, f32[4,128,128]{2,1,0:T(8,128)S(1)} %slice-done, f32[8,4,128,128]{3,2,1,0:T(8,128)S(1)} %copy-done, f32[32]{0:T(128)S(1)} %get-tuple-element.34, ...), kind=kLoop, calls=%fused_computation.5 | loop fusion | flops 5767168 | bytes 7160032 | tf_op jit(solution)/shard_map/broadcast_in_dim | solution.py:188
  (58 shorter events, 2.6 us)
Async XLA Ops:
  7.8 11.9 %all-to-all-start = ((s32[8,1,8]{2,1,0:T(1,128)}), s32[8,1,8]{2,1,0:T(1,128)S(1)}, u32[]{:S(2)}, u32[]{:S(2)}) async-start(s32[8,1,8]{2,1,0:T(1,128)} %broadcast_in_dim.82), calls=%async_computation | async-start | bytes 8192 | tf_op jit(solution)/shard_map/all_to_all | solution.py:103
  19.7 13.9 %all-to-all-start.1 = ((f32[8,1,128,128]{2,3,1,0:T(8,128)}), f32[8,1,128,128]{2,3,1,0:T(8,128)S(1)}, u32[]{:S(2)}, u32[]{:S(2)}) async-start(f32[8,1,128,128]{2,3,1,0:T(8,128)} %slice.80), calls=%async_computation.1 | async-start | bytes 1048576 | tf_op jit(solution)/shard_map/all_to_all | solution.py:123
  23.9 92.5 %reduce-scatter.5.cloned.1.call-start = ((), (), s32[]{:S(2)}) async-start(), calls=%async_computation.11 | async-start | bytes 1638400 | tf_op jit(solution)/shard_map/reduce_scatter | solution.py:148
  39.3 18.9 %all-to-all-start.2 = ((f32[8,2,128,128]{2,3,1,0:T(8,128)}), f32[8,2,128,128]{2,3,1,0:T(8,128)S(1)}, u32[]{:S(2)}, u32[]{:S(2)}) async-start(f32[8,2,128,128]{2,3,1,0:T(8,128)} %get-tuple-element.9), calls=%async_computation.3 | async-start | bytes 2097152 | tf_op jit(solution)/shard_map/all_to_all | solution.py:123
  42.9 144.6 %reduce-scatter.7.cloned.1.call-start = ((), (), s32[]{:S(2)}) async-start(), calls=%async_computation.12 | async-start | bytes 2621440 | tf_op jit(solution)/shard_map/reduce_scatter | solution.py:148
  61.4 18.9 %all-to-all-start.3 = ((f32[8,2,128,128]{2,3,1,0:T(8,128)}), f32[8,2,128,128]{2,3,1,0:T(8,128)S(1)}, u32[]{:S(2)}, u32[]{:S(2)}) async-start(f32[8,2,128,128]{2,3,1,0:T(8,128)} %get-tuple-element.10), calls=%async_computation.4 | async-start | bytes 2097152 | tf_op jit(solution)/shard_map/all_to_all | solution.py:123
  65.0 123.8 %reduce-scatter.9.cloned.1.call-start = ((), (), s32[]{:S(2)}) async-start(), calls=%async_computation.13 | async-start | bytes 2621440 | tf_op jit(solution)/shard_map/reduce_scatter | solution.py:148
  86.2 24.5 %all-to-all-start.4 = ((f32[8,3,128,128]{2,3,1,0:T(8,128)}), f32[8,3,128,128]{2,3,1,0:T(8,128)S(1)}, u32[]{:S(2)}, u32[]{:S(2)}) async-start(f32[8,3,128,128]{2,3,1,0:T(8,128)} %slice.82), calls=%async_computation.5 | async-start | bytes 3145728 | tf_op jit(solution)/shard_map/all_to_all | solution.py:123
  89.8 133.9 %reduce-scatter.11.cloned.1.call-start = ((), (), s32[]{:S(2)}) async-start(), calls=%async_computation.14 | async-start | bytes 3932160 | tf_op jit(solution)/shard_map/reduce_scatter | solution.py:148
  118.1 25.3 %copy-start.1 = (f32[4096]{0:T(1024)S(1)}, f32[4096]{0:T(1024)}, u32[]{:S(2)}) copy-start(f32[4096]{0:T(1024)} %param.5) | copy-start | bytes 49156
  118.1 20.6 %all-to-all-start.5 = ((f32[4,128,128]{2,1,0:T(8,128)}), f32[4,128,128]{2,1,0:T(8,128)S(1)}, u32[]{:S(2)}, u32[]{:S(2)}) async-start(f32[4,128,128]{2,1,0:T(8,128)} %broadcast_in_dim.85), calls=%async_computation.6 | async-start | bytes 524288 | tf_op jit(solution)/shard_map/all_to_all | solution.py:156
  139.8 18.9 %all-to-all-start.6 = ((f32[8,2,128,128]{3,2,1,0:T(8,128)}), f32[8,2,128,128]{3,2,1,0:T(8,128)S(1)}, u32[]{:S(2)}, u32[]{:S(2)}) async-start(f32[8,2,128,128]{3,2,1,0:T(8,128)} %broadcast_in_dim.86), calls=%async_computation.7 | async-start | bytes 2097152 | tf_op jit(solution)/shard_map/all_to_all | solution.py:158
  185.6 38.1 %slice-start = ((f32[5,128,128]{2,1,0:T(8,128)}), f32[4,128,128]{2,1,0:T(8,128)S(1)}, s32[]{:S(2)}) async-start(f32[5,128,128]{2,1,0:T(8,128)} %reduce-scatter.5.cloned.1.call-done), calls=%async_computation.15 | async-start | bytes 524288 | tf_op jit(solution)/shard_map/slice | solution.py:149
  187.5 36.2 %copy-start = (f32[8,4,128,128]{3,2,1,0:T(8,128)S(1)}, f32[8,4,128,128]{3,2,1,0:T(8,128)}, u32[]{:S(2)}) copy-start(f32[8,4,128,128]{3,2,1,0:T(8,128)} %copy.61) | copy-start | bytes 6291460
Sparse Core Ops, SparseCore 0:
  36.3 30.5 reduce-scatter.4
  69.2 42.6 reduce-scatter.6
  114.3 47.3 reduce-scatter.8
  163.8 59.8 reduce-scatter.10

commit v4 on v3

--- a/solution.py
+++ b/solution.py
@@ -99,15 +99,9 @@
     eye = jnp.eye(BLK, dtype=jnp.float32)
     ridge_blocks = ridge.reshape(NB, BLK)
 
-    ids_out = jnp.broadcast_to(active_blocks[None], (n_mem, 1, ACT))
-    everyone = lax.all_to_all(ids_out, "mem", split_axis=0, concat_axis=0, tiled=True)
-    everyone = everyone.reshape(n_mem, ACT)
     blocks = design.reshape(row_count, ACT, BLK)
-    outgoing = jnp.einsum("nak,nbl->bakl", blocks, blocks, preferred_element_type=jnp.float32)
-
-    row_grp = everyone // 8
-    col_grp = jnp.take(everyone, member, axis=1) // 8
-    zero_on = everyone[:, 0] == 0
+    id_rows = jnp.zeros((8, BLK), jnp.float32).at[0, :ACT].set(active_blocks[0].astype(jnp.float32))
+    id_rows = jnp.broadcast_to(id_rows[None, None], (n_mem, 1, 8, BLK))
     grp_ids = jnp.arange(n_grp, dtype=jnp.int32)
     q_ids = jnp.arange(per_row, dtype=jnp.int32)
 
@@ -117,10 +111,20 @@
         per_chunk = sizes[k]
         lo = starts[k]
         pos_ids = jnp.arange(per_chunk, dtype=jnp.int32)
-        piece = outgoing[:, lo:lo + per_chunk]
+        piece = jnp.einsum(
+            "nak,nbl->bakl", blocks[:, lo:lo + per_chunk], blocks, preferred_element_type=jnp.float32
+        )
         if prev is not None:
             piece, prev = lax.optimization_barrier((piece, prev))
+        else:
+            piece = jnp.concatenate([piece, id_rows], axis=2)
         got_piece = lax.all_to_all(piece, "mem", split_axis=0, concat_axis=0, tiled=True)
+        if prev is None:
+            everyone = got_piece[:, 0, BLK, :ACT].astype(jnp.int32)
+            got_piece = got_piece[:, :, :BLK]
+            row_grp = everyone // 8
+            col_grp = jnp.take(everyone, member, axis=1) // 8
+            zero_on = everyone[:, 0] == 0
         got_piece = got_piece.reshape(n_mem, per_chunk, BLK, BLK)
         prev = got_piece
         rg = row_grp[:, lo:lo + per_chunk]

time: 235 us -> 226 us (0.962)
  local copies, waits for them, and re-layouts: 25.5 us -> 16.4 us
  starting transfers between devices: 28.8 us -> 25.2 us
  waiting for transfers between devices: 122 us -> 125 us
    slice x3 -> x1, local copies, waits for them, and re-layouts: 7.7 us -> 0.01 us  [on_device_fast(): everyone = got_piece[:, 0, BLK, :ACT].astype(jnp.int32)]
    all_to_all x1 -> x0, starting transfers between devices: 5.17 us -> none  [on_device_fast(): lax.all_to_all(ids_out, 'mem', split_axis=0, concat_axis=0, tiled=True)]
    reduce_scatter x4, waiting for transfers between devices: 33 us -> 35.7 us  [on_device_fast(): got = lax.psum_scatter(send, 'grp', scatter_dimension=0, tiled=True)]
  transfers between devices with their start and end apart: 11 -> 10, of which waited for: 7 -> 7; matrix products, arithmetic and copies ran while one was open for 27% -> 23% of each run, Pallas kernels for 0% -> 0%
where the time goes in v4:
time: 226 us
  waiting for transfers between devices  125 us (55%)
  other arithmetic  29.4 us (13%)
  starting transfers between devices  25.2 us (11%)
  matrix products  16.6 us (7%)
  local copies, waits for them, and re-layouts  16.4 us (7%)
  between operations  13.5 us (6%)
    all_to_all x4, waiting for transfers between devices, on_device_fast(): lax.all_to_all(piece, 'mem', split_axis=0, concat_axis=0, tiled=True)  60.2 us
    reduce_scatter x4, waiting for transfers between devices, on_device_fast(): got = lax.psum_scatter(send, 'grp', scatter_dimension=0, tiled=True)  35.7 us
    all_to_all x4, starting transfers between devices, on_device_fast(): lax.all_to_all(piece, 'mem', split_axis=0, concat_axis=0, tiled=True)  15.9 us
    all_to_all x1, waiting for transfers between devices, on_device_fast(): pairs = lax.all_to_all(pair, 'mem', split_axis=0, concat_axis=0, tiled=True)  14.6 us
    all_to_all x1, waiting for transfers between devices, on_device_fast(): lax.all_to_all(spread, 'grp', split_axis=0, concat_axis=0, tiled=True)  13.9 us
    another operation x3, other arithmetic, on_device_fast(): chol = jnp.linalg.cholesky(a00)  12.4 us
    another operation x2, other arithmetic, on_device_fast(): lax.linalg.triangular_solve(chol, eye, left_side=True, lower=True)  10.4 us
    dot_general x4, matrix products, on_device_fast(): jnp.dot(sel.reshape(n_grp * width, n_mem * per_chunk).astype(jnp.float32)...  9.08 us
  transfers between devices with their start and end apart: 10, of which 7 were waited for; matrix products, arithmetic and copies ran while one was open for 23% of the time, Pallas kernels for 0%

profile of v4, /device:TPU:0, one launch (start us, length us, event | category | flops | bytes accessed | tf_op | source)
XLA Modules:
  0.0 225.6 jit_solution(18187430033410215662)
XLA Ops:
  6.5 0.7 convert_element_type.28
  7.2 1.2 copy.54
  8.4 0.3 convolution_bitcast_fusion.4
  8.8 0.8 maximum_bitcast_fusion
  9.6 5.2 %all-to-all-start = ((f32[8,1,136,128]{3,2,1,0:T(8,128)}), f32[8,1,136,128]{3,2,1,0:T(8,128)S(1)}, u32[]{:S(2)}, u32[]{:S(2)}) async-start(f32[8,1,136,128]{3,2,1,0:T(8,128)} %maximum_bitcast_fusion), calls=%async_computation | async-start | bytes 1114112 | tf_op jit(solution)/shard_map/all_to_all | solution.py:121
  14.8 10.0 %all-to-all-done = f32[8,1,136,128]{3,2,1,0:T(8,128)S(1)} async-done(((f32[8,1,136,128]{3,2,1,0:T(8,128)}), f32[8,1,136,128]{3,2,1,0:T(8,128)S(1)}, u32[]{:S(2)}, u32[]{:S(2)}) %all-to-all-start) | async-done | bytes 557088 | tf_op jit(solution)/shard_map/all_to_all | solution.py:121
  25.2 0.2 select_reduce_fusion.1
  25.8 0.9 fusion.13
  26.8 1.3 copy.58
  28.1 1.3 convolution_bitcast_fusion.2
  29.4 3.6 %all-to-all-start.1 = ((f32[8,2,128,128]{2,3,1,0:T(8,128)}), f32[8,2,128,128]{2,3,1,0:T(8,128)S(1)}, u32[]{:S(2)}, u32[]{:S(2)}) async-start(f32[8,2,128,128]{2,3,1,0:T(8,128)} %convolution_bitcast_fusion.2), calls=%async_computation.2 | async-start | bytes 2097152 | tf_op jit(solution)/shard_map/all_to_all | solution.py:121
  33.3 0.2 broadcast_and_fusion.2
  33.7 14.7 %all-to-all-done.1 = f32[8,2,128,128]{2,3,1,0:T(8,128)S(1)} async-done(((f32[8,2,128,128]{2,3,1,0:T(8,128)}), f32[8,2,128,128]{2,3,1,0:T(8,128)S(1)}, u32[]{:S(2)}, u32[]{:S(2)}) %all-to-all-start.1) | async-done | bytes 1048608 | tf_op jit(solution)/shard_map/all_to_all | solution.py:121
  48.3 0.3 copy.65
  48.7 2.8 %fusion.10 = f32[32,128,128]{2,0,1:T(8,128)} fusion(pred[32,16,1]{0,1,2:T(8,128)(4,1)S(1)} %reshape.545, f32[2,8,128,128]{3,2,1,0:T(8,128)S(1)} %bitcast.162), kind=kOutput, calls=%fused_computation.24 | convolution fusion | flops 100663296 | bytes 3146240 | tf_op jit(solution)/shard_map/dot_general | solution.py:146
  51.5 1.3 convolution_bitcast_fusion.3
  52.8 3.6 %all-to-all-start.2 = ((f32[8,2,128,128]{2,3,1,0:T(8,128)}), f32[8,2,128,128]{2,3,1,0:T(8,128)S(1)}, u32[]{:S(2)}, u32[]{:S(2)}) async-start(f32[8,2,128,128]{2,3,1,0:T(8,128)} %convolution_bitcast_fusion.3), calls=%async_computation.3 | async-start | bytes 2097152 | tf_op jit(solution)/shard_map/all_to_all | solution.py:121
  56.6 15.2 %all-to-all-done.2 = f32[8,2,128,128]{2,3,1,0:T(8,128)S(1)} async-done(((f32[8,2,128,128]{2,3,1,0:T(8,128)}), f32[8,2,128,128]{2,3,1,0:T(8,128)S(1)}, u32[]{:S(2)}, u32[]{:S(2)}) %all-to-all-start.2) | async-done | bytes 1048608 | tf_op jit(solution)/shard_map/all_to_all | solution.py:121
  71.7 0.3 copy.67
  72.1 2.8 %fusion.7 = f32[32,128,128]{2,0,1:T(8,128)} fusion(pred[32,16,1]{0,1,2:T(8,128)(4,1)S(1)} %reshape.546, f32[2,8,128,128]{3,2,1,0:T(8,128)S(1)} %bitcast.163), kind=kOutput, calls=%fused_computation.21 | convolution fusion | flops 100663296 | bytes 3146240 | tf_op jit(solution)/shard_map/dot_general | solution.py:146
  74.9 1.6 convolution_bitcast_fusion.1
  76.5 3.6 %all-to-all-start.3 = ((f32[8,3,128,128]{2,3,1,0:T(8,128)}), f32[8,3,128,128]{2,3,1,0:T(8,128)S(1)}, u32[]{:S(2)}, u32[]{:S(2)}) async-start(f32[8,3,128,128]{2,3,1,0:T(8,128)} %convolution_bitcast_fusion.1), calls=%async_computation.4 | async-start | bytes 3145728 | tf_op jit(solution)/shard_map/all_to_all | solution.py:121
  80.7 20.3 %all-to-all-done.3 = f32[8,3,128,128]{2,3,1,0:T(8,128)S(1)} async-done(((f32[8,3,128,128]{2,3,1,0:T(8,128)}), f32[8,3,128,128]{2,3,1,0:T(8,128)S(1)}, u32[]{:S(2)}, u32[]{:S(2)}) %all-to-all-start.3) | async-done | bytes 1572896 | tf_op jit(solution)/shard_map/all_to_all | solution.py:121
  101.1 0.5 copy.69
  101.5 2.5 %fusion.4 = f32[48,128,128]{2,0,1:T(8,128)S(1)} fusion(pred[48,24,1]{0,1,2:T(8,128)(4,1)S(1)} %reshape.547, f32[3,8,128,128]{3,2,1,0:T(8,128)S(1)} %bitcast.161), kind=kOutput, calls=%fused_computation.9 | convolution fusion | flops 226492416 | bytes 4719744 | tf_op jit(solution)/shard_map/dot_general | solution.py:146
  104.1 2.6 %copy.71 = f32[48,128,128]{2,1,0:T(8,128)} copy(f32[48,128,128]{2,0,1:T(8,128)S(1)} %fusion.4) | data formatting | bytes 6291456 | tf_op jit(solution)/shard_map/dot_general | solution.py:146
  106.7 0.8 slice.107
  107.7 0.7 broadcast_in_dim.82
  108.4 5.0 %all-to-all-start.4 = ((f32[4,128,128]{2,1,0:T(8,128)}), f32[4,128,128]{2,1,0:T(8,128)S(1)}, u32[]{:S(2)}, u32[]{:S(2)}) async-start(f32[4,128,128]{2,1,0:T(8,128)} %broadcast_in_dim.82), calls=%async_computation.5 | async-start | bytes 524288 | tf_op jit(solution)/shard_map/all_to_all | solution.py:160
  113.4 13.9 %all-to-all-done.4 = f32[4,128,128]{2,1,0:T(8,128)S(1)} async-done(((f32[4,128,128]{2,1,0:T(8,128)}), f32[4,128,128]{2,1,0:T(8,128)S(1)}, u32[]{:S(2)}, u32[]{:S(2)}) %all-to-all-start.4) | async-done | bytes 262176 | tf_op jit(solution)/shard_map/all_to_all | solution.py:160
  127.3 1.1 broadcast_in_dim.83
  128.4 4.2 %all-to-all-start.5 = ((f32[8,2,128,128]{3,2,1,0:T(8,128)}), f32[8,2,128,128]{3,2,1,0:T(8,128)S(1)}, u32[]{:S(2)}, u32[]{:S(2)}) async-start(f32[8,2,128,128]{3,2,1,0:T(8,128)} %broadcast_in_dim.83), calls=%async_computation.6 | async-start | bytes 2097152 | tf_op jit(solution)/shard_map/all_to_all | solution.py:162
  132.6 0.6 gather_fusion
  133.3 14.6 %all-to-all-done.5 = f32[8,2,128,128]{3,2,1,0:T(8,128)S(1)} async-done(((f32[8,2,128,128]{3,2,1,0:T(8,128)}), f32[8,2,128,128]{3,2,1,0:T(8,128)S(1)}, u32[]{:S(2)}, u32[]{:S(2)}) %all-to-all-start.5) | async-done | bytes 1048608 | tf_op jit(solution)/shard_map/all_to_all | solution.py:162
  148.1 11.7 %cholesky.23 = f32[128,128]{1,0:T(8,128)S(1)} custom-call(f32[128,128]{1,0:T(8,128)S(1)} %fusion.19), custom_call_target="Cholesky" | custom-call | tf_op jit(solution)/shard_map/jit(cholesky)/cholesky | solution.py:165
  159.9 0.6 compare_reduce_fusion
  160.5 0.6 select_bitcast_fusion
  161.1 9.8 %custom-call.6 = f32[1,128,128]{1,2,0:T(8,128)S(1)} custom-call(f32[1,128,128]{2,1,0:T(8,128)S(1)} %get-tuple-element.36), custom_call_target="InvertDiagBlocksLowerTriangular" | custom-call | tf_op jit(solution)/shard_map/triangular_solve | solution.py:166
  170.9 0.2 convolution_bitcast_fusion.5
  171.2 0.4 convolution_select_fusion.1
  171.6 0.8 copy.64
  172.4 0.6 convolution_select_fusion
  173.0 1.8 convolution_bitcast_fusion
  174.8 1.8 copy.74
  176.7 1.3 copy.72
  178.0 1.9 copy.73
  179.9 35.6 %reduce-scatter.11.cloned.1.call-done = f32[12,128,128]{2,1,0:T(8,128)} async-done(((f32[48,128,128]{2,1,0:T(8,128)}), f32[12,128,128]{2,1,0:T(8,128)}) %reduce-scatter.11.cloned.1.call-update) | async-done | bytes 786448 | tf_op jit(solution)/shard_map/reduce_scatter | solution.py:152
  215.6 3.5 %fusion.2 = f32[1,32,128,128]{3,2,1,0:T(8,128)} fusion(f32[12,128,128]{2,1,0:T(8,128)} %reduce-scatter.11.cloned.1.call-done, f32[8,128,128]{2,1,0:T(8,128)} %copy.73, f32[8,128,128]{2,1,0:T(8,128)S(1)} %copy.72, f32[4,128,128]{2,1,0:T(8,128)S(1)} %slice-done, f32[8,4,128,128]{3,2,1,0:T(8,128)S(1)} %copy-done, f32[32]{0:T(128)S(1)} %get-tuple-element.44, ...), kind=kLoop, calls=%fused_computation.4 | loop fusion | flops 5767168 | bytes 7160032 | tf_op jit(solution)/shard_map/broadcast_in_dim | solution.py:192
  (62 shorter events, 2.5 us)
Async XLA Ops:
  9.6 15.3 %all-to-all-start = ((f32[8,1,136,128]{3,2,1,0:T(8,128)}), f32[8,1,136,128]{3,2,1,0:T(8,128)S(1)}, u32[]{:S(2)}, u32[]{:S(2)}) async-start(f32[8,1,136,128]{3,2,1,0:T(8,128)} %maximum_bitcast_fusion), calls=%async_computation | async-start | bytes 1114112 | tf_op jit(solution)/shard_map/all_to_all | solution.py:121
  14.8 91.9 %reduce-scatter.5.cloned.1.call-start = ((), (), s32[]{:S(2)}) async-start(), calls=%async_computation.10 | async-start | bytes 1638400 | tf_op jit(solution)/shard_map/reduce_scatter | solution.py:152
  29.4 18.9 %all-to-all-start.1 = ((f32[8,2,128,128]{2,3,1,0:T(8,128)}), f32[8,2,128,128]{2,3,1,0:T(8,128)S(1)}, u32[]{:S(2)}, u32[]{:S(2)}) async-start(f32[8,2,128,128]{2,3,1,0:T(8,128)} %convolution_bitcast_fusion.2), calls=%async_computation.2 | async-start | bytes 2097152 | tf_op jit(solution)/shard_map/all_to_all | solution.py:121
  33.0 143.7 %reduce-scatter.7.cloned.1.call-start = ((), (), s32[]{:S(2)}) async-start(), calls=%async_computation.11 | async-start | bytes 2621440 | tf_op jit(solution)/shard_map/reduce_scatter | solution.py:152
  52.8 18.9 %all-to-all-start.2 = ((f32[8,2,128,128]{2,3,1,0:T(8,128)}), f32[8,2,128,128]{2,3,1,0:T(8,128)S(1)}, u32[]{:S(2)}, u32[]{:S(2)}) async-start(f32[8,2,128,128]{2,3,1,0:T(8,128)} %convolution_bitcast_fusion.3), calls=%async_computation.3 | async-start | bytes 2097152 | tf_op jit(solution)/shard_map/all_to_all | solution.py:121
  56.4 121.6 %reduce-scatter.9.cloned.1.call-start = ((), (), s32[]{:S(2)}) async-start(), calls=%async_computation.12 | async-start | bytes 2621440 | tf_op jit(solution)/shard_map/reduce_scatter | solution.py:152
  76.5 24.5 %all-to-all-start.3 = ((f32[8,3,128,128]{2,3,1,0:T(8,128)}), f32[8,3,128,128]{2,3,1,0:T(8,128)S(1)}, u32[]{:S(2)}, u32[]{:S(2)}) async-start(f32[8,3,128,128]{2,3,1,0:T(8,128)} %convolution_bitcast_fusion.1), calls=%async_computation.4 | async-start | bytes 3145728 | tf_op jit(solution)/shard_map/all_to_all | solution.py:121
  80.1 135.5 %reduce-scatter.11.cloned.1.call-start = ((), (), s32[]{:S(2)}) async-start(), calls=%async_computation.13 | async-start | bytes 3932160 | tf_op jit(solution)/shard_map/reduce_scatter | solution.py:152
  108.4 24.2 %copy-start.1 = (f32[4096]{0:T(1024)S(1)}, f32[4096]{0:T(1024)}, u32[]{:S(2)}) copy-start(f32[4096]{0:T(1024)} %param.7) | copy-start | bytes 49156
  108.4 18.9 %all-to-all-start.4 = ((f32[4,128,128]{2,1,0:T(8,128)}), f32[4,128,128]{2,1,0:T(8,128)S(1)}, u32[]{:S(2)}, u32[]{:S(2)}) async-start(f32[4,128,128]{2,1,0:T(8,128)} %broadcast_in_dim.82), calls=%async_computation.5 | async-start | bytes 524288 | tf_op jit(solution)/shard_map/all_to_all | solution.py:160
  128.4 19.6 %all-to-all-start.5 = ((f32[8,2,128,128]{3,2,1,0:T(8,128)}), f32[8,2,128,128]{3,2,1,0:T(8,128)S(1)}, u32[]{:S(2)}, u32[]{:S(2)}) async-start(f32[8,2,128,128]{3,2,1,0:T(8,128)} %broadcast_in_dim.83), calls=%async_computation.6 | async-start | bytes 2097152 | tf_op jit(solution)/shard_map/all_to_all | solution.py:162
  174.8 40.8 %slice-start = ((f32[5,128,128]{2,1,0:T(8,128)}), f32[4,128,128]{2,1,0:T(8,128)S(1)}, s32[]{:S(2)}) async-start(f32[5,128,128]{2,1,0:T(8,128)} %reduce-scatter.5.cloned.1.call-done), calls=%async_computation.14 | async-start | bytes 524288 | tf_op jit(solution)/shard_map/slice | solution.py:153
  176.7 38.9 %copy-start = (f32[8,4,128,128]{3,2,1,0:T(8,128)S(1)}, f32[8,4,128,128]{3,2,1,0:T(8,128)}, u32[]{:S(2)}) copy-start(f32[8,4,128,128]{3,2,1,0:T(8,128)} %copy.74) | copy-start | bytes 6291460
Sparse Core Ops, SparseCore 0:
  28.2 30.5 reduce-scatter.4
  61.2 42.6 reduce-scatter.6
  106.3 46.4 reduce-scatter.8
  154.9 60.6 reduce-scatter.10

commit v5 on v4

--- a/solution.py
+++ b/solution.py
@@ -149,7 +149,13 @@
             precision=HI,
             preferred_element_type=jnp.float32,
         ).reshape(n_grp * width, BLK, BLK)
-        got = lax.psum_scatter(send, "grp", scatter_dimension=0, tiled=True)
+        if k == len(sizes) - 1:
+            parts = lax.all_to_all(
+                send.reshape(n_grp, width, BLK, BLK), "grp", split_axis=0, concat_axis=0, tiled=True
+            )
+            got = jnp.sum(parts, axis=0)
+        else:
+            got = lax.psum_scatter(send, "grp", scatter_dimension=0, tiled=True)
         owned_parts.append(got[: per_chunk * per_row])
         if k == 0:
             col_tile = jnp.transpose(got[per_chunk * per_row]) / divisor

time: 226 us -> 253 us (1.12)
  local copies, waits for them, and re-layouts: 16.4 us -> 27.7 us
  matrix products: 16.6 us -> 22.7 us
  other arithmetic: 29.4 us -> 33.4 us
  starting transfers between devices: 25.2 us -> 29 us
    all_to_all x0 -> x1, waiting for transfers between devices: none -> 54.3 us  [on_device_fast(): lax.all_to_all(send.reshape(n_grp, width, BLK, BLK), 'grp', split_axis=0,...]
    reduce_scatter x4 -> x3, waiting for transfers between devices: 35.7 us -> 0.06 us  [on_device_fast(): got = lax.psum_scatter(send, 'grp', scatter_dimension=0, tiled=True)]
    all_to_all x4, waiting for transfers between devices: 60.2 us -> 51.8 us  [on_device_fast(): lax.all_to_all(piece, 'mem', split_axis=0, concat_axis=0, tiled=True)]
    all_to_all x1, waiting for transfers between devices: 14.6 us -> 9.19 us  [on_device_fast(): pairs = lax.all_to_all(pair, 'mem', split_axis=0, concat_axis=0, tiled=True)]
    all_to_all x1, waiting for transfers between devices: 13.9 us -> 9.06 us  [on_device_fast(): lax.all_to_all(spread, 'grp', split_axis=0, concat_axis=0, tiled=True)]
    broadcast_in_dim x0 -> x2, local copies, waits for them, and re-layouts: none -> 4.19 us  [the longest x1 2.54 us: on_device_fast(): return tiles[None]]
    all_to_all x0 -> x1, starting transfers between devices: none -> 3.7 us  [on_device_fast(): lax.all_to_all(send.reshape(n_grp, width, BLK, BLK), 'grp', split_axis=0,...]
    unnamed x7 -> x29, local copies, waits for them, and re-layouts: 1.37 us -> 4.87 us
  transfers between devices with their start and end apart: 10 -> 10, of which waited for: 7 -> 7; matrix products, arithmetic and copies ran while one was open for 23% -> 27% of each run, Pallas kernels for 0% -> 0%
where the time goes in v5:
time: 253 us; the launch traced here: 251 us
  waiting for transfers between devices  124 us (49%)
  other arithmetic  33.4 us (13%)
  starting transfers between devices  29 us (11%)
  local copies, waits for them, and re-layouts  27.7 us (11%)
  matrix products  22.7 us (9%)
  between operations  13.6 us (5%)
    all_to_all x1, waiting for transfers between devices, on_device_fast(): lax.all_to_all(send.reshape(n_grp, width, BLK, BLK), 'grp', split_axis=0,...  54.3 us
    all_to_all x4, waiting for transfers between devices, on_device_fast(): lax.all_to_all(piece, 'mem', split_axis=0, concat_axis=0, tiled=True)  51.8 us
    all_to_all x4, starting transfers between devices, on_device_fast(): lax.all_to_all(piece, 'mem', split_axis=0, concat_axis=0, tiled=True)  15.9 us
    another operation x3, other arithmetic, on_device_fast(): chol = jnp.linalg.cholesky(a00)  12.4 us
    dot_general x4, matrix products, on_device_fast(): jnp.dot(sel.reshape(n_grp * width, n_mem * per_chunk).astype(jnp.float32)...  11.8 us
    another operation x2, other arithmetic, on_device_fast(): lax.linalg.triangular_solve(chol, eye, left_side=True, lower=True)  10.4 us
    all_to_all x1, waiting for transfers between devices, on_device_fast(): pairs = lax.all_to_all(pair, 'mem', split_axis=0, concat_axis=0, tiled=True)  9.19 us
    all_to_all x1, waiting for transfers between devices, on_device_fast(): lax.all_to_all(spread, 'grp', split_axis=0, concat_axis=0, tiled=True)  9.06 us
  transfers between devices with their start and end apart: 10, of which 7 were waited for; matrix products, arithmetic and copies ran while one was open for 27% of the time, Pallas kernels for 0%

profile of v5, /device:TPU:0, one launch (start us, length us, event | category | flops | bytes accessed | tf_op | source)
XLA Modules:
  0.0 250.8 jit_solution(14270474618453654982)
XLA Ops:
  7.2 1.2 copy.39
  8.8 0.8 maximum_bitcast_fusion
  9.6 5.2 %all-to-all-start = ((f32[8,1,136,128]{3,2,1,0:T(8,128)}), f32[8,1,136,128]{3,2,1,0:T(8,128)S(1)}, u32[]{:S(2)}, u32[]{:S(2)}) async-start(f32[8,1,136,128]{3,2,1,0:T(8,128)} %maximum_bitcast_fusion), calls=%async_computation | async-start | bytes 1114112 | tf_op jit(solution)/shard_map/all_to_all | solution.py:121
  14.8 10.0 %all-to-all-done = f32[8,1,136,128]{3,2,1,0:T(8,128)S(1)} async-done(((f32[8,1,136,128]{3,2,1,0:T(8,128)}), f32[8,1,136,128]{3,2,1,0:T(8,128)S(1)}, u32[]{:S(2)}, u32[]{:S(2)}) %all-to-all-start) | async-done | bytes 557088 | tf_op jit(solution)/shard_map/all_to_all | solution.py:121
  25.9 0.9 fusion.12
  26.9 1.3 copy.44
  28.2 1.3 convolution_bitcast_fusion.2
  29.5 3.6 %all-to-all-start.1 = ((f32[8,2,128,128]{2,3,1,0:T(8,128)}), f32[8,2,128,128]{2,3,1,0:T(8,128)S(1)}, u32[]{:S(2)}, u32[]{:S(2)}) async-start(f32[8,2,128,128]{2,3,1,0:T(8,128)} %convolution_bitcast_fusion.2), calls=%async_computation.2 | async-start | bytes 2097152 | tf_op jit(solution)/shard_map/all_to_all | solution.py:121
  33.1 1.3 convolution_bitcast_fusion.3
  35.0 13.4 %all-to-all-done.1 = f32[8,2,128,128]{2,3,1,0:T(8,128)S(1)} async-done(((f32[8,2,128,128]{2,3,1,0:T(8,128)}), f32[8,2,128,128]{2,3,1,0:T(8,128)S(1)}, u32[]{:S(2)}, u32[]{:S(2)}) %all-to-all-start.1) | async-done | bytes 1048608 | tf_op jit(solution)/shard_map/all_to_all | solution.py:121
  48.4 3.6 %all-to-all-start.2 = ((f32[8,2,128,128]{2,3,1,0:T(8,128)}), f32[8,2,128,128]{2,3,1,0:T(8,128)S(1)}, u32[]{:S(2)}, u32[]{:S(2)}) async-start(f32[8,2,128,128]{2,3,1,0:T(8,128)} %convolution_bitcast_fusion.3), calls=%async_computation.3 | async-start | bytes 2097152 | tf_op jit(solution)/shard_map/all_to_all | solution.py:121
  52.0 1.3 copy.54
  53.3 4.0 %fusion.9 = f32[32,128,128]{2,0,1:T(8,128)} fusion(pred[32,16,1]{0,1,2:T(8,128)(4,1)S(1)} %reshape.554, f32[2,8,128,128]{3,2,1,0:T(8,128)} %bitcast.167), kind=kOutput, calls=%fused_computation.24 | convolution fusion | flops 100663296 | bytes 3146240 | tf_op jit(solution)/shard_map/dot_general | solution.py:146
  57.4 1.6 convolution_bitcast_fusion.1
  59.0 8.3 %all-to-all-done.2 = f32[8,2,128,128]{2,3,1,0:T(8,128)S(1)} async-done(((f32[8,2,128,128]{2,3,1,0:T(8,128)}), f32[8,2,128,128]{2,3,1,0:T(8,128)S(1)}, u32[]{:S(2)}, u32[]{:S(2)}) %all-to-all-start.2) | async-done | bytes 1048608 | tf_op jit(solution)/shard_map/all_to_all | solution.py:121
  67.3 1.0 copy-done.1
  68.3 3.6 %all-to-all-start.3 = ((f32[8,3,128,128]{2,3,1,0:T(8,128)}), f32[8,3,128,128]{2,3,1,0:T(8,128)S(1)}, u32[]{:S(2)}, u32[]{:S(2)}) async-start(f32[8,3,128,128]{2,3,1,0:T(8,128)} %convolution_bitcast_fusion.1), calls=%async_computation.4 | async-start | bytes 3145728 | tf_op jit(solution)/shard_map/all_to_all | solution.py:121
  71.9 0.8 slice.107
  72.9 20.0 %all-to-all-done.3 = f32[8,3,128,128]{2,3,1,0:T(8,128)S(1)} async-done(((f32[8,3,128,128]{2,3,1,0:T(8,128)}), f32[8,3,128,128]{2,3,1,0:T(8,128)S(1)}, u32[]{:S(2)}, u32[]{:S(2)}) %all-to-all-start.3) | async-done | bytes 1572896 | tf_op jit(solution)/shard_map/all_to_all | solution.py:121
  92.9 0.7 broadcast_in_dim.82
  93.6 4.9 %all-to-all-start.4 = ((f32[4,128,128]{2,1,0:T(8,128)}), f32[4,128,128]{2,1,0:T(8,128)S(1)}, u32[]{:S(2)}, u32[]{:S(2)}) async-start(f32[4,128,128]{2,1,0:T(8,128)} %broadcast_in_dim.82), calls=%async_computation.5 | async-start | bytes 524288 | tf_op jit(solution)/shard_map/all_to_all | solution.py:166
  98.5 9.1 %all-to-all-done.4 = f32[4,128,128]{2,1,0:T(8,128)S(1)} async-done(((f32[4,128,128]{2,1,0:T(8,128)}), f32[4,128,128]{2,1,0:T(8,128)S(1)}, u32[]{:S(2)}, u32[]{:S(2)}) %all-to-all-start.4) | async-done | bytes 262176 | tf_op jit(solution)/shard_map/all_to_all | solution.py:166
  107.6 1.1 broadcast_in_dim.83
  108.7 4.3 %all-to-all-start.5 = ((f32[8,2,128,128]{3,2,1,0:T(8,128)}), f32[8,2,128,128]{3,2,1,0:T(8,128)}, u32[]{:S(2)}, u32[]{:S(2)}) async-start(f32[8,2,128,128]{3,2,1,0:T(8,128)} %broadcast_in_dim.83), calls=%async_computation.6 | async-start | bytes 2097152 | tf_op jit(solution)/shard_map/all_to_all | solution.py:168
  113.7 2.8 %fusion.4 = f32[4,12,128,128]{3,1,2,0:T(8,128)S(1)} fusion(pred[4,12,24,1]{2,0,1,3:T(4,128)(4,1)S(1)} %bitcast.174, f32[3,8,128,128]{3,2,1,0:T(8,128)S(1)} %bitcast.166), kind=kOutput, calls=%fused_computation.10 | convolution fusion | flops 226492416 | bytes 4719744 | tf_op jit(solution)/shard_map/dot_general | solution.py:146
  116.6 2.6 %copy.61 = f32[4,12,128,128]{3,2,1,0:T(8,128)} copy(f32[4,12,128,128]{3,1,2,0:T(8,128)S(1)} %fusion.4) | data formatting | bytes 6291456 | tf_op jit(solution)/shard_map/dot_general | solution.py:146
  119.2 9.2 %all-to-all-done.5 = f32[8,2,128,128]{3,2,1,0:T(8,128)} async-done(((f32[8,2,128,128]{3,2,1,0:T(8,128)}), f32[8,2,128,128]{3,2,1,0:T(8,128)}, u32[]{:S(2)}, u32[]{:S(2)}) %all-to-all-start.5) | async-done | bytes 1048608 | tf_op jit(solution)/shard_map/all_to_all | solution.py:168
  128.4 3.7 %all-to-all-start.6 = ((f32[4,12,128,128]{3,2,1,0:T(8,128)}), f32[4,12,128,128]{3,2,1,0:T(8,128)S(1)}, u32[]{:S(2)}, u32[]{:S(2)}) async-start(f32[4,12,128,128]{3,2,1,0:T(8,128)} %copy.61), calls=%async_computation.9 | async-start | bytes 6291456 | tf_op jit(solution)/shard_map/all_to_all | solution.py:153
  132.4 2.6 %copy.56 = f32[8,2,128,128]{3,2,1,0:T(8,128)} copy(f32[8,2,128,128]{2,3,1,0:T(8,128)} %copy-done.1) | data formatting | bytes 2097152 | tf_op jit(solution)/shard_map/all_to_all | solution.py:121
  135.0 4.0 %fusion.6 = f32[32,128,128]{2,0,1:T(8,128)} fusion(pred[32,16,1]{0,1,2:T(8,128)(4,1)S(1)} %reshape.555, f32[2,8,128,128]{3,2,1,0:T(8,128)} %bitcast.168), kind=kOutput, calls=%fused_computation.21 | convolution fusion | flops 100663296 | bytes 3146240 | tf_op jit(solution)/shard_map/dot_general | solution.py:146
  142.6 0.9 copy.81
  143.5 0.9 fusion.16
  144.4 0.9 fusion.18
  145.3 11.7 %cholesky.23 = f32[128,128]{1,0:T(8,128)S(1)} custom-call(f32[128,128]{1,0:T(8,128)S(1)} %fusion.18), custom_call_target="Cholesky" | custom-call | tf_op jit(solution)/shard_map/jit(cholesky)/cholesky | solution.py:171
  158.4 9.8 %custom-call.6 = f32[1,128,128]{1,2,0:T(8,128)S(1)} custom-call(f32[1,128,128]{2,1,0:T(8,128)S(1)} %get-tuple-element.36), custom_call_target="InvertDiagBlocksLowerTriangular" | custom-call | tf_op jit(solution)/shard_map/triangular_solve | solution.py:172
  168.4 1.3 convolution_select_fusion.1
  169.8 0.8 copy.50
  170.6 1.6 convolution_select_fusion
  172.2 1.1 copy.51
  173.3 3.2 %convolution_bitcast_fusion = f32[8,4,128,128]{2,3,0,1:T(8,128)} fusion(f32[8,128,128]{2,1,0:T(8,128)S(1)} %convolution_select_fusion, f32[4,128,128]{2,1,0:T(8,128)S(1)} %convolution_select_fusion.1), kind=kOutput, calls=%fused_computation.7 | convolution fusion | flops 805306368 | bytes 2883584 | tf_op jit(solution)/shard_map/apr,qsr->aqps/dot_general | solution.py:188
  176.5 2.9 %copy.63 = f32[8,4,128,128]{3,2,1,0:T(8,128)} copy(f32[8,4,128,128]{2,3,0,1:T(8,128)} %convolution_bitcast_fusion) | data formatting | bytes 4194304 | tf_op jit(solution)/shard_map/apr,qsr->aqps/transpose | solution.py:188
  179.5 54.3 %all-to-all-done.6 = f32[4,12,128,128]{3,2,1,0:T(8,128)S(1)} async-done(((f32[4,12,128,128]{3,2,1,0:T(8,128)}), f32[4,12,128,128]{3,2,1,0:T(8,128)S(1)}, u32[]{:S(2)}, u32[]{:S(2)}) %all-to-all-start.6) | async-done | bytes 3145760 | tf_op jit(solution)/shard_map/all_to_all | solution.py:153
  233.7 1.2 reduce_sum.9
  234.9 1.6 copy.78
  236.7 1.4 tile.4
  238.0 1.7 broadcast_in_dim.91
  239.8 2.0 fusion.2
  241.8 2.5 %copy.65 = f32[1,32,128,128]{3,2,1,0:T(8,128)} copy(f32[1,32,128,128]{3,1,2,0:T(8,128)S(1)} %fusion.2) | data formatting | bytes 4194304 | tf_op jit(solution)/shard_map/broadcast_in_dim | solution.py:198
  (88 shorter events, 9.2 us)
Async XLA Ops:
  9.6 15.3 %all-to-all-start = ((f32[8,1,136,128]{3,2,1,0:T(8,128)}), f32[8,1,136,128]{3,2,1,0:T(8,128)S(1)}, u32[]{:S(2)}, u32[]{:S(2)}) async-start(f32[8,1,136,128]{3,2,1,0:T(8,128)} %maximum_bitcast_fusion), calls=%async_computation | async-start | bytes 1114112 | tf_op jit(solution)/shard_map/all_to_all | solution.py:121
  14.8 57.1 %reduce-scatter.4.cloned.1.call-start = ((), (), s32[]{:S(2)}) async-start(), calls=%async_computation.10 | async-start | bytes 1638400 | tf_op jit(solution)/shard_map/reduce_scatter | solution.py:158
  29.5 18.9 %all-to-all-start.1 = ((f32[8,2,128,128]{2,3,1,0:T(8,128)}), f32[8,2,128,128]{2,3,1,0:T(8,128)S(1)}, u32[]{:S(2)}, u32[]{:S(2)}) async-start(f32[8,2,128,128]{2,3,1,0:T(8,128)} %convolution_bitcast_fusion.2), calls=%async_computation.2 | async-start | bytes 2097152 | tf_op jit(solution)/shard_map/all_to_all | solution.py:121
  48.4 18.9 %all-to-all-start.2 = ((f32[8,2,128,128]{2,3,1,0:T(8,128)}), f32[8,2,128,128]{2,3,1,0:T(8,128)S(1)}, u32[]{:S(2)}, u32[]{:S(2)}) async-start(f32[8,2,128,128]{2,3,1,0:T(8,128)} %convolution_bitcast_fusion.3), calls=%async_computation.3 | async-start | bytes 2097152 | tf_op jit(solution)/shard_map/all_to_all | solution.py:121
  52.0 184.6 %reduce-scatter.6.cloned.1.call-start = ((), (), s32[]{:S(2)}) async-start(), calls=%async_computation.11 | async-start | bytes 2621440 | tf_op jit(solution)/shard_map/reduce_scatter | solution.py:158
  67.3 1.0 copy-start.1
  68.3 24.5 %all-to-all-start.3 = ((f32[8,3,128,128]{2,3,1,0:T(8,128)}), f32[8,3,128,128]{2,3,1,0:T(8,128)S(1)}, u32[]{:S(2)}, u32[]{:S(2)}) async-start(f32[8,3,128,128]{2,3,1,0:T(8,128)} %convolution_bitcast_fusion.1), calls=%async_computation.4 | async-start | bytes 3145728 | tf_op jit(solution)/shard_map/all_to_all | solution.py:121
  93.6 14.0 %all-to-all-start.4 = ((f32[4,128,128]{2,1,0:T(8,128)}), f32[4,128,128]{2,1,0:T(8,128)S(1)}, u32[]{:S(2)}, u32[]{:S(2)}) async-start(f32[4,128,128]{2,1,0:T(8,128)} %broadcast_in_dim.82), calls=%async_computation.5 | async-start | bytes 524288 | tf_op jit(solution)/shard_map/all_to_all | solution.py:166
  107.6 5.5 %copy-start.2 = (f32[4,128,128]{2,1,0:T(8,128)}, f32[4,128,128]{2,1,0:T(8,128)S(1)}, u32[]{:S(2)}) copy-start(f32[4,128,128]{2,1,0:T(8,128)S(1)} %all-to-all-done.4) | copy-start | bytes 786436
  108.7 19.7 %all-to-all-start.5 = ((f32[8,2,128,128]{3,2,1,0:T(8,128)}), f32[8,2,128,128]{3,2,1,0:T(8,128)}, u32[]{:S(2)}, u32[]{:S(2)}) async-start(f32[8,2,128,128]{3,2,1,0:T(8,128)} %broadcast_in_dim.83), calls=%async_computation.6 | async-start | bytes 2097152 | tf_op jit(solution)/shard_map/all_to_all | solution.py:168
  128.4 105.4 %all-to-all-start.6 = ((f32[4,12,128,128]{3,2,1,0:T(8,128)}), f32[4,12,128,128]{3,2,1,0:T(8,128)S(1)}, u32[]{:S(2)}, u32[]{:S(2)}) async-start(f32[4,12,128,128]{3,2,1,0:T(8,128)} %copy.61), calls=%async_computation.9 | async-start | bytes 6291456 | tf_op jit(solution)/shard_map/all_to_all | solution.py:153
  132.1 104.5 %reduce-scatter.8.cloned.1.call-start = ((), (), s32[]{:S(2)}) async-start(), calls=%async_computation.12 | async-start | bytes 2621440 | tf_op jit(solution)/shard_map/reduce_scatter | solution.py:158
  135.0 4.0 %copy-start.4 = (f32[4096]{0:T(1024)S(1)}, f32[4096]{0:T(1024)}, u32[]{:S(2)}) copy-start(f32[4096]{0:T(1024)} %param.7) | copy-start | bytes 49156
  139.0 3.6 %slice-start = ((f32[5,128,128]{2,1,0:T(8,128)}), f32[4,128,128]{2,1,0:T(8,128)S(1)}, s32[]{:S(2)}) async-start(f32[5,128,128]{2,1,0:T(8,128)} %reduce-scatter.4.cloned.1.call-done), calls=%async_computation.13 | async-start | bytes 524288 | tf_op jit(solution)/shard_map/slice | solution.py:159
  236.5 3.2 %copy-start = (f32[8,4,128,128]{3,2,1,0:T(8,128)S(1)}, f32[8,4,128,128]{3,2,1,0:T(8,128)}, u32[]{:S(2)}) copy-start(f32[8,4,128,128]{3,2,1,0:T(8,128)} %copy.63) | copy-start | bytes 6291460
  236.5 3.2 %copy-start.3 = (f32[4,128,128]{2,0,1:T(4,128)S(1)}, f32[4,128,128]{2,0,1:T(4,128)}, u32[]{:S(2)}) copy-start(f32[4,128,128]{2,0,1:T(4,128)} %copy.81) | copy-start | bytes 786436
  236.5 3.2 %copy-start.7 = (f32[128,128]{1,0:T(8,128)S(1)}, f32[128,128]{1,0:T(8,128)}, u32[]{:S(2)}) copy-start(f32[128,128]{1,0:T(8,128)} %fusion.19) | copy-start | bytes 196612
  236.5 3.2 %copy-start.8 = (f32[32]{0:T(128)S(1)}, f32[32]{0:T(128)}, u32[]{:S(2)}) copy-start(f32[32]{0:T(128)} %get-tuple-element.44) | copy-start | bytes 388
  236.5 3.2 %copy-start.9 = (pred[32]{0:T(512)(128)(4,1)S(1)}, pred[32]{0:T(512)(128)(4,1)}, u32[]{:S(2)}) copy-start(pred[32]{0:T(512)(128)(4,1)} %get-tuple-element.45) | copy-start | bytes 100
  236.6 3.2 %copy-start.10 = (pred[32]{0:T(512)(128)(4,1)S(1)}, pred[32]{0:T(512)(128)(4,1)}, u32[]{:S(2)}) copy-start(pred[32]{0:T(512)(128)(4,1)} %get-tuple-element.46) | copy-start | bytes 100
  236.6 3.2 %copy-start.11 = (pred[32]{0:T(512)(128)(4,1)S(1)}, pred[32]{0:T(512)(128)(4,1)}, u32[]{:S(2)}) copy-start(pred[32]{0:T(512)(128)(4,1)} %get-tuple-element.47) | copy-start | bytes 100
  236.6 3.1 %copy-start.5 = (f32[8,128,128]{2,0,1:T(8,128)S(1)}, f32[8,128,128]{2,0,1:T(8,128)}, u32[]{:S(2)}) copy-start(f32[8,128,128]{2,0,1:T(8,128)} %reduce-scatter.6.cloned.1.call-done) | copy-start | bytes 1572868
  236.6 3.1 %copy-start.6 = (f32[8,128,128]{2,0,1:T(8,128)S(1)}, f32[8,128,128]{2,0,1:T(8,128)}, u32[]{:S(2)}) copy-start(f32[8,128,128]{2,0,1:T(8,128)} %reduce-scatter.8.cloned.1.call-done) | copy-start | bytes 1572868
Sparse Core Ops, SparseCore 0:
  28.3 30.5 reduce-scatter.3
  61.2 44.1 reduce-scatter.5
  139.2 84.2 reduce-scatter.7

commit v6 on v4

--- a/solution.py
+++ b/solution.py
@@ -94,6 +94,7 @@
     per_row = NB // ACT
     sizes = (1, 2, 2, 3)
     starts = (0, 1, 3, 5)
+    tail = starts[-1]
     row_count = design.shape[0]
     divisor = jnp.float32(row_count * n_grp * n_mem // 16)
     eye = jnp.eye(BLK, dtype=jnp.float32)
@@ -101,22 +102,24 @@
 
     blocks = design.reshape(row_count, ACT, BLK)
     id_rows = jnp.zeros((8, BLK), jnp.float32).at[0, :ACT].set(active_blocks[0].astype(jnp.float32))
-    id_rows = jnp.broadcast_to(id_rows[None, None], (n_mem, 1, 8, BLK))
+    id_rows = jnp.broadcast_to(id_rows[None, None], (n_mem, 2, 8, BLK))
     grp_ids = jnp.arange(n_grp, dtype=jnp.int32)
     q_ids = jnp.arange(per_row, dtype=jnp.int32)
 
-    owned_parts = []
+    by_d = {}
     prev = None
     for k in range(len(sizes)):
         per_chunk = sizes[k]
         lo = starts[k]
         pos_ids = jnp.arange(per_chunk, dtype=jnp.int32)
-        piece = jnp.einsum(
-            "nak,nbl->bakl", blocks[:, lo:lo + per_chunk], blocks, preferred_element_type=jnp.float32
-        )
+        rows_at = [[(b + lo + dl) % ACT for dl in range(per_chunk)] for b in range(n_mem)]
+        left = blocks[:, jnp.array(rows_at, dtype=jnp.int32)]
+        piece = jnp.einsum("nbdk,nbl->bdkl", left, blocks, preferred_element_type=jnp.float32)
         if prev is not None:
             piece, prev = lax.optimization_barrier((piece, prev))
         else:
+            row0 = jnp.einsum("nk,nbl->bkl", blocks[:, 0], blocks, preferred_element_type=jnp.float32)
+            piece = jnp.concatenate([piece, row0[:, None]], axis=1)
             piece = jnp.concatenate([piece, id_rows], axis=2)
         got_piece = lax.all_to_all(piece, "mem", split_axis=0, concat_axis=0, tiled=True)
         if prev is None:
@@ -125,35 +128,60 @@
             row_grp = everyone // 8
             col_grp = jnp.take(everyone, member, axis=1) // 8
             zero_on = everyone[:, 0] == 0
-        got_piece = got_piece.reshape(n_mem, per_chunk, BLK, BLK)
+            row0_got = got_piece[:, per_chunk]
+            got_piece = got_piece[:, :per_chunk]
         prev = got_piece
-        rg = row_grp[:, lo:lo + per_chunk]
+        flat = got_piece.reshape(n_mem * per_chunk, BLK * BLK)
+        apos = (member + lo + pos_ids) % ACT
+        rg = jnp.take(row_grp, apos, axis=1)
         sel = (
             (pos_ids[None, :, None, None, None] == pos_ids[None, None, None, None, :])
             & (rg[None, None, None, :, :] == grp_ids[:, None, None, None, None])
             & (col_grp[None, None, None, :, None] == q_ids[None, None, :, None, None])
         )
-        sel = sel.reshape(n_grp, per_chunk * per_row, n_mem * per_chunk)
+        if lo >= tail:
+            sel = jnp.stack([sel[g][:, [q for q in range(per_row) if q != g]] for g in range(n_grp)])
+        kept = sel.shape[2]
+        sel = sel.reshape(n_grp, per_chunk * kept, n_mem * per_chunk)
         if k == 0:
-            first = pos_ids == 0
             col_sel = (
-                (col_grp[None, :, None] == grp_ids[:, None, None])
-                & zero_on[None, :, None]
-                & first[None, None, :]
-            ).reshape(n_grp, 1, n_mem * per_chunk)
-            sel = jnp.concatenate([sel, col_sel], axis=1)
-        width = sel.shape[1]
+                (col_grp[None, :] == grp_ids[:, None]) & zero_on[None, :]
+            ).astype(jnp.float32)
+            col_part = jnp.dot(
+                col_sel, row0_got.reshape(n_mem, BLK * BLK), precision=HI,
+                preferred_element_type=jnp.float32,
+            ).reshape(n_grp, 1, BLK * BLK)
         send = jnp.dot(
-            sel.reshape(n_grp * width, n_mem * per_chunk).astype(jnp.float32),
-            got_piece.reshape(n_mem * per_chunk, BLK * BLK),
+            sel.reshape(n_grp * per_chunk * kept, n_mem * per_chunk).astype(jnp.float32),
+            flat,
             precision=HI,
             preferred_element_type=jnp.float32,
-        ).reshape(n_grp * width, BLK, BLK)
-        got = lax.psum_scatter(send, "grp", scatter_dimension=0, tiled=True)
-        owned_parts.append(got[: per_chunk * per_row])
+        ).reshape(n_grp, per_chunk * kept, BLK * BLK)
         if k == 0:
-            col_tile = jnp.transpose(got[per_chunk * per_row]) / divisor
-    owned = jnp.concatenate(owned_parts, axis=0)
+            send = jnp.concatenate([send, col_part], axis=1)
+        width = send.shape[1]
+        got = lax.psum_scatter(
+            send.reshape(n_grp * width, BLK, BLK), "grp", scatter_dimension=0, tiled=True
+        )
+        if k == 0:
+            col_tile = jnp.transpose(got[per_chunk * kept]) / divisor
+            got = got[: per_chunk * kept]
+        got = got.reshape(per_chunk, kept, BLK, BLK)
+        for dl in range(per_chunk):
+            by_d[lo + dl] = got[dl]
+
+    for d in range(tail, ACT):
+        shift = ACT - d
+        src_tile = jnp.transpose(jnp.take(by_d[shift], group, axis=0))
+        moved = lax.ppermute(
+            src_tile, "mem", perm=[(j, (j + shift) % n_mem) for j in range(n_mem)]
+        )
+        others = by_d[d]
+        q_pos = jnp.clip(q_ids - (q_ids > group).astype(jnp.int32), 0, per_row - 2)
+        spread = jnp.take(others, q_pos, axis=0)
+        by_d[d] = jnp.where((q_ids == group)[:, None, None], moved[None], spread)
+    owned_d = jnp.stack([by_d[d] for d in range(ACT)])
+    owned = jnp.roll(owned_d, member, axis=0).reshape(ACT * per_row, BLK, BLK)
 
     col_tile, prev = lax.optimization_barrier((col_tile, prev))
     spread = jnp.broadcast_to(col_tile[None], (n_grp, BLK, BLK))

time: 226 us -> 244 us (1.080)
  local copies, waits for them, and re-layouts: 16.4 us -> 47.1 us
  waiting for transfers between devices: 125 us -> 97.6 us
  other arithmetic: 29.4 us -> 42.3 us
    reduce_scatter x4, waiting for transfers between devices: 35.7 us -> 11.7 us  [on_device_fast(): lax.psum_scatter(send.reshape(n_grp * width, BLK, BLK), 'grp', scatter_di...]
    unnamed x7 -> x55, local copies, waits for them, and re-layouts: 1.37 us -> 14.3 us
    gather x0 -> x17, local copies, waits for them, and re-layouts: none -> 9.13 us  [the longest x6 2.71 us: on_device_fast(): spread = jnp.take(others, q_pos, axis=0)]
    unnamed x0 -> x5, other arithmetic: none -> 6.43 us
    reshape x1 -> x4, local copies, waits for them, and re-layouts: 0.09 us -> 4.82 us  [the longest x2 4.54 us: on_device_fast(): send.reshape(n_grp * width, BLK, BLK)]
    all_to_all x1, waiting for transfers between devices: 14.6 us -> 11.2 us  [on_device_fast(): pairs = lax.all_to_all(pair, 'mem', split_axis=0, concat_axis=0, tiled=True)]
    reduce_scatter x2 -> x0, local copies, waits for them, and re-layouts: 3.25 us -> none  [on_device_fast(): got = lax.psum_scatter(send, 'grp', scatter_dimension=0, tiled=True)]
    all_to_all x1, waiting for transfers between devices: 13.9 us -> 10.9 us  [on_device_fast(): lax.all_to_all(spread, 'grp', split_axis=0, concat_axis=0, tiled=True)]
  transfers between devices with their start and end apart: 10 -> 13, of which waited for: 7 -> 9; matrix products, arithmetic and copies ran while one was open for 23% -> 29% of each run, Pallas kernels for 0% -> 0%
where the time goes in v6:
time: 244 us; the launch traced here: 243 us
  waiting for transfers between devices  97.6 us (40%)
  local copies, waits for them, and re-layouts  47.1 us (19%)
  other arithmetic  42.3 us (17%)
  starting transfers between devices  25.1 us (10%)
  matrix products  17.2 us (7%)
  between operations  14 us (6%)
    all_to_all x4, waiting for transfers between devices, on_device_fast(): lax.all_to_all(piece, 'mem', split_axis=0, concat_axis=0, tiled=True)  61.5 us
    all_to_all x4, starting transfers between devices, on_device_fast(): lax.all_to_all(piece, 'mem', split_axis=0, concat_axis=0, tiled=True)  15.9 us
    unnamed x55, local copies, waits for them, and re-layouts  14.3 us
    another operation x3, other arithmetic, on_device_fast(): chol = jnp.linalg.cholesky(a00)  12.4 us
    reduce_scatter x4, waiting for transfers between devices, on_device_fast(): lax.psum_scatter(send.reshape(n_grp * width, BLK, BLK), 'grp', scatter_di...  11.7 us
    all_to_all x1, waiting for transfers between devices, on_device_fast(): pairs = lax.all_to_all(pair, 'mem', split_axis=0, concat_axis=0, tiled=True)  11.2 us
    all_to_all x1, waiting for transfers between devices, on_device_fast(): lax.all_to_all(spread, 'grp', split_axis=0, concat_axis=0, tiled=True)  10.9 us
    another operation x2, other arithmetic, on_device_fast(): lax.linalg.triangular_solve(chol, eye, left_side=True, lower=True)  10.4 us
  transfers between devices with their start and end apart: 13, of which 9 were waited for; matrix products, arithmetic and copies ran while one was open for 29% of the time, Pallas kernels for 0%

profile of v6, /device:TPU:0, one launch (start us, length us, event | category | flops | bytes accessed | tf_op | source)
XLA Modules:
  0.0 243.4 jit_solution(2086479670568712254)
XLA Ops:
  6.5 1.3 copy.69
  9.2 1.1 copy.72
  10.2 5.2 %all-to-all-start = ((f32[8,2,136,128]{3,2,1,0:T(8,128)}), f32[8,2,136,128]{3,2,1,0:T(8,128)S(1)}, u32[]{:S(2)}, u32[]{:S(2)}) async-start(f32[8,2,136,128]{3,2,1,0:T(8,128)} %copy.72), calls=%async_computation | async-start | bytes 2228224 | tf_op jit(solution)/shard_map/all_to_all | solution.py:124
  15.5 16.0 %all-to-all-done = f32[8,2,136,128]{3,2,1,0:T(8,128)S(1)} async-done(((f32[8,2,136,128]{3,2,1,0:T(8,128)}), f32[8,2,136,128]{3,2,1,0:T(8,128)S(1)}, u32[]{:S(2)}, u32[]{:S(2)}) %all-to-all-start) | async-done | bytes 1114144 | tf_op jit(solution)/shard_map/all_to_all | solution.py:124
  34.2 1.7 reshape.533
  35.9 2.8 %copy.78 = f32[20,128,128]{1,2,0:T(8,128)} copy(f32[20,128,128]{2,1,0:T(8,128)} %reshape.533) | data formatting | bytes 2621440 | tf_op jit(solution)/shard_map/reshape | solution.py:164
  39.5 1.4 fusion.55
  40.9 3.6 %all-to-all-start.1 = ((f32[8,2,128,128]{3,2,1,0:T(8,128)}), f32[8,2,128,128]{3,2,1,0:T(8,128)S(1)}, u32[]{:S(2)}, u32[]{:S(2)}) async-start(f32[8,2,128,128]{3,2,1,0:T(8,128)} %fusion.55), calls=%async_computation.2 | async-start | bytes 2097152 | tf_op jit(solution)/shard_map/all_to_all | solution.py:124
  46.6 13.2 %all-to-all-done.1 = f32[8,2,128,128]{3,2,1,0:T(8,128)S(1)} async-done(((f32[8,2,128,128]{3,2,1,0:T(8,128)}), f32[8,2,128,128]{3,2,1,0:T(8,128)S(1)}, u32[]{:S(2)}, u32[]{:S(2)}) %all-to-all-start.1) | async-done | bytes 1048608 | tf_op jit(solution)/shard_map/all_to_all | solution.py:124
  59.8 1.0 copy-done.1
  60.8 2.7 %fusion.9 = f32[32,128,128]{2,0,1:T(8,128)S(1)} fusion(pred[32,16,1]{0,1,2:T(8,128)(4,1)S(1)} %reshape.819, f32[2,8,128,128]{3,2,1,0:T(8,128)} %bitcast.243), kind=kOutput, calls=%fused_computation.37 | convolution fusion | flops 100663296 | bytes 3146240 | tf_op jit(solution)/shard_map/dot_general | solution.py:154
  63.4 1.9 copy.87
  66.0 1.4 fusion.54
  67.4 3.6 %all-to-all-start.2 = ((f32[8,2,128,128]{3,2,1,0:T(8,128)}), f32[8,2,128,128]{3,2,1,0:T(8,128)S(1)}, u32[]{:S(2)}, u32[]{:S(2)}) async-start(f32[8,2,128,128]{3,2,1,0:T(8,128)} %fusion.54), calls=%async_computation.3 | async-start | bytes 2097152 | tf_op jit(solution)/shard_map/all_to_all | solution.py:124
  71.1 15.2 %all-to-all-done.2 = f32[8,2,128,128]{3,2,1,0:T(8,128)S(1)} async-done(((f32[8,2,128,128]{3,2,1,0:T(8,128)}), f32[8,2,128,128]{3,2,1,0:T(8,128)S(1)}, u32[]{:S(2)}, u32[]{:S(2)}) %all-to-all-start.2) | async-done | bytes 1048608 | tf_op jit(solution)/shard_map/all_to_all | solution.py:124
  86.3 1.0 copy-done.2
  87.3 2.7 %fusion.6 = f32[32,128,128]{2,0,1:T(8,128)S(1)} fusion(pred[32,16,1]{0,1,2:T(8,128)(4,1)S(1)} %reshape.820, f32[2,8,128,128]{3,2,1,0:T(8,128)} %bitcast.244), kind=kOutput, calls=%fused_computation.34 | convolution fusion | flops 100663296 | bytes 3146240 | tf_op jit(solution)/shard_map/dot_general | solution.py:154
  89.9 1.9 copy.90
  92.7 1.7 fusion.53
  95.0 3.6 %all-to-all-start.3 = ((f32[8,3,128,128]{3,2,1,0:T(8,128)}), f32[8,3,128,128]{3,2,1,0:T(8,128)S(1)}, u32[]{:S(2)}, u32[]{:S(2)}) async-start(f32[8,3,128,128]{3,2,1,0:T(8,128)} %fusion.53), calls=%async_computation.4 | async-start | bytes 3145728 | tf_op jit(solution)/shard_map/all_to_all | solution.py:124
  101.7 0.8 fusion.23
  102.5 17.1 %all-to-all-done.3 = f32[8,3,128,128]{3,2,1,0:T(8,128)S(1)} async-done(((f32[8,3,128,128]{3,2,1,0:T(8,128)}), f32[8,3,128,128]{3,2,1,0:T(8,128)S(1)}, u32[]{:S(2)}, u32[]{:S(2)}) %all-to-all-start.3) | async-done | bytes 1572896 | tf_op jit(solution)/shard_map/all_to_all | solution.py:124
  120.3 4.9 %all-to-all-start.4 = ((f32[4,128,128]{2,1,0:T(8,128)}), f32[4,128,128]{2,1,0:T(8,128)S(1)}, u32[]{:S(2)}, u32[]{:S(2)}) async-start(f32[4,128,128]{2,1,0:T(8,128)} %broadcast_in_dim.239), calls=%async_computation.5 | async-start | bytes 524288 | tf_op jit(solution)/shard_map/all_to_all | solution.py:188
  125.2 2.4 fusion.3
  127.6 1.9 copy.95
  130.0 10.9 %all-to-all-done.4 = f32[4,128,128]{2,1,0:T(8,128)S(1)} async-done(((f32[4,128,128]{2,1,0:T(8,128)}), f32[4,128,128]{2,1,0:T(8,128)S(1)}, u32[]{:S(2)}, u32[]{:S(2)}) %all-to-all-start.4) | async-done | bytes 262176 | tf_op jit(solution)/shard_map/all_to_all | solution.py:188
  141.0 1.1 broadcast_in_dim.240
  142.1 3.6 %all-to-all-start.5 = ((f32[8,2,128,128]{3,2,1,0:T(8,128)}), f32[8,2,128,128]{3,2,1,0:T(8,128)S(1)}, u32[]{:S(2)}, u32[]{:S(2)}) async-start(f32[8,2,128,128]{3,2,1,0:T(8,128)} %broadcast_in_dim.240), calls=%async_computation.6 | async-start | bytes 2097152 | tf_op jit(solution)/shard_map/all_to_all | solution.py:190
  149.8 11.2 %all-to-all-done.5 = f32[8,2,128,128]{3,2,1,0:T(8,128)S(1)} async-done(((f32[8,2,128,128]{3,2,1,0:T(8,128)}), f32[8,2,128,128]{3,2,1,0:T(8,128)S(1)}, u32[]{:S(2)}, u32[]{:S(2)}) %all-to-all-start.5) | async-done | bytes 1048608 | tf_op jit(solution)/shard_map/all_to_all | solution.py:190
  161.1 11.7 %cholesky.23 = f32[128,128]{1,0:T(8,128)S(1)} custom-call(f32[128,128]{1,0:T(8,128)S(1)} %fusion.25), custom_call_target="Cholesky" | custom-call | tf_op jit(solution)/shard_map/jit(cholesky)/cholesky | solution.py:193
  174.2 9.8 %custom-call.6 = f32[1,128,128]{1,2,0:T(8,128)S(1)} custom-call(f32[1,128,128]{2,1,0:T(8,128)S(1)} %get-tuple-element.61), custom_call_target="InvertDiagBlocksLowerTriangular" | custom-call | tf_op jit(solution)/shard_map/triangular_solve | solution.py:194
  185.4 1.8 convolution_bitcast_fusion
  187.2 1.9 copy.102
  189.1 1.1 fusion.52
  190.8 1.7 bitcast_dynamic-update-slice_fusion.10
  192.5 1.7 bitcast_dynamic-update-slice_fusion.8
  194.2 1.9 collective-permute-done.1
  196.9 1.0 slice.201
  198.0 1.7 bitcast_dynamic-update-slice_fusion.6
  199.7 1.7 fusion.20
  202.4 11.7 %reduce-scatter.11.cloned.1.call-done = f32[9,128,128]{2,1,0:T(8,128)} async-done(((f32[36,128,128]{2,1,0:T(8,128)}), f32[9,128,128]{2,1,0:T(8,128)}) %reduce-scatter.11.cloned.1.call-update) | async-done | bytes 589840 | tf_op jit(solution)/shard_map/reduce_scatter | solution.py:163
  214.1 1.2 fusion.51
  218.1 1.7 bitcast_dynamic-update-slice_fusion.4
  219.8 1.4 bitcast_dynamic-update-slice_fusion.2
  221.2 1.7 bitcast_dynamic-update-slice_fusion
  228.9 1.7 dynamic-slice_multiply_fusion
  230.7 1.8 copy.101
  232.6 4.2 %fusion.2 = f32[1,32,128,128]{3,2,1,0:T(8,128)} fusion(f32[8,4,128,128]{3,2,1,0:T(8,128)} %copy.102, f32[32,128,128]{2,1,0:T(8,128)} %copy.101, f32[32]{0:T(128)S(1)} %copy-done.12, f32[32,128]{1,0:T(8,128)S(1)} %broadcast_select_fusion, f32[128,128]{1,0:T(8,128)S(1)} %copy-done.8, f32[8,128,128]{2,1,0:T(8,128)S(1)} %convolution_select_fusion, ...), kind=kLoop, calls=%fused_computation.18 | loop fusion | flops 3670016 | bytes 7160032 | tf_op jit(solution)/shard_map/broadcast_in_dim | solution.py:220
  (173 shorter events, 31.5 us)
Async XLA Ops:
  6.5 1.6 copy-start.20
  7.8 1.2 copy-start.21
  10.2 21.3 %all-to-all-start = ((f32[8,2,136,128]{3,2,1,0:T(8,128)}), f32[8,2,136,128]{3,2,1,0:T(8,128)S(1)}, u32[]{:S(2)}, u32[]{:S(2)}) async-start(f32[8,2,136,128]{3,2,1,0:T(8,128)} %copy.72), calls=%async_computation | async-start | bytes 2228224 | tf_op jit(solution)/shard_map/all_to_all | solution.py:124
  15.4 86.3 %reduce-scatter.5.cloned.1.call-start = ((), (), s32[]{:S(2)}) async-start(), calls=%async_computation.10 | async-start | bytes 1638400 | tf_op jit(solution)/shard_map/reduce_scatter | solution.py:163
  35.9 2.8 %copy-start.18 = (s32[16]{0:T(128)S(1)}, s32[16]{0:T(128)}, u32[]{:S(2)}) copy-start(s32[16]{0:T(128)} %constant.429) | copy-start | bytes 196
  35.9 2.8 %copy-start.19 = (s32[16]{0:T(128)S(1)}, s32[16]{0:T(128)}, u32[]{:S(2)}) copy-start(s32[16]{0:T(128)} %constant.430) | copy-start | bytes 196
  40.9 18.9 %all-to-all-start.1 = ((f32[8,2,128,128]{3,2,1,0:T(8,128)}), f32[8,2,128,128]{3,2,1,0:T(8,128)S(1)}, u32[]{:S(2)}, u32[]{:S(2)}) async-start(f32[8,2,128,128]{3,2,1,0:T(8,128)} %fusion.55), calls=%async_computation.2 | async-start | bytes 2097152 | tf_op jit(solution)/shard_map/all_to_all | solution.py:124
  44.5 144.6 %reduce-scatter.7.cloned.1.call-start = ((), (), s32[]{:S(2)}) async-start(), calls=%async_computation.11 | async-start | bytes 2621440 | tf_op jit(solution)/shard_map/reduce_scatter | solution.py:163
  59.8 1.0 copy-start.1
  67.4 18.9 %all-to-all-start.2 = ((f32[8,2,128,128]{3,2,1,0:T(8,128)}), f32[8,2,128,128]{3,2,1,0:T(8,128)S(1)}, u32[]{:S(2)}, u32[]{:S(2)}) async-start(f32[8,2,128,128]{3,2,1,0:T(8,128)} %fusion.54), calls=%async_computation.3 | async-start | bytes 2097152 | tf_op jit(solution)/shard_map/all_to_all | solution.py:124
  70.9 126.0 %reduce-scatter.9.cloned.1.call-start = ((), (), s32[]{:S(2)}) async-start(), calls=%async_computation.12 | async-start | bytes 2621440 | tf_op jit(solution)/shard_map/reduce_scatter | solution.py:163
  86.3 1.0 copy-start.2
  91.9 0.8 copy-start.17
  91.9 0.8 copy-start.15
  91.9 0.8 copy-start.16
  95.0 24.6 %all-to-all-start.3 = ((f32[8,3,128,128]{3,2,1,0:T(8,128)}), f32[8,3,128,128]{3,2,1,0:T(8,128)S(1)}, u32[]{:S(2)}, u32[]{:S(2)}) async-start(f32[8,3,128,128]{3,2,1,0:T(8,128)} %fusion.53), calls=%async_computation.4 | async-start | bytes 3145728 | tf_op jit(solution)/shard_map/all_to_all | solution.py:124
  120.3 20.7 %all-to-all-start.4 = ((f32[4,128,128]{2,1,0:T(8,128)}), f32[4,128,128]{2,1,0:T(8,128)S(1)}, u32[]{:S(2)}, u32[]{:S(2)}) async-start(f32[4,128,128]{2,1,0:T(8,128)} %broadcast_in_dim.239), calls=%async_computation.5 | async-start | bytes 524288 | tf_op jit(solution)/shard_map/all_to_all | solution.py:188
  125.2 88.9 %reduce-scatter.11.cloned.1.call-start = ((), (), s32[]{:S(2)}) async-start(), calls=%async_computation.13 | async-start | bytes 2949120 | tf_op jit(solution)/shard_map/reduce_scatter | solution.py:163
  129.4 16.7 %copy-start.5 = (f32[4096]{0:T(1024)S(1)}, f32[4096]{0:T(1024)}, u32[]{:S(2)}) copy-start(f32[4096]{0:T(1024)} %param.21) | copy-start | bytes 49156
  129.5 19.7 %copy-start.4 = (f32[5,128,128]{1,2,0:T(8,128)S(1)}, f32[5,128,128]{1,2,0:T(8,128)}, u32[]{:S(2)}) copy-start(f32[5,128,128]{1,2,0:T(8,128)} %reduce-scatter.5.cloned.1.call-done) | copy-start | bytes 983044
  142.1 18.9 %all-to-all-start.5 = ((f32[8,2,128,128]{3,2,1,0:T(8,128)}), f32[8,2,128,128]{3,2,1,0:T(8,128)S(1)}, u32[]{:S(2)}, u32[]{:S(2)}) async-start(f32[8,2,128,128]{3,2,1,0:T(8,128)} %broadcast_in_dim.240), calls=%async_computation.6 | async-start | bytes 2097152 | tf_op jit(solution)/shard_map/all_to_all | solution.py:190
  190.2 5.9 %collective-permute-start.1 = (f32[128,128]{1,0:T(8,128)S(1)}, f32[128,128]{1,0:T(8,128)S(1)}, u32[]{:S(2)}, u32[]{:S(2)}) collective-permute-start(f32[128,128]{1,0:T(8,128)S(1)} %select_bitcast_fusion.1), channel_id=1, source_target_pairs={{0,2},{1,3},{2,4},{3,5},{4,6},{5,7},{6,0},{7,1},{8,10},{9,11},{10,... | collective-permute-start | bytes 196616 | tf_op jit(solution)/shard_map/ppermute | solution.py:176
  190.8 5.4 %collective-permute-start.2 = (f32[128,128]{1,0:T(8,128)S(1)}, f32[128,128]{1,0:T(8,128)S(1)}, u32[]{:S(2)}, u32[]{:S(2)}) collective-permute-start(f32[128,128]{1,0:T(8,128)S(1)} %select_bitcast_fusion), channel_id=1, source_target_pairs={{0,1},{1,2},{2,3},{3,4},{4,5},{5,6},{6,7},{7,0},{8,9},{9,10},{10,1... | collective-permute-start | bytes 196616 | tf_op jit(solution)/shard_map/ppermute | solution.py:176
  197.9 3.7 %collective-permute-start = (f32[128,128]{1,0:T(8,128)S(1)}, f32[128,128]{1,0:T(8,128)S(1)}, u32[]{:S(2)}, u32[]{:S(2)}) collective-permute-start(f32[128,128]{1,0:T(8,128)S(1)} %select_bitcast_fusion.2), channel_id=1, source_target_pairs={{0,3},{1,4},{2,5},{3,6},{4,7},{5,0},{6,1},{7,2},{8,11},{9,12},{10,... | collective-permute-start | bytes 196616 | tf_op jit(solution)/shard_map/ppermute | solution.py:176
  216.1 7.5 %copy-start = (f32[8,128,128]{1,2,0:T(8,128)S(1)}, f32[8,128,128]{1,2,0:T(8,128)}, u32[]{:S(2)}) copy-start(f32[8,128,128]{1,2,0:T(8,128)} %reduce-scatter.7.cloned.1.call-done) | copy-start | bytes 1572868
  217.1 8.0 %copy-start.3 = (f32[8,128,128]{1,2,0:T(8,128)S(1)}, f32[8,128,128]{1,2,0:T(8,128)}, u32[]{:S(2)}) copy-start(f32[8,128,128]{1,2,0:T(8,128)} %reduce-scatter.9.cloned.1.call-done) | copy-start | bytes 1572868
  218.0 8.5 %copy-start.7 = (f32[128,128]{0,1:T(8,128)S(1)}, f32[128,128]{0,1:T(8,128)}, u32[]{:S(2)}) copy-start(f32[128,128]{0,1:T(8,128)} %copy.91) | copy-start | bytes 196612
  218.1 8.5 %copy-start.9 = (pred[4]{0:T(512)(128)(4,1)S(1)}, pred[4]{0:T(512)(128)(4,1)}, u32[]{:S(2)}) copy-start(pred[4]{0:T(512)(128)(4,1)} %get-tuple-element.96) | copy-start | bytes 16
  218.1 8.5 %copy-start.10 = (pred[4]{0:T(512)(128)(4,1)S(1)}, pred[4]{0:T(512)(128)(4,1)}, u32[]{:S(2)}) copy-start(pred[4]{0:T(512)(128)(4,1)} %get-tuple-element.97) | copy-start | bytes 16
  221.2 6.9 %copy-start.6 = (f32[128,128]{0,1:T(8,128)S(1)}, f32[128,128]{0,1:T(8,128)}, u32[]{:S(2)}) copy-start(f32[128,128]{0,1:T(8,128)} %copy.99) | copy-start | bytes 196612
  230.7 1.9 copy-start.8
  230.7 1.9 copy-start.11
  230.7 1.9 copy-start.12
  230.7 1.8 copy-start.13
  230.7 1.8 copy-start.14
Sparse Core Ops, SparseCore 0:
  38.9 30.6 reduce-scatter.4
  71.8 42.6 reduce-scatter.6
  116.9 47.3 reduce-scatter.8
  166.5 47.5 reduce-scatter.10

commit v7 on v6

--- a/solution.py
+++ b/solution.py
@@ -102,7 +102,7 @@
 
     blocks = design.reshape(row_count, ACT, BLK)
     id_rows = jnp.zeros((8, BLK), jnp.float32).at[0, :ACT].set(active_blocks[0].astype(jnp.float32))
-    id_rows = jnp.broadcast_to(id_rows[None, None], (n_mem, 2, 8, BLK))
+    id_rows = jnp.broadcast_to(id_rows[None, None], (n_mem, 1, 8, BLK))
     grp_ids = jnp.arange(n_grp, dtype=jnp.int32)
     q_ids = jnp.arange(per_row, dtype=jnp.int32)
 
@@ -115,11 +115,12 @@
         rows_at = [[(b + lo + dl) % ACT for dl in range(per_chunk)] for b in range(n_mem)]
         left = blocks[:, jnp.array(rows_at, dtype=jnp.int32)]
         piece = jnp.einsum("nbdk,nbl->bdkl", left, blocks, preferred_element_type=jnp.float32)
+        if k == 1:
+            row0 = jnp.einsum("nk,nbl->bkl", blocks[:, 0], blocks, preferred_element_type=jnp.float32)
+            piece = jnp.concatenate([piece, row0[:, None]], axis=1)
         if prev is not None:
             piece, prev = lax.optimization_barrier((piece, prev))
         else:
-            row0 = jnp.einsum("nk,nbl->bkl", blocks[:, 0], blocks, preferred_element_type=jnp.float32)
-            piece = jnp.concatenate([piece, row0[:, None]], axis=1)
             piece = jnp.concatenate([piece, id_rows], axis=2)
         got_piece = lax.all_to_all(piece, "mem", split_axis=0, concat_axis=0, tiled=True)
         if prev is None:
@@ -128,6 +129,7 @@
             row_grp = everyone // 8
             col_grp = jnp.take(everyone, member, axis=1) // 8
             zero_on = everyone[:, 0] == 0
+        if k == 1:
             row0_got = got_piece[:, per_chunk]
             got_piece = got_piece[:, :per_chunk]
         prev = got_piece
@@ -143,7 +145,7 @@
             sel = jnp.stack([sel[g][:, [q for q in range(per_row) if q != g]] for g in range(n_grp)])
         kept = sel.shape[2]
         sel = sel.reshape(n_grp, per_chunk * kept, n_mem * per_chunk)
-        if k == 0:
+        if k == 1:
             col_sel = (
                 (col_grp[None, :] == grp_ids[:, None]) & zero_on[None, :]
             ).astype(jnp.float32)
@@ -157,13 +159,13 @@
             precision=HI,
             preferred_element_type=jnp.float32,
         ).reshape(n_grp, per_chunk * kept, BLK * BLK)
-        if k == 0:
+        if k == 1:
             send = jnp.concatenate([send, col_part], axis=1)
         width = send.shape[1]
         got = lax.psum_scatter(
             send.reshape(n_grp * width, BLK, BLK), "grp", scatter_dimension=0, tiled=True
         )
-        if k == 0:
+        if k == 1:
             col_tile = jnp.transpose(got[per_chunk * kept]) / divisor
             got = got[: per_chunk * kept]
         got = got.reshape(per_chunk, kept, BLK, BLK)
@@ -177,11 +179,13 @@
             src_tile, "mem", perm=[(j, (j + shift) % n_mem) for j in range(n_mem)]
         )
         others = by_d[d]
-        q_pos = jnp.clip(q_ids - (q_ids > group).astype(jnp.int32), 0, per_row - 2)
-        spread = jnp.take(others, q_pos, axis=0)
-        by_d[d] = jnp.where((q_ids == group)[:, None, None], moved[None], spread)
-    owned_d = jnp.stack([by_d[d] for d in range(ACT)])
-    owned = jnp.roll(owned_d, member, axis=0).reshape(ACT * per_row, BLK, BLK)
+        slots = []
+        for q in range(per_row):
+            below = others[min(q, per_row - 2)]
+            above = others[max(q - 1, 0)]
+            slots.append(jnp.where(q == group, moved, jnp.where(q < group, below, above)))
+        by_d[d] = jnp.stack(slots)
+    owned = jnp.stack([by_d[d] for d in range(ACT)]).reshape(ACT * per_row, BLK, BLK)
 
     col_tile, prev = lax.optimization_barrier((col_tile, prev))
     spread = jnp.broadcast_to(col_tile[None], (n_grp, BLK, BLK))
@@ -193,8 +197,9 @@
     chol = jnp.linalg.cholesky(a00)
     chol_inv = lax.linalg.triangular_solve(chol, eye, left_side=True, lower=True)
 
+    a_of_d = (member + jnp.arange(ACT, dtype=jnp.int32)) % ACT
     t = jnp.arange(ACT * per_row, dtype=jnp.int32)
-    tile_rows = group * 8 + t // per_row
+    tile_rows = group * 8 + jnp.take(a_of_d, t // per_row)
     tile_cols = (t % per_row) * 8 + member
     same = (tile_rows == tile_cols).astype(jnp.float32)
     diag = eye[None] * jnp.take(ridge_blocks, tile_rows, axis=0)[:, None, :] * same[:, None, None]
@@ -202,7 +207,8 @@
 
     p_rows = jnp.einsum("ipr,qr->ipq", col_rows, chol_inv, precision=HI)
     p_cols = jnp.einsum("ipr,qr->ipq", col_cols, chol_inv, precision=HI)
-    row_ids = group * 8 + jnp.arange(8, dtype=jnp.int32)
+    p_rows = jnp.take(p_rows, a_of_d, axis=0)
+    row_ids = group * 8 + a_of_d
     col_ids = jnp.arange(per_row, dtype=jnp.int32) * 8 + member
     p_rows = jnp.where((row_ids == 0)[:, None, None], chol[None], p_rows)
     p_cols = jnp.where((col_ids == 0)[:, None, None], chol[None], p_cols)
@@ -217,7 +223,8 @@
     tiles = jnp.where(trailing, tiles - update, tiles)
     tiles = jnp.where(on_column, left_tiles, tiles)
     tiles = jnp.where(on_row, jnp.transpose(right_tiles, (0, 2, 1)), tiles)
-    return tiles[None]
+    tiles = jnp.roll(tiles.reshape(ACT, per_row, BLK, BLK), member, axis=0)
+    return tiles.reshape(1, ACT * per_row, BLK, BLK)
 
 
 def solution(mesh):

time: 244 us -> 229 us (0.939)
  waiting for transfers between devices: 97.6 us -> 83.1 us
  local copies, waits for them, and re-layouts: 47.1 us -> 41.1 us
  other arithmetic: 42.3 us -> 47.8 us
    all_to_all x1, waiting for transfers between devices: 11.2 us -> 0.01 us  [on_device_fast(): pairs = lax.all_to_all(pair, 'mem', split_axis=0, concat_axis=0, tiled=True)]
    all_to_all x4, waiting for transfers between devices: 61.5 us -> 53.8 us  [on_device_fast(): lax.all_to_all(piece, 'mem', split_axis=0, concat_axis=0, tiled=True)]
    unnamed x55 -> x40, local copies, waits for them, and re-layouts: 14.3 us -> 7.16 us
    reduce_scatter x4, waiting for transfers between devices: 11.7 us -> 18.6 us  [on_device_fast(): lax.psum_scatter(send.reshape(n_grp * width, BLK, BLK), 'grp', scatter_di...]
    unnamed x5 -> x2, other arithmetic: 6.43 us -> 1.44 us
    broadcast_in_dim x1 -> x0, other arithmetic: 4.23 us -> none  [on_device_fast(): return tiles[None]]
    slice x3 -> x6, local copies, waits for them, and re-layouts: 3.19 us -> 7.19 us  [on_device_fast(): by_d[lo + dl] = got[dl]]
    another operation x0 -> x4, other arithmetic: none -> 3.58 us  [the longest x3 2.87 us: on_device_fast(): by_d[d] = jnp.stack(slots)]
  transfers between devices with their start and end apart: 13 -> 13, of which waited for: 9 -> 7; matrix products, arithmetic and copies ran while one was open for 29% -> 41% of each run, Pallas kernels for 0% -> 0%
where the time goes in v7:
time: 229 us; the launch traced here: 228 us
  waiting for transfers between devices  83.1 us (36%)
  other arithmetic  47.8 us (21%)
  local copies, waits for them, and re-layouts  41.1 us (18%)
  starting transfers between devices  26 us (11%)
  matrix products  16.3 us (7%)
  between operations  13.8 us (6%)
    all_to_all x4, waiting for transfers between devices, on_device_fast(): lax.all_to_all(piece, 'mem', split_axis=0, concat_axis=0, tiled=True)  53.8 us
    reduce_scatter x4, waiting for transfers between devices, on_device_fast(): lax.psum_scatter(send.reshape(n_grp * width, BLK, BLK), 'grp', scatter_di...  18.6 us
    all_to_all x4, starting transfers between devices, on_device_fast(): lax.all_to_all(piece, 'mem', split_axis=0, concat_axis=0, tiled=True)  16 us
    another operation x3, other arithmetic, on_device_fast(): chol = jnp.linalg.cholesky(a00)  12.4 us
    all_to_all x1, waiting for transfers between devices, on_device_fast(): lax.all_to_all(spread, 'grp', split_axis=0, concat_axis=0, tiled=True)  10.6 us
    another operation x2, other arithmetic, on_device_fast(): lax.linalg.triangular_solve(chol, eye, left_side=True, lower=True)  10.5 us
    slice x6, local copies, waits for them, and re-layouts, on_device_fast(): by_d[lo + dl] = got[dl]  7.19 us
    unnamed x40, local copies, waits for them, and re-layouts  7.16 us
  transfers between devices with their start and end apart: 13, of which 7 were waited for; matrix products, arithmetic and copies ran while one was open for 41% of the time, Pallas kernels for 0%

profile of v7, /device:TPU:0, one launch (start us, length us, event | category | flops | bytes accessed | tf_op | source)
XLA Modules:
  0.0 228.2 jit_solution(18195230085161854395)
XLA Ops:
  6.5 1.3 copy.69
  10.3 5.2 %all-to-all-start = ((f32[8,1,136,128]{3,2,1,0:T(8,128)}), f32[8,1,136,128]{3,2,1,0:T(8,128)S(1)}, u32[]{:S(2)}, u32[]{:S(2)}) async-start(f32[8,1,136,128]{3,2,1,0:T(8,128)} %maximum_bitcast_fusion), calls=%async_computation | async-start | bytes 1114112 | tf_op jit(solution)/shard_map/all_to_all | solution.py:125
  16.8 1.3 pad_maximum_fusion.1
  18.1 7.4 %all-to-all-done = f32[8,1,136,128]{3,2,1,0:T(8,128)S(1)} async-done(((f32[8,1,136,128]{3,2,1,0:T(8,128)}), f32[8,1,136,128]{3,2,1,0:T(8,128)S(1)}, u32[]{:S(2)}, u32[]{:S(2)}) %all-to-all-start) | async-done | bytes 557088 | tf_op jit(solution)/shard_map/all_to_all | solution.py:125
  25.5 3.6 %all-to-all-start.1 = ((f32[8,3,128,128]{3,2,1,0:T(8,128)}), f32[8,3,128,128]{3,2,1,0:T(8,128)S(1)}, u32[]{:S(2)}, u32[]{:S(2)}) async-start(f32[8,3,128,128]{3,2,1,0:T(8,128)} %pad_maximum_fusion.1), calls=%async_computation.1 | async-start | bytes 3145728 | tf_op jit(solution)/shard_map/all_to_all | solution.py:125
  32.8 1.3 copy.90
  34.4 15.7 %all-to-all-done.1 = f32[8,3,128,128]{3,2,1,0:T(8,128)S(1)} async-done(((f32[8,3,128,128]{3,2,1,0:T(8,128)}), f32[8,3,128,128]{3,2,1,0:T(8,128)S(1)}, u32[]{:S(2)}, u32[]{:S(2)}) %all-to-all-start.1) | async-done | bytes 1572896 | tf_op jit(solution)/shard_map/all_to_all | solution.py:125
  50.1 1.0 slice.245
  51.1 1.4 reshape.929
  54.4 2.3 %pad_maximum_fusion = f32[4,9,16384]{2,1,0:T(8,128)} fusion(f32[4,1,16384]{2,1,0:T(1,128)S(1)} %reshape.661, f32[4,8,16384]{2,1,0:T(8,128)S(1)} %fusion.53), kind=kLoop, calls=%fused_computation.14 | loop fusion | flops 589824 | bytes 4718592 | tf_op jit(solution)/shard_map/concatenate | solution.py:163
  56.7 2.4 %reshape.662 = f32[36,128,128]{2,1,0:T(8,128)S(1)} reshape(f32[4,9,16384]{2,1,0:T(8,128)} %pad_maximum_fusion) | data formatting | bytes 4718592 | tf_op jit(solution)/shard_map/reshape | solution.py:166
  59.1 2.0 copy.84
  62.4 1.4 fusion.55
  63.8 3.6 %all-to-all-start.2 = ((f32[8,2,128,128]{3,2,1,0:T(8,128)}), f32[8,2,128,128]{3,2,1,0:T(8,128)S(1)}, u32[]{:S(2)}, u32[]{:S(2)}) async-start(f32[8,2,128,128]{3,2,1,0:T(8,128)} %fusion.55), calls=%async_computation.3 | async-start | bytes 2097152 | tf_op jit(solution)/shard_map/all_to_all | solution.py:125
  67.6 15.2 %all-to-all-done.2 = f32[8,2,128,128]{3,2,1,0:T(8,128)S(1)} async-done(((f32[8,2,128,128]{3,2,1,0:T(8,128)}), f32[8,2,128,128]{3,2,1,0:T(8,128)S(1)}, u32[]{:S(2)}, u32[]{:S(2)}) %all-to-all-start.2) | async-done | bytes 1048608 | tf_op jit(solution)/shard_map/all_to_all | solution.py:125
  82.8 1.0 copy-done.1
  83.7 2.7 %fusion.6 = f32[32,128,128]{2,0,1:T(8,128)S(1)} fusion(pred[32,16,1]{0,1,2:T(8,128)(4,1)S(1)} %reshape.934, f32[2,8,128,128]{3,2,1,0:T(8,128)} %bitcast.325), kind=kOutput, calls=%fused_computation.33 | convolution fusion | flops 100663296 | bytes 3146240 | tf_op jit(solution)/shard_map/dot_general | solution.py:156
  86.4 1.9 copy.94
  92.3 1.8 fusion.54
  94.0 3.7 %all-to-all-start.3 = ((f32[8,3,128,128]{3,2,1,0:T(8,128)}), f32[8,3,128,128]{3,2,1,0:T(8,128)S(1)}, u32[]{:S(2)}, u32[]{:S(2)}) async-start(f32[8,3,128,128]{3,2,1,0:T(8,128)} %fusion.54), calls=%async_computation.4 | async-start | bytes 3145728 | tf_op jit(solution)/shard_map/all_to_all | solution.py:125
  103.3 15.4 %all-to-all-done.3 = f32[8,3,128,128]{3,2,1,0:T(8,128)S(1)} async-done(((f32[8,3,128,128]{3,2,1,0:T(8,128)}), f32[8,3,128,128]{3,2,1,0:T(8,128)S(1)}, u32[]{:S(2)}, u32[]{:S(2)}) %all-to-all-start.3) | async-done | bytes 1572896 | tf_op jit(solution)/shard_map/all_to_all | solution.py:125
  118.7 2.4 %fusion.3 = f32[36,128,128]{2,0,1:T(8,128)S(1)} fusion(pred[36,24]{1,0:T(8,128)(4,1)S(1)} %reshape_reshape.2, f32[3,8,128,128]{3,2,1,0:T(8,128)S(1)} %bitcast.322), kind=kOutput, calls=%fused_computation.24 | convolution fusion | flops 169869312 | bytes 3933024 | tf_op jit(solution)/shard_map/dot_general | solution.py:156
  121.1 1.8 copy.98
  124.1 1.0 bitcast_dynamic-update-slice_fusion.1
  126.7 4.9 %all-to-all-start.4 = ((f32[4,128,128]{2,1,0:T(8,128)}), f32[4,128,128]{2,1,0:T(8,128)S(1)}, u32[]{:S(2)}, u32[]{:S(2)}) async-start(f32[4,128,128]{2,1,0:T(8,128)} %broadcast_in_dim.212), calls=%async_computation.5 | async-start | bytes 524288 | tf_op jit(solution)/shard_map/all_to_all | solution.py:192
  131.6 1.8 fusion.50
  135.5 1.5 select_bitcast_fusion
  136.9 10.6 %all-to-all-done.4 = f32[4,128,128]{2,1,0:T(8,128)S(1)} async-done(((f32[4,128,128]{2,1,0:T(8,128)}), f32[4,128,128]{2,1,0:T(8,128)S(1)}, u32[]{:S(2)}, u32[]{:S(2)}) %all-to-all-start.4) | async-done | bytes 262176 | tf_op jit(solution)/shard_map/all_to_all | solution.py:192
  147.6 1.1 broadcast_in_dim.213
  148.7 3.6 %all-to-all-start.5 = ((f32[8,2,128,128]{3,2,1,0:T(8,128)}), f32[8,2,128,128]{3,2,1,0:T(8,128)S(1)}, u32[]{:S(2)}, u32[]{:S(2)}) async-start(f32[8,2,128,128]{3,2,1,0:T(8,128)} %broadcast_in_dim.213), calls=%async_computation.6 | async-start | bytes 2097152 | tf_op jit(solution)/shard_map/all_to_all | solution.py:194
  152.2 1.0 constant_dynamic-update-slice_fusion.2
  153.2 9.0 %reduce-scatter.9.cloned.1.call-done = f32[8,128,128]{1,2,0:T(8,128)} async-done(((f32[32,128,128]{1,2,0:T(8,128)}), f32[8,128,128]{1,2,0:T(8,128)}) %reduce-scatter.9.cloned.1.call-update) | async-done | bytes 524304 | tf_op jit(solution)/shard_map/reduce_scatter | solution.py:165
  162.2 1.8 fusion.51
  165.3 1.8 copy.100
  168.0 1.0 constant_dynamic-update-slice_fusion.1
  168.9 1.0 constant_dynamic-update-slice_fusion
  170.1 11.7 %cholesky.23 = f32[128,128]{1,0:T(8,128)S(1)} custom-call(f32[128,128]{1,0:T(8,128)S(1)} %fusion.24), custom_call_target="Cholesky" | custom-call | tf_op jit(solution)/shard_map/jit(cholesky)/cholesky | solution.py:197
  183.2 9.8 %custom-call.6 = f32[1,128,128]{1,2,0:T(8,128)S(1)} custom-call(f32[1,128,128]{2,1,0:T(8,128)S(1)} %get-tuple-element.62), custom_call_target="InvertDiagBlocksLowerTriangular" | custom-call | tf_op jit(solution)/shard_map/triangular_solve | solution.py:198
  193.3 1.4 fusion.14
  194.6 1.7 gather_fusion.5
  196.4 1.3 convolution_select_fusion
  198.5 1.8 convolution_bitcast_fusion
  200.5 1.8 copy.102
  202.3 9.6 %reduce-scatter.11.cloned.1.call-done = f32[9,128,128]{2,1,0:T(8,128)} async-done(((f32[36,128,128]{2,1,0:T(8,128)}), f32[9,128,128]{2,1,0:T(8,128)}) %reduce-scatter.11.cloned.1.call-update) | async-done | bytes 589840 | tf_op jit(solution)/shard_map/reduce_scatter | solution.py:165
  213.6 1.0 select_bitcast_fusion.10
  215.3 1.0 select_bitcast_fusion.6
  217.0 2.0 broadcast_multiply_fusion
  219.9 1.7 fusion.2
  (160 shorter events, 34.0 us)
Async XLA Ops:
  6.5 2.8 %copy-start.15 = (s32[1,8]{1,0:T(1,128)S(1)}, s32[1,8]{1,0:T(1,128)}, u32[]{:S(2)}) copy-start(s32[1,8]{1,0:T(1,128)} %param.18) | copy-start | bytes 100
  10.3 15.3 %all-to-all-start = ((f32[8,1,136,128]{3,2,1,0:T(8,128)}), f32[8,1,136,128]{3,2,1,0:T(8,128)S(1)}, u32[]{:S(2)}, u32[]{:S(2)}) async-start(f32[8,1,136,128]{3,2,1,0:T(8,128)} %maximum_bitcast_fusion), calls=%async_computation | async-start | bytes 1114112 | tf_op jit(solution)/shard_map/all_to_all | solution.py:125
  25.5 24.5 %all-to-all-start.1 = ((f32[8,3,128,128]{3,2,1,0:T(8,128)}), f32[8,3,128,128]{3,2,1,0:T(8,128)S(1)}, u32[]{:S(2)}, u32[]{:S(2)}) async-start(f32[8,3,128,128]{3,2,1,0:T(8,128)} %pad_maximum_fusion.1), calls=%async_computation.1 | async-start | bytes 3145728 | tf_op jit(solution)/shard_map/all_to_all | solution.py:125
  29.1 95.0 %reduce-scatter.7.cloned.1.call-start = ((), (), s32[]{:S(2)}) async-start(), calls=%async_computation.11 | async-start | bytes 1310720 | tf_op jit(solution)/shard_map/reduce_scatter | solution.py:165
  34.2 90.9 %reduce-scatter.5.cloned.1.call-start = ((), (), s32[]{:S(2)}) async-start(), calls=%async_computation.10 | async-start | bytes 2949120 | tf_op jit(solution)/shard_map/reduce_scatter | solution.py:165
  61.1 0.7 copy-start.13
  61.1 0.7 copy-start.14
  63.8 18.9 %all-to-all-start.2 = ((f32[8,2,128,128]{3,2,1,0:T(8,128)}), f32[8,2,128,128]{3,2,1,0:T(8,128)S(1)}, u32[]{:S(2)}, u32[]{:S(2)}) async-start(f32[8,2,128,128]{3,2,1,0:T(8,128)} %fusion.55), calls=%async_computation.3 | async-start | bytes 2097152 | tf_op jit(solution)/shard_map/all_to_all | solution.py:125
  67.4 94.8 %reduce-scatter.9.cloned.1.call-start = ((), (), s32[]{:S(2)}) async-start(), calls=%async_computation.12 | async-start | bytes 2621440 | tf_op jit(solution)/shard_map/reduce_scatter | solution.py:165
  82.8 1.0 copy-start.1
  88.3 3.9 %copy-start.12 = (s32[3]{0:T(128)S(1)}, s32[3]{0:T(128)}, u32[]{:S(2)}) copy-start(s32[3]{0:T(128)} %constant.462) | copy-start | bytes 40
  88.3 3.9 %copy-start.10 = (s32[3]{0:T(128)S(1)}, s32[3]{0:T(128)}, u32[]{:S(2)}) copy-start(s32[3]{0:T(128)} %constant.460) | copy-start | bytes 40
  88.3 3.9 %copy-start.11 = (s32[3]{0:T(128)S(1)}, s32[3]{0:T(128)}, u32[]{:S(2)}) copy-start(s32[3]{0:T(128)} %constant.461) | copy-start | bytes 40
  94.0 4.5 %copy-start.4 = (f32[4096]{0:T(1024)S(1)}, f32[4096]{0:T(1024)}, u32[]{:S(2)}) copy-start(f32[4096]{0:T(1024)} %param.19) | copy-start | bytes 49156
  94.0 24.7 %all-to-all-start.3 = ((f32[8,3,128,128]{3,2,1,0:T(8,128)}), f32[8,3,128,128]{3,2,1,0:T(8,128)S(1)}, u32[]{:S(2)}, u32[]{:S(2)}) async-start(f32[8,3,128,128]{3,2,1,0:T(8,128)} %fusion.54), calls=%async_computation.4 | async-start | bytes 3145728 | tf_op jit(solution)/shard_map/all_to_all | solution.py:125
  97.7 114.2 %reduce-scatter.11.cloned.1.call-start = ((), (), s32[]{:S(2)}) async-start(), calls=%async_computation.13 | async-start | bytes 2949120 | tf_op jit(solution)/shard_map/reduce_scatter | solution.py:165
  126.7 20.9 %all-to-all-start.4 = ((f32[4,128,128]{2,1,0:T(8,128)}), f32[4,128,128]{2,1,0:T(8,128)S(1)}, u32[]{:S(2)}, u32[]{:S(2)}) async-start(f32[4,128,128]{2,1,0:T(8,128)} %broadcast_in_dim.212), calls=%async_computation.5 | async-start | bytes 524288 | tf_op jit(solution)/shard_map/all_to_all | solution.py:192
  134.1 79.5 %collective-permute-start.1 = (f32[128,128]{1,0:T(8,128)}, f32[128,128]{1,0:T(8,128)}, u32[]{:S(2)}, u32[]{:S(2)}) collective-permute-start(f32[128,128]{1,0:T(8,128)} %select_bitcast_fusion.1), channel_id=1, source_target_pairs={{0,2},{1,3},{2,4},{3,5},{4,6},{5,7},{6,0},{7,1},{8,10},{9,11},{10,... | collective-permute-start | bytes 196616 | tf_op jit(solution)/shard_map/ppermute | solution.py:178
  136.9 78.4 %collective-permute-start.2 = (f32[128,128]{1,0:T(8,128)}, f32[128,128]{1,0:T(8,128)}, u32[]{:S(2)}, u32[]{:S(2)}) collective-permute-start(f32[128,128]{1,0:T(8,128)} %select_bitcast_fusion), channel_id=1, source_target_pairs={{0,1},{1,2},{2,3},{3,4},{4,5},{5,6},{6,7},{7,0},{8,9},{9,10},{10,1... | collective-permute-start | bytes 196616 | tf_op jit(solution)/shard_map/ppermute | solution.py:178
  147.6 1.1 copy-start.3
  148.7 21.3 %all-to-all-start.5 = ((f32[8,2,128,128]{3,2,1,0:T(8,128)}), f32[8,2,128,128]{3,2,1,0:T(8,128)S(1)}, u32[]{:S(2)}, u32[]{:S(2)}) async-start(f32[8,2,128,128]{3,2,1,0:T(8,128)} %broadcast_in_dim.213), calls=%async_computation.6 | async-start | bytes 2097152 | tf_op jit(solution)/shard_map/all_to_all | solution.py:194
  164.7 37.6 %collective-permute-start = (f32[128,128]{1,0:T(8,128)}, f32[128,128]{1,0:T(8,128)}, u32[]{:S(2)}, u32[]{:S(2)}) collective-permute-start(f32[128,128]{1,0:T(8,128)} %select_bitcast_fusion.2), channel_id=1, source_target_pairs={{0,3},{1,4},{2,5},{3,6},{4,7},{5,0},{6,1},{7,2},{8,11},{9,12},{10,... | collective-permute-start | bytes 196616 | tf_op jit(solution)/shard_map/ppermute | solution.py:178
  170.0 27.8 %copy-start.2 = (f32[8,4,128,128]{3,2,1,0:T(8,128)}, f32[8,4,128,128]{3,2,1,0:T(8,128)S(1)}, u32[]{:S(2)}) copy-start(f32[8,4,128,128]{3,2,1,0:T(8,128)S(1)} %constant_dynamic-update-slice_fusion) | copy-start | bytes 6291460
  216.9 2.2 copy-start
  216.9 2.2 copy-start.5
  216.9 2.2 copy-start.6
  216.9 2.2 copy-start.7
  217.0 2.2 copy-start.8
  217.0 2.2 copy-start.9
Sparse Core Ops, SparseCore 0:
  34.3 28.7 reduce-scatter.6
  65.5 46.7 reduce-scatter.4
  114.6 47.5 reduce-scatter.8
  164.4 47.4 reduce-scatter.10

commit v8 on v4

--- a/solution.py
+++ b/solution.py
@@ -92,8 +92,8 @@
     member = lax.axis_index("mem")
     group = lax.axis_index("grp")
     per_row = NB // ACT
-    sizes = (1, 2, 2, 3)
-    starts = (0, 1, 3, 5)
+    sizes = (1, 3, 4)
+    starts = (0, 1, 4)
     row_count = design.shape[0]
     divisor = jnp.float32(row_count * n_grp * n_mem // 16)
     eye = jnp.eye(BLK, dtype=jnp.float32)

time: 226 us -> 219 us (0.969)
  waiting for transfers between devices: 125 us -> 116 us
  local copies, waits for them, and re-layouts: 16.4 us -> 21.4 us
  starting transfers between devices: 25.2 us -> 21.2 us
  other arithmetic: 29.4 us -> 27.1 us
    reduce_scatter x4 -> x3, waiting for transfers between devices: 35.7 us -> 29.7 us  [on_device_fast(): got = lax.psum_scatter(send, 'grp', scatter_dimension=0, tiled=True)]
    all_to_all x4 -> x3, waiting for transfers between devices: 60.2 us -> 56.2 us  [on_device_fast(): lax.all_to_all(piece, 'mem', split_axis=0, concat_axis=0, tiled=True)]
    all_to_all x4 -> x3, starting transfers between devices: 15.9 us -> 12.4 us  [on_device_fast(): lax.all_to_all(piece, 'mem', split_axis=0, concat_axis=0, tiled=True)]
    broadcast_in_dim x0 -> x2, local copies, waits for them, and re-layouts: none -> 3.15 us  [the longest x1 2.54 us: on_device_fast(): return tiles[None]]
    all_to_all x1, waiting for transfers between devices: 13.9 us -> 16.3 us  [on_device_fast(): lax.all_to_all(spread, 'grp', split_axis=0, concat_axis=0, tiled=True)]
    dot_general x4 -> x3, matrix products: 9.08 us -> 11.5 us  [on_device_fast(): jnp.dot(sel.reshape(n_grp * width, n_mem * per_chunk).astype(jnp.float32)...]
    broadcast_in_dim x1, other arithmetic: 3.46 us -> 1.15 us  [on_device_fast(): return tiles[None]]
    all_to_all x3 -> x2, local copies, waits for them, and re-layouts: 1.12 us -> 3.42 us  [on_device_fast(): lax.all_to_all(piece, 'mem', split_axis=0, concat_axis=0, tiled=True)]
  transfers between devices with their start and end apart: 10 -> 8, of which waited for: 7 -> 6; matrix products, arithmetic and copies ran while one was open for 23% -> 25% of each run, Pallas kernels for 0% -> 0%
where the time goes in v8:
time: 219 us; the launch traced here: 218 us
  waiting for transfers between devices  116 us (53%)
  other arithmetic  27.1 us (12%)
  local copies, waits for them, and re-layouts  21.4 us (10%)
  starting transfers between devices  21.2 us (10%)
  matrix products  18.2 us (8%)
  between operations  13.5 us (6%)
    all_to_all x3, waiting for transfers between devices, on_device_fast(): lax.all_to_all(piece, 'mem', split_axis=0, concat_axis=0, tiled=True)  56.2 us
    reduce_scatter x3, waiting for transfers between devices, on_device_fast(): got = lax.psum_scatter(send, 'grp', scatter_dimension=0, tiled=True)  29.7 us
    all_to_all x1, waiting for transfers between devices, on_device_fast(): lax.all_to_all(spread, 'grp', split_axis=0, concat_axis=0, tiled=True)  16.3 us
    all_to_all x1, waiting for transfers between devices, on_device_fast(): pairs = lax.all_to_all(pair, 'mem', split_axis=0, concat_axis=0, tiled=True)  14.2 us
    another operation x3, other arithmetic, on_device_fast(): chol = jnp.linalg.cholesky(a00)  12.4 us
    all_to_all x3, starting transfers between devices, on_device_fast(): lax.all_to_all(piece, 'mem', split_axis=0, concat_axis=0, tiled=True)  12.4 us
    dot_general x3, matrix products, on_device_fast(): jnp.dot(sel.reshape(n_grp * width, n_mem * per_chunk).astype(jnp.float32)...  11.5 us
    another operation x2, other arithmetic, on_device_fast(): lax.linalg.triangular_solve(chol, eye, left_side=True, lower=True)  10.5 us
  transfers between devices with their start and end apart: 8, of which 6 were waited for; matrix products, arithmetic and copies ran while one was open for 25% of the time, Pallas kernels for 0%

profile of v8, /device:TPU:0, one launch (start us, length us, event | category | flops | bytes accessed | tf_op | source)
XLA Modules:
  0.0 217.8 jit_solution(14923424034435454754)
XLA Ops:
  6.5 0.7 convert_element_type.27
  7.2 1.2 copy.30
  8.4 0.3 convolution_bitcast_fusion.3
  8.8 0.8 maximum_bitcast_fusion
  9.6 5.2 %all-to-all-start = ((f32[8,1,136,128]{3,2,1,0:T(8,128)}), f32[8,1,136,128]{3,2,1,0:T(8,128)S(1)}, u32[]{:S(2)}, u32[]{:S(2)}) async-start(f32[8,1,136,128]{3,2,1,0:T(8,128)} %maximum_bitcast_fusion), calls=%async_computation | async-start | bytes 1114112 | tf_op jit(solution)/shard_map/all_to_all | solution.py:121
  14.8 10.0 %all-to-all-done = f32[8,1,136,128]{3,2,1,0:T(8,128)S(1)} async-done(((f32[8,1,136,128]{3,2,1,0:T(8,128)}), f32[8,1,136,128]{3,2,1,0:T(8,128)S(1)}, u32[]{:S(2)}, u32[]{:S(2)}) %all-to-all-start) | async-done | bytes 557088 | tf_op jit(solution)/shard_map/all_to_all | solution.py:121
  25.2 0.2 select_reduce_fusion.1
  25.8 0.9 fusion.10
  26.8 1.4 copy.34
  28.1 1.6 convolution_bitcast_fusion.2
  29.7 3.6 %all-to-all-start.1 = ((f32[8,3,128,128]{2,3,1,0:T(8,128)}), f32[8,3,128,128]{2,3,1,0:T(8,128)S(1)}, u32[]{:S(2)}, u32[]{:S(2)}) async-start(f32[8,3,128,128]{2,3,1,0:T(8,128)} %convolution_bitcast_fusion.2), calls=%async_computation.2 | async-start | bytes 3145728 | tf_op jit(solution)/shard_map/all_to_all | solution.py:121
  34.0 20.3 %all-to-all-done.1 = f32[8,3,128,128]{2,3,1,0:T(8,128)S(1)} async-done(((f32[8,3,128,128]{2,3,1,0:T(8,128)}), f32[8,3,128,128]{2,3,1,0:T(8,128)S(1)}, u32[]{:S(2)}, u32[]{:S(2)}) %all-to-all-start.1) | async-done | bytes 1572896 | tf_op jit(solution)/shard_map/all_to_all | solution.py:121
  54.3 1.6 copy.42
  55.9 3.9 %fusion.7 = f32[48,128,128]{2,0,1:T(8,128)S(1)} fusion(pred[48,24,1]{0,1,2:T(8,128)(4,1)S(1)} %reshape.514, f32[3,8,128,128]{3,2,1,0:T(8,128)} %bitcast.137), kind=kOutput, calls=%fused_computation.14 | convolution fusion | flops 226492416 | bytes 4719744 | tf_op jit(solution)/shard_map/dot_general | solution.py:146
  59.8 2.6 %copy.44 = f32[48,128,128]{2,1,0:T(8,128)} copy(f32[48,128,128]{2,0,1:T(8,128)S(1)} %fusion.7) | data formatting | bytes 6291456 | tf_op jit(solution)/shard_map/dot_general | solution.py:146
  62.5 1.8 convolution_bitcast_fusion.1
  64.3 3.6 %all-to-all-start.2 = ((f32[8,4,128,128]{2,3,1,0:T(8,128)}), f32[8,4,128,128]{2,3,1,0:T(8,128)S(1)}, u32[]{:S(2)}, u32[]{:S(2)}) async-start(f32[8,4,128,128]{2,3,1,0:T(8,128)} %convolution_bitcast_fusion.1), calls=%async_computation.3 | async-start | bytes 4194304 | tf_op jit(solution)/shard_map/all_to_all | solution.py:121
  68.2 0.2 broadcast_and_fusion
  68.6 25.9 %all-to-all-done.2 = f32[8,4,128,128]{2,3,1,0:T(8,128)S(1)} async-done(((f32[8,4,128,128]{2,3,1,0:T(8,128)}), f32[8,4,128,128]{2,3,1,0:T(8,128)S(1)}, u32[]{:S(2)}, u32[]{:S(2)}) %all-to-all-start.2) | async-done | bytes 2097184 | tf_op jit(solution)/shard_map/all_to_all | solution.py:121
  94.4 1.8 copy.45
  96.2 6.7 %fusion.3 = f32[64,128,128]{2,0,1:T(8,128)} fusion(pred[64,32,1]{0,1,2:T(32,128)(4,1)S(1)} %reshape.515, f32[4,8,128,128]{3,2,1,0:T(8,128)} %bitcast.136), kind=kOutput, calls=%fused_computation.6 | convolution fusion | flops 402653184 | bytes 6293504 | tf_op jit(solution)/shard_map/dot_general | solution.py:146
  103.0 0.8 slice.99
  103.9 0.7 broadcast_in_dim.85
  104.6 5.0 %all-to-all-start.3 = ((f32[4,128,128]{2,1,0:T(8,128)}), f32[4,128,128]{2,1,0:T(8,128)S(1)}, u32[]{:S(2)}, u32[]{:S(2)}) async-start(f32[4,128,128]{2,1,0:T(8,128)} %broadcast_in_dim.85), calls=%async_computation.4 | async-start | bytes 524288 | tf_op jit(solution)/shard_map/all_to_all | solution.py:160
  109.7 16.3 %all-to-all-done.3 = f32[4,128,128]{2,1,0:T(8,128)S(1)} async-done(((f32[4,128,128]{2,1,0:T(8,128)}), f32[4,128,128]{2,1,0:T(8,128)S(1)}, u32[]{:S(2)}, u32[]{:S(2)}) %all-to-all-start.3) | async-done | bytes 262176 | tf_op jit(solution)/shard_map/all_to_all | solution.py:160
  126.0 1.1 broadcast_in_dim.130
  127.0 3.7 %all-to-all-start.4 = ((f32[8,2,128,128]{3,2,1,0:T(8,128)}), f32[8,2,128,128]{3,2,1,0:T(8,128)S(1)}, u32[]{:S(2)}, u32[]{:S(2)}) async-start(f32[8,2,128,128]{3,2,1,0:T(8,128)} %broadcast_in_dim.130), calls=%async_computation.5 | async-start | bytes 2097152 | tf_op jit(solution)/shard_map/all_to_all | solution.py:162
  130.8 0.6 gather_fusion
  131.6 0.2 copy.59
  131.7 14.2 %all-to-all-done.4 = f32[8,2,128,128]{3,2,1,0:T(8,128)S(1)} async-done(((f32[8,2,128,128]{3,2,1,0:T(8,128)}), f32[8,2,128,128]{3,2,1,0:T(8,128)S(1)}, u32[]{:S(2)}, u32[]{:S(2)}) %all-to-all-start.4) | async-done | bytes 1048608 | tf_op jit(solution)/shard_map/all_to_all | solution.py:162
  146.1 11.7 %cholesky.23 = f32[128,128]{1,0:T(8,128)S(1)} custom-call(f32[128,128]{1,0:T(8,128)S(1)} %fusion.16), custom_call_target="Cholesky" | custom-call | tf_op jit(solution)/shard_map/jit(cholesky)/cholesky | solution.py:165
  157.8 0.6 compare_reduce_fusion
  158.5 0.7 select_bitcast_fusion
  159.1 9.8 %custom-call.6 = f32[1,128,128]{1,2,0:T(8,128)S(1)} custom-call(f32[1,128,128]{2,1,0:T(8,128)S(1)} %get-tuple-element.34), custom_call_target="InvertDiagBlocksLowerTriangular" | custom-call | tf_op jit(solution)/shard_map/triangular_solve | solution.py:166
  169.0 0.2 convolution_bitcast_fusion.4
  169.2 0.4 convolution_select_fusion.1
  169.8 0.6 convolution_select_fusion
  170.3 0.3 copy.40
  170.7 1.8 convolution_bitcast_fusion
  172.5 2.0 copy.48
  174.4 1.6 copy.47
  176.1 29.7 %reduce-scatter.8.cloned.1.call-done = f32[16,128,128]{2,0,1:T(8,128)} async-done(((f32[64,128,128]{2,0,1:T(8,128)}), f32[16,128,128]{2,0,1:T(8,128)}) %reduce-scatter.8.cloned.1.call-update) | async-done | bytes 1048592 | tf_op jit(solution)/shard_map/reduce_scatter | solution.py:152
  205.7 0.6 broadcast_in_dim.135
  206.4 0.3 tile.4
  206.6 0.7 copy-done
  207.3 0.3 copy-done.1
  207.6 1.1 fusion.2
  208.7 2.5 %copy.49 = f32[1,32,128,128]{3,2,1,0:T(8,128)} copy(f32[1,32,128,128]{3,1,2,0:T(8,128)S(1)} %fusion.2) | data formatting | bytes 4194304 | tf_op jit(solution)/shard_map/broadcast_in_dim | solution.py:192
  (59 shorter events, 2.5 us)
Async XLA Ops:
  9.6 15.3 %all-to-all-start = ((f32[8,1,136,128]{3,2,1,0:T(8,128)}), f32[8,1,136,128]{3,2,1,0:T(8,128)S(1)}, u32[]{:S(2)}, u32[]{:S(2)}) async-start(f32[8,1,136,128]{3,2,1,0:T(8,128)} %maximum_bitcast_fusion), calls=%async_computation | async-start | bytes 1114112 | tf_op jit(solution)/shard_map/all_to_all | solution.py:121
  14.8 88.2 %reduce-scatter.4.cloned.1.call-start = ((), (), s32[]{:S(2)}) async-start(), calls=%async_computation.8 | async-start | bytes 1638400 | tf_op jit(solution)/shard_map/reduce_scatter | solution.py:152
  29.7 24.5 %all-to-all-start.1 = ((f32[8,3,128,128]{2,3,1,0:T(8,128)}), f32[8,3,128,128]{2,3,1,0:T(8,128)S(1)}, u32[]{:S(2)}, u32[]{:S(2)}) async-start(f32[8,3,128,128]{2,3,1,0:T(8,128)} %convolution_bitcast_fusion.2), calls=%async_computation.2 | async-start | bytes 3145728 | tf_op jit(solution)/shard_map/all_to_all | solution.py:121
  33.3 141.1 %reduce-scatter.6.cloned.1.call-start = ((), (), s32[]{:S(2)}) async-start(), calls=%async_computation.9 | async-start | bytes 3932160 | tf_op jit(solution)/shard_map/reduce_scatter | solution.py:152
  64.3 30.2 %all-to-all-start.2 = ((f32[8,4,128,128]{2,3,1,0:T(8,128)}), f32[8,4,128,128]{2,3,1,0:T(8,128)S(1)}, u32[]{:S(2)}, u32[]{:S(2)}) async-start(f32[8,4,128,128]{2,3,1,0:T(8,128)} %convolution_bitcast_fusion.1), calls=%async_computation.3 | async-start | bytes 4194304 | tf_op jit(solution)/shard_map/all_to_all | solution.py:121
  67.9 137.9 %reduce-scatter.8.cloned.1.call-start = ((), (), s32[]{:S(2)}) async-start(), calls=%async_computation.10 | async-start | bytes 5242880 | tf_op jit(solution)/shard_map/reduce_scatter | solution.py:152
  104.6 26.2 %copy-start.2 = (f32[4096]{0:T(1024)S(1)}, f32[4096]{0:T(1024)}, u32[]{:S(2)}) copy-start(f32[4096]{0:T(1024)} %param.7) | copy-start | bytes 49156
  104.6 21.3 %all-to-all-start.3 = ((f32[4,128,128]{2,1,0:T(8,128)}), f32[4,128,128]{2,1,0:T(8,128)S(1)}, u32[]{:S(2)}, u32[]{:S(2)}) async-start(f32[4,128,128]{2,1,0:T(8,128)} %broadcast_in_dim.85), calls=%async_computation.4 | async-start | bytes 524288 | tf_op jit(solution)/shard_map/all_to_all | solution.py:160
  126.0 5.6 %slice-start = ((f32[5,128,128]{2,1,0:T(8,128)}), f32[4,128,128]{2,1,0:T(8,128)S(1)}, s32[]{:S(2)}) async-start(f32[5,128,128]{2,1,0:T(8,128)} %reduce-scatter.4.cloned.1.call-done), calls=%async_computation.11 | async-start | bytes 524288 | tf_op jit(solution)/shard_map/slice | solution.py:153
  127.0 18.9 %all-to-all-start.4 = ((f32[8,2,128,128]{3,2,1,0:T(8,128)}), f32[8,2,128,128]{3,2,1,0:T(8,128)S(1)}, u32[]{:S(2)}, u32[]{:S(2)}) async-start(f32[8,2,128,128]{3,2,1,0:T(8,128)} %broadcast_in_dim.130), calls=%async_computation.5 | async-start | bytes 2097152 | tf_op jit(solution)/shard_map/all_to_all | solution.py:162
  205.7 1.6 copy-start
  205.7 1.9 copy-start.1
Sparse Core Ops, SparseCore 0:
  28.3 30.5 reduce-scatter.3
  62.6 63.7 reduce-scatter.5
  128.7 76.9 reduce-scatter.7

commit v9 on v8

--- a/solution.py
+++ b/solution.py
@@ -92,8 +92,8 @@
     member = lax.axis_index("mem")
     group = lax.axis_index("grp")
     per_row = NB // ACT
-    sizes = (1, 3, 4)
-    starts = (0, 1, 4)
+    sizes = (2, 6)
+    starts = (0, 2)
     row_count = design.shape[0]
     divisor = jnp.float32(row_count * n_grp * n_mem // 16)
     eye = jnp.eye(BLK, dtype=jnp.float32)
@@ -117,7 +117,8 @@
         if prev is not None:
             piece, prev = lax.optimization_barrier((piece, prev))
         else:
-            piece = jnp.concatenate([piece, id_rows], axis=2)
+            ids_here = jnp.broadcast_to(id_rows, (n_mem, per_chunk, 8, BLK))
+            piece = jnp.concatenate([piece, ids_here], axis=2)
         got_piece = lax.all_to_all(piece, "mem", split_axis=0, concat_axis=0, tiled=True)
         if prev is None:
             everyone = got_piece[:, 0, BLK, :ACT].astype(jnp.int32)

time: 219 us -> 218 us (level)
  waiting for transfers between devices: 116 us -> 124 us
  matrix products: 18.2 us -> 14.5 us
  local copies, waits for them, and re-layouts: 21.4 us -> 19 us
    reduce_scatter x3 -> x2, waiting for transfers between devices: 29.7 us -> 42.8 us  [on_device_fast(): got = lax.psum_scatter(send, 'grp', scatter_dimension=0, tiled=True)]
    all_to_all x1, waiting for transfers between devices: 16.3 us -> 13.3 us  [on_device_fast(): lax.all_to_all(spread, 'grp', split_axis=0, concat_axis=0, tiled=True)]
    all_to_all x3 -> x2, waiting for transfers between devices: 56.2 us -> 53.3 us  [on_device_fast(): lax.all_to_all(piece, 'mem', split_axis=0, concat_axis=0, tiled=True)]
    all_to_all x3 -> x2, starting transfers between devices: 12.4 us -> 9.61 us  [on_device_fast(): lax.all_to_all(piece, 'mem', split_axis=0, concat_axis=0, tiled=True)]
    dot_general x3 -> x2, matrix products: 11.5 us -> 8.91 us  [on_device_fast(): jnp.dot(sel.reshape(n_grp * width, n_mem * per_chunk).astype(jnp.float32)...]
  transfers between devices with their start and end apart: 8 -> 6, of which waited for: 6 -> 5; matrix products, arithmetic and copies ran while one was open for 25% -> 21% of each run, Pallas kernels for 0% -> 0%
where the time goes in v9:
time: 218 us; the launch traced here: 217 us
  waiting for transfers between devices  124 us (57%)
  other arithmetic  26.7 us (12%)
  starting transfers between devices  19.3 us (9%)
  local copies, waits for them, and re-layouts  19 us (9%)
  matrix products  14.5 us (7%)
  between operations  13.8 us (6%)
    all_to_all x2, waiting for transfers between devices, on_device_fast(): lax.all_to_all(piece, 'mem', split_axis=0, concat_axis=0, tiled=True)  53.3 us
    reduce_scatter x2, waiting for transfers between devices, on_device_fast(): got = lax.psum_scatter(send, 'grp', scatter_dimension=0, tiled=True)  42.8 us
    all_to_all x1, waiting for transfers between devices, on_device_fast(): pairs = lax.all_to_all(pair, 'mem', split_axis=0, concat_axis=0, tiled=True)  14.3 us
    all_to_all x1, waiting for transfers between devices, on_device_fast(): lax.all_to_all(spread, 'grp', split_axis=0, concat_axis=0, tiled=True)  13.3 us
    another operation x3, other arithmetic, on_device_fast(): chol = jnp.linalg.cholesky(a00)  12.4 us
    another operation x2, other arithmetic, on_device_fast(): lax.linalg.triangular_solve(chol, eye, left_side=True, lower=True)  10.5 us
    all_to_all x2, starting transfers between devices, on_device_fast(): lax.all_to_all(piece, 'mem', split_axis=0, concat_axis=0, tiled=True)  9.61 us
    dot_general x2, matrix products, on_device_fast(): jnp.dot(sel.reshape(n_grp * width, n_mem * per_chunk).astype(jnp.float32)...  8.91 us
  transfers between devices with their start and end apart: 6, of which 5 were waited for; matrix products, arithmetic and copies ran while one was open for 21% of the time, Pallas kernels for 0%

profile of v9, /device:TPU:0, one launch (start us, length us, event | category | flops | bytes accessed | tf_op | source)
XLA Modules:
  0.0 217.1 jit_solution(17141206585540519179)
XLA Ops:
  6.5 1.2 copy.70
  7.8 0.7 convert_element_type.26
  8.4 0.3 convolution_bitcast_fusion.2
  8.8 1.1 pad_maximum_fusion
  9.9 5.2 %all-to-all-start = ((f32[8,2,136,128]{3,2,1,0:T(8,128)}), f32[8,2,136,128]{3,2,1,0:T(8,128)S(1)}, u32[]{:S(2)}, u32[]{:S(2)}) async-start(f32[8,2,136,128]{3,2,1,0:T(8,128)} %pad_maximum_fusion), calls=%async_computation | async-start | bytes 2228224 | tf_op jit(solution)/shard_map/all_to_all | solution.py:122
  15.2 15.9 %all-to-all-done = f32[8,2,136,128]{3,2,1,0:T(8,128)S(1)} async-done(((f32[8,2,136,128]{3,2,1,0:T(8,128)}), f32[8,2,136,128]{3,2,1,0:T(8,128)S(1)}, u32[]{:S(2)}, u32[]{:S(2)}) %all-to-all-start) | async-done | bytes 1114144 | tf_op jit(solution)/shard_map/all_to_all | solution.py:122
  31.2 0.1 fusion.20
  31.3 0.3 fusion.18
  31.7 0.1 and.258
  32.2 0.1 copy.73
  32.5 0.2 copy.74
  32.8 0.1 slice.90
  32.9 1.7 fusion.7
  34.6 1.9 copy.76
  36.5 2.3 %convolution_bitcast_fusion = f32[8,6,128,128]{2,3,1,0:T(8,128)} fusion(bf16[256,8,128,1]{0,2,3,1:T(8,128)(2,1)S(1)} %bitcast.115, bf16[256,8,128]{0,2,1:T(8,128)(2,1)S(1)} %bitcast.116), kind=kOutput, calls=%fused_computation.11 | convolution fusion | flops 402653184 | bytes 4063232 | tf_op jit(solution)/shard_map/nak,nbl->bakl/dot_general | solution.py:114
  38.8 4.4 %all-to-all-start.1 = ((f32[8,6,128,128]{2,3,1,0:T(8,128)}), f32[8,6,128,128]{2,3,1,0:T(8,128)}, u32[]{:S(2)}, u32[]{:S(2)}) async-start(f32[8,6,128,128]{2,3,1,0:T(8,128)} %convolution_bitcast_fusion), calls=%async_computation.2 | async-start | bytes 6291456 | tf_op jit(solution)/shard_map/all_to_all | solution.py:122
  43.4 0.1 broadcast_and_fusion
  43.5 0.2 and.276
  43.7 37.4 %all-to-all-done.1 = f32[8,6,128,128]{2,3,1,0:T(8,128)} async-done(((f32[8,6,128,128]{2,3,1,0:T(8,128)}), f32[8,6,128,128]{2,3,1,0:T(8,128)}, u32[]{:S(2)}, u32[]{:S(2)}) %all-to-all-start.1) | async-done | bytes 3145760 | tf_op jit(solution)/shard_map/all_to_all | solution.py:122
  81.1 2.4 %copy.83 = f32[8,6,128,128]{3,2,1,0:T(8,128)S(1)} copy(f32[8,6,128,128]{2,3,1,0:T(8,128)} %all-to-all-done.1) | data formatting | bytes 6291456 | tf_op jit(solution)/shard_map/all_to_all | solution.py:122
  83.5 7.2 %fusion = f32[96,128,128]{2,0,1:T(8,128)} fusion(pred[96,48]{1,0:T(32,128)(4,1)S(1)} %and.276, f32[6,8,128,128]{3,2,1,0:T(8,128)S(1)} %bitcast.109), kind=kOutput, calls=%fused_computation.2 | convolution fusion | flops 905969664 | bytes 9441792 | tf_op jit(solution)/shard_map/dot_general | solution.py:147
  90.8 0.8 slice.91
  91.8 0.7 broadcast_in_dim.120
  92.5 5.1 %all-to-all-start.2 = ((f32[4,128,128]{2,1,0:T(8,128)}), f32[4,128,128]{2,1,0:T(8,128)S(1)}, u32[]{:S(2)}, u32[]{:S(2)}) async-start(f32[4,128,128]{2,1,0:T(8,128)} %broadcast_in_dim.120), calls=%async_computation.3 | async-start | bytes 524288 | tf_op jit(solution)/shard_map/all_to_all | solution.py:161
  97.5 13.3 %all-to-all-done.2 = f32[4,128,128]{2,1,0:T(8,128)S(1)} async-done(((f32[4,128,128]{2,1,0:T(8,128)}), f32[4,128,128]{2,1,0:T(8,128)S(1)}, u32[]{:S(2)}, u32[]{:S(2)}) %all-to-all-start.2) | async-done | bytes 262176 | tf_op jit(solution)/shard_map/all_to_all | solution.py:161
  110.9 1.1 broadcast_in_dim.121
  112.0 4.5 %all-to-all-start.3 = ((f32[8,2,128,128]{3,2,1,0:T(8,128)}), f32[8,2,128,128]{3,2,1,0:T(8,128)S(1)}, u32[]{:S(2)}, u32[]{:S(2)}) async-start(f32[8,2,128,128]{3,2,1,0:T(8,128)} %broadcast_in_dim.121), calls=%async_computation.4 | async-start | bytes 2097152 | tf_op jit(solution)/shard_map/all_to_all | solution.py:163
  116.5 0.6 gather_fusion
  117.3 0.3 copy.98
  117.6 14.3 %all-to-all-done.3 = f32[8,2,128,128]{3,2,1,0:T(8,128)S(1)} async-done(((f32[8,2,128,128]{3,2,1,0:T(8,128)}), f32[8,2,128,128]{3,2,1,0:T(8,128)S(1)}, u32[]{:S(2)}, u32[]{:S(2)}) %all-to-all-start.3) | async-done | bytes 1048608 | tf_op jit(solution)/shard_map/all_to_all | solution.py:163
  132.0 11.7 %cholesky.23 = f32[128,128]{1,0:T(8,128)S(1)} custom-call(f32[128,128]{1,0:T(8,128)S(1)} %fusion.14), custom_call_target="Cholesky" | custom-call | tf_op jit(solution)/shard_map/jit(cholesky)/cholesky | solution.py:166
  143.8 0.6 compare_reduce_fusion
  144.4 0.7 select_bitcast_fusion
  145.1 9.8 %custom-call.6 = f32[1,128,128]{1,2,0:T(8,128)S(1)} custom-call(f32[1,128,128]{2,1,0:T(8,128)S(1)} %get-tuple-element.32), custom_call_target="InvertDiagBlocksLowerTriangular" | custom-call | tf_op jit(solution)/shard_map/triangular_solve | solution.py:167
  154.9 0.2 convolution_bitcast_fusion.3
  155.2 0.6 convolution_select_fusion
  155.7 1.1 copy.81
  156.9 0.4 convolution_select_fusion.1
  157.3 0.8 copy.80
  158.1 1.8 convolution_bitcast_fusion.1
  159.9 2.0 copy.86
  161.9 42.7 %reduce-scatter.5.cloned.1.call-done = f32[24,128,128]{2,0,1:T(8,128)} async-done(((f32[96,128,128]{2,0,1:T(8,128)}), f32[24,128,128]{2,0,1:T(8,128)}) %reduce-scatter.5.cloned.1.call-update) | async-done | bytes 1572880 | tf_op jit(solution)/shard_map/reduce_scatter | solution.py:153
  204.6 0.6 broadcast_in_dim.126
  205.2 0.3 tile.4
  205.5 0.7 copy-done
  206.2 0.4 copy-done.2
  206.7 1.0 fusion.5
  207.7 2.5 %copy.87 = f32[1,32,128,128]{3,2,1,0:T(8,128)} copy(f32[1,32,128,128]{3,1,2,0:T(8,128)S(1)} %fusion.5) | data formatting | bytes 4194304 | tf_op jit(solution)/shard_map/broadcast_in_dim | solution.py:193
  (58 shorter events, 1.5 us)
Async XLA Ops:
  9.9 21.3 %all-to-all-start = ((f32[8,2,136,128]{3,2,1,0:T(8,128)}), f32[8,2,136,128]{3,2,1,0:T(8,128)S(1)}, u32[]{:S(2)}, u32[]{:S(2)}) async-start(f32[8,2,136,128]{3,2,1,0:T(8,128)} %pad_maximum_fusion), calls=%async_computation | async-start | bytes 2228224 | tf_op jit(solution)/shard_map/all_to_all | solution.py:122
  15.0 75.7 %reduce-scatter.3.cloned.1.call-start = ((), (), s32[]{:S(2)}) async-start(), calls=%async_computation.6 | async-start | bytes 2949120 | tf_op jit(solution)/shard_map/reduce_scatter | solution.py:153
  38.8 42.3 %all-to-all-start.1 = ((f32[8,6,128,128]{2,3,1,0:T(8,128)}), f32[8,6,128,128]{2,3,1,0:T(8,128)}, u32[]{:S(2)}, u32[]{:S(2)}) async-start(f32[8,6,128,128]{2,3,1,0:T(8,128)} %convolution_bitcast_fusion), calls=%async_computation.2 | async-start | bytes 6291456 | tf_op jit(solution)/shard_map/all_to_all | solution.py:122
  43.2 161.4 %reduce-scatter.5.cloned.1.call-start = ((), (), s32[]{:S(2)}) async-start(), calls=%async_computation.7 | async-start | bytes 7864320 | tf_op jit(solution)/shard_map/reduce_scatter | solution.py:153
  92.5 24.0 %copy-start.4 = (f32[4096]{0:T(1024)S(1)}, f32[4096]{0:T(1024)}, u32[]{:S(2)}) copy-start(f32[4096]{0:T(1024)} %param.7) | copy-start | bytes 49156
  92.5 18.4 %all-to-all-start.2 = ((f32[4,128,128]{2,1,0:T(8,128)}), f32[4,128,128]{2,1,0:T(8,128)S(1)}, u32[]{:S(2)}, u32[]{:S(2)}) async-start(f32[4,128,128]{2,1,0:T(8,128)} %broadcast_in_dim.120), calls=%async_computation.3 | async-start | bytes 524288 | tf_op jit(solution)/shard_map/all_to_all | solution.py:161
  110.9 6.4 %slice-start = ((f32[9,128,128]{2,1,0:T(8,128)}), f32[8,128,128]{2,1,0:T(8,128)S(1)}, s32[]{:S(2)}) async-start(f32[9,128,128]{2,1,0:T(8,128)} %reduce-scatter.3.cloned.1.call-done), calls=%async_computation.8 | async-start | bytes 1048576 | tf_op jit(solution)/shard_map/slice | solution.py:154
  112.0 19.9 %all-to-all-start.3 = ((f32[8,2,128,128]{3,2,1,0:T(8,128)}), f32[8,2,128,128]{3,2,1,0:T(8,128)S(1)}, u32[]{:S(2)}, u32[]{:S(2)}) async-start(f32[8,2,128,128]{3,2,1,0:T(8,128)} %broadcast_in_dim.121), calls=%async_computation.4 | async-start | bytes 2097152 | tf_op jit(solution)/shard_map/all_to_all | solution.py:163
  159.9 44.7 %copy-start.1 = (f32[8,128,128]{2,0,1:T(8,128)S(1)}, f32[8,128,128]{2,0,1:T(8,128)}, u32[]{:S(2)}) copy-start(f32[8,128,128]{2,0,1:T(8,128)} %copy.81) | copy-start | bytes 1572868
  161.9 43.4 %copy-start.3 = (f32[4,128,128]{1,0,2:T(4,128)S(1)}, f32[4,128,128]{1,0,2:T(4,128)}, u32[]{:S(2)}) copy-start(f32[4,128,128]{1,0,2:T(4,128)} %copy.80) | copy-start | bytes 786436
  204.6 1.6 copy-start
  204.6 2.0 copy-start.2
Sparse Core Ops, SparseCore 0:
  36.6 47.4 reduce-scatter.2
  90.9 113.6 reduce-scatter.4

commit v10 on v9

--- a/solution.py
+++ b/solution.py
@@ -147,7 +147,7 @@
         send = jnp.dot(
             sel.reshape(n_grp * width, n_mem * per_chunk).astype(jnp.float32),
             got_piece.reshape(n_mem * per_chunk, BLK * BLK),
-            precision=HI,
+            precision=lax.Precision.HIGH,
             preferred_element_type=jnp.float32,
         ).reshape(n_grp * width, BLK, BLK)
         got = lax.psum_scatter(send, "grp", scatter_dimension=0, tiled=True)

time: 218 us -> 217 us (level)
  no operation moved by 1% of the time
where the time goes in v10:
time: 217 us; the launch traced here: 215 us
  waiting for transfers between devices  124 us (57%)
  other arithmetic  26.7 us (12%)
  starting transfers between devices  19.2 us (9%)
  local copies, waits for them, and re-layouts  19 us (9%)
  between operations  13.8 us (6%)
  matrix products  12.9 us (6%)
    all_to_all x2, waiting for transfers between devices, on_device_fast(): lax.all_to_all(piece, 'mem', split_axis=0, concat_axis=0, tiled=True)  53.3 us
    reduce_scatter x2, waiting for transfers between devices, on_device_fast(): got = lax.psum_scatter(send, 'grp', scatter_dimension=0, tiled=True)  42.8 us
    all_to_all x1, waiting for transfers between devices, on_device_fast(): pairs = lax.all_to_all(pair, 'mem', split_axis=0, concat_axis=0, tiled=True)  14.3 us
    all_to_all x1, waiting for transfers between devices, on_device_fast(): lax.all_to_all(spread, 'grp', split_axis=0, concat_axis=0, tiled=True)  13.3 us
    another operation x3, other arithmetic, on_device_fast(): chol = jnp.linalg.cholesky(a00)  12.4 us
    another operation x2, other arithmetic, on_device_fast(): lax.linalg.triangular_solve(chol, eye, left_side=True, lower=True)  10.5 us
    all_to_all x2, starting transfers between devices, on_device_fast(): lax.all_to_all(piece, 'mem', split_axis=0, concat_axis=0, tiled=True)  9.61 us
    dot_general x2, matrix products, on_device_fast(): jnp.dot(sel.reshape(n_grp * width, n_mem * per_chunk).astype(jnp.float32)...  7.24 us
  transfers between devices with their start and end apart: 6, of which 5 were waited for; matrix products, arithmetic and copies ran while one was open for 21% of the time, Pallas kernels for 0%

profile of v10, /device:TPU:0, one launch (start us, length us, event | category | flops | bytes accessed | tf_op | source)
XLA Modules:
  0.0 215.4 jit_solution(14537441622132120993)
XLA Ops:
  6.5 1.2 copy.70
  7.8 0.7 convert_element_type.26
  8.4 0.3 convolution_bitcast_fusion.2
  8.8 1.1 pad_maximum_fusion
  9.9 5.2 %all-to-all-start = ((f32[8,2,136,128]{3,2,1,0:T(8,128)}), f32[8,2,136,128]{3,2,1,0:T(8,128)S(1)}, u32[]{:S(2)}, u32[]{:S(2)}) async-start(f32[8,2,136,128]{3,2,1,0:T(8,128)} %pad_maximum_fusion), calls=%async_computation | async-start | bytes 2228224 | tf_op jit(solution)/shard_map/all_to_all | solution.py:122
  15.2 15.9 %all-to-all-done = f32[8,2,136,128]{3,2,1,0:T(8,128)S(1)} async-done(((f32[8,2,136,128]{3,2,1,0:T(8,128)}), f32[8,2,136,128]{3,2,1,0:T(8,128)S(1)}, u32[]{:S(2)}, u32[]{:S(2)}) %all-to-all-start) | async-done | bytes 1114144 | tf_op jit(solution)/shard_map/all_to_all | solution.py:122
  31.2 0.1 fusion.20
  31.3 0.3 fusion.18
  31.7 0.1 and.258
  32.2 0.1 copy.73
  32.5 0.2 copy.74
  32.8 0.1 slice.90
  32.9 1.2 fusion.7
  34.1 1.9 copy.76
  36.0 2.3 %convolution_bitcast_fusion = f32[8,6,128,128]{2,3,1,0:T(8,128)} fusion(bf16[256,8,128,1]{0,2,3,1:T(8,128)(2,1)S(1)} %bitcast.115, bf16[256,8,128]{0,2,1:T(8,128)(2,1)S(1)} %bitcast.116), kind=kOutput, calls=%fused_computation.11 | convolution fusion | flops 402653184 | bytes 4063232 | tf_op jit(solution)/shard_map/nak,nbl->bakl/dot_general | solution.py:114
  38.3 4.4 %all-to-all-start.1 = ((f32[8,6,128,128]{2,3,1,0:T(8,128)}), f32[8,6,128,128]{2,3,1,0:T(8,128)}, u32[]{:S(2)}, u32[]{:S(2)}) async-start(f32[8,6,128,128]{2,3,1,0:T(8,128)} %convolution_bitcast_fusion), calls=%async_computation.2 | async-start | bytes 6291456 | tf_op jit(solution)/shard_map/all_to_all | solution.py:122
  42.9 0.1 broadcast_and_fusion
  43.0 0.2 and.276
  43.2 37.4 %all-to-all-done.1 = f32[8,6,128,128]{2,3,1,0:T(8,128)} async-done(((f32[8,6,128,128]{2,3,1,0:T(8,128)}), f32[8,6,128,128]{2,3,1,0:T(8,128)}, u32[]{:S(2)}, u32[]{:S(2)}) %all-to-all-start.1) | async-done | bytes 3145760 | tf_op jit(solution)/shard_map/all_to_all | solution.py:122
  80.6 2.4 %copy.83 = f32[8,6,128,128]{3,2,1,0:T(8,128)S(1)} copy(f32[8,6,128,128]{2,3,1,0:T(8,128)} %all-to-all-done.1) | data formatting | bytes 6291456 | tf_op jit(solution)/shard_map/all_to_all | solution.py:122
  83.0 6.1 %fusion = f32[96,128,128]{2,0,1:T(8,128)} fusion(pred[96,48]{1,0:T(32,128)(4,1)S(1)} %and.276, f32[6,8,128,128]{3,2,1,0:T(8,128)S(1)} %bitcast.109), kind=kOutput, calls=%fused_computation.2 | convolution fusion | flops 452984832 | bytes 9441792 | tf_op jit(solution)/shard_map/dot_general | solution.py:147
  89.1 0.8 slice.91
  90.1 0.7 broadcast_in_dim.120
  90.8 5.1 %all-to-all-start.2 = ((f32[4,128,128]{2,1,0:T(8,128)}), f32[4,128,128]{2,1,0:T(8,128)S(1)}, u32[]{:S(2)}, u32[]{:S(2)}) async-start(f32[4,128,128]{2,1,0:T(8,128)} %broadcast_in_dim.120), calls=%async_computation.3 | async-start | bytes 524288 | tf_op jit(solution)/shard_map/all_to_all | solution.py:161
  95.9 13.3 %all-to-all-done.2 = f32[4,128,128]{2,1,0:T(8,128)S(1)} async-done(((f32[4,128,128]{2,1,0:T(8,128)}), f32[4,128,128]{2,1,0:T(8,128)S(1)}, u32[]{:S(2)}, u32[]{:S(2)}) %all-to-all-start.2) | async-done | bytes 262176 | tf_op jit(solution)/shard_map/all_to_all | solution.py:161
  109.2 1.1 broadcast_in_dim.121
  110.3 4.5 %all-to-all-start.3 = ((f32[8,2,128,128]{3,2,1,0:T(8,128)}), f32[8,2,128,128]{3,2,1,0:T(8,128)S(1)}, u32[]{:S(2)}, u32[]{:S(2)}) async-start(f32[8,2,128,128]{3,2,1,0:T(8,128)} %broadcast_in_dim.121), calls=%async_computation.4 | async-start | bytes 2097152 | tf_op jit(solution)/shard_map/all_to_all | solution.py:163
  114.8 0.6 gather_fusion
  115.6 0.3 copy.98
  115.9 14.3 %all-to-all-done.3 = f32[8,2,128,128]{3,2,1,0:T(8,128)S(1)} async-done(((f32[8,2,128,128]{3,2,1,0:T(8,128)}), f32[8,2,128,128]{3,2,1,0:T(8,128)S(1)}, u32[]{:S(2)}, u32[]{:S(2)}) %all-to-all-start.3) | async-done | bytes 1048608 | tf_op jit(solution)/shard_map/all_to_all | solution.py:163
  130.4 11.7 %cholesky.23 = f32[128,128]{1,0:T(8,128)S(1)} custom-call(f32[128,128]{1,0:T(8,128)S(1)} %fusion.14), custom_call_target="Cholesky" | custom-call | tf_op jit(solution)/shard_map/jit(cholesky)/cholesky | solution.py:166
  142.1 0.6 compare_reduce_fusion
  142.8 0.7 select_bitcast_fusion
  143.4 9.8 %custom-call.6 = f32[1,128,128]{1,2,0:T(8,128)S(1)} custom-call(f32[1,128,128]{2,1,0:T(8,128)S(1)} %get-tuple-element.32), custom_call_target="InvertDiagBlocksLowerTriangular" | custom-call | tf_op jit(solution)/shard_map/triangular_solve | solution.py:167
  153.2 0.2 convolution_bitcast_fusion.3
  153.5 0.6 convolution_select_fusion
  154.1 1.1 copy.81
  155.2 0.4 convolution_select_fusion.1
  155.6 0.8 copy.80
  156.4 1.8 convolution_bitcast_fusion.1
  158.2 2.0 copy.86
  160.2 42.7 %reduce-scatter.5.cloned.1.call-done = f32[24,128,128]{2,0,1:T(8,128)} async-done(((f32[96,128,128]{2,0,1:T(8,128)}), f32[24,128,128]{2,0,1:T(8,128)}) %reduce-scatter.5.cloned.1.call-update) | async-done | bytes 1572880 | tf_op jit(solution)/shard_map/reduce_scatter | solution.py:153
  203.0 0.6 broadcast_in_dim.126
  203.6 0.3 tile.4
  203.9 0.7 copy-done
  204.5 0.4 copy-done.2
  205.0 1.0 fusion.5
  206.0 2.5 %copy.87 = f32[1,32,128,128]{3,2,1,0:T(8,128)} copy(f32[1,32,128,128]{3,1,2,0:T(8,128)S(1)} %fusion.5) | data formatting | bytes 4194304 | tf_op jit(solution)/shard_map/broadcast_in_dim | solution.py:193
  (58 shorter events, 1.5 us)
Async XLA Ops:
  9.9 21.3 %all-to-all-start = ((f32[8,2,136,128]{3,2,1,0:T(8,128)}), f32[8,2,136,128]{3,2,1,0:T(8,128)S(1)}, u32[]{:S(2)}, u32[]{:S(2)}) async-start(f32[8,2,136,128]{3,2,1,0:T(8,128)} %pad_maximum_fusion), calls=%async_computation | async-start | bytes 2228224 | tf_op jit(solution)/shard_map/all_to_all | solution.py:122
  15.0 74.1 %reduce-scatter.3.cloned.1.call-start = ((), (), s32[]{:S(2)}) async-start(), calls=%async_computation.6 | async-start | bytes 2949120 | tf_op jit(solution)/shard_map/reduce_scatter | solution.py:153
  38.3 42.3 %all-to-all-start.1 = ((f32[8,6,128,128]{2,3,1,0:T(8,128)}), f32[8,6,128,128]{2,3,1,0:T(8,128)}, u32[]{:S(2)}, u32[]{:S(2)}) async-start(f32[8,6,128,128]{2,3,1,0:T(8,128)} %convolution_bitcast_fusion), calls=%async_computation.2 | async-start | bytes 6291456 | tf_op jit(solution)/shard_map/all_to_all | solution.py:122
  42.8 160.2 %reduce-scatter.5.cloned.1.call-start = ((), (), s32[]{:S(2)}) async-start(), calls=%async_computation.7 | async-start | bytes 7864320 | tf_op jit(solution)/shard_map/reduce_scatter | solution.py:153
  90.8 24.0 %copy-start.4 = (f32[4096]{0:T(1024)S(1)}, f32[4096]{0:T(1024)}, u32[]{:S(2)}) copy-start(f32[4096]{0:T(1024)} %param.7) | copy-start | bytes 49156
  90.8 18.4 %all-to-all-start.2 = ((f32[4,128,128]{2,1,0:T(8,128)}), f32[4,128,128]{2,1,0:T(8,128)S(1)}, u32[]{:S(2)}, u32[]{:S(2)}) async-start(f32[4,128,128]{2,1,0:T(8,128)} %broadcast_in_dim.120), calls=%async_computation.3 | async-start | bytes 524288 | tf_op jit(solution)/shard_map/all_to_all | solution.py:161
  109.2 6.4 %slice-start = ((f32[9,128,128]{2,1,0:T(8,128)}), f32[8,128,128]{2,1,0:T(8,128)S(1)}, s32[]{:S(2)}) async-start(f32[9,128,128]{2,1,0:T(8,128)} %reduce-scatter.3.cloned.1.call-done), calls=%async_computation.8 | async-start | bytes 1048576 | tf_op jit(solution)/shard_map/slice | solution.py:154
  110.3 19.9 %all-to-all-start.3 = ((f32[8,2,128,128]{3,2,1,0:T(8,128)}), f32[8,2,128,128]{3,2,1,0:T(8,128)S(1)}, u32[]{:S(2)}, u32[]{:S(2)}) async-start(f32[8,2,128,128]{3,2,1,0:T(8,128)} %broadcast_in_dim.121), calls=%async_computation.4 | async-start | bytes 2097152 | tf_op jit(solution)/shard_map/all_to_all | solution.py:163
  158.2 44.7 %copy-start.1 = (f32[8,128,128]{2,0,1:T(8,128)S(1)}, f32[8,128,128]{2,0,1:T(8,128)}, u32[]{:S(2)}) copy-start(f32[8,128,128]{2,0,1:T(8,128)} %copy.81) | copy-start | bytes 1572868
  160.2 43.4 %copy-start.3 = (f32[4,128,128]{1,0,2:T(4,128)S(1)}, f32[4,128,128]{1,0,2:T(4,128)}, u32[]{:S(2)}) copy-start(f32[4,128,128]{1,0,2:T(4,128)} %copy.80) | copy-start | bytes 786436
  202.9 1.6 copy-start
  203.0 2.0 copy-start.2
Sparse Core Ops, SparseCore 0:
  36.1 47.4 reduce-scatter.2
  89.2 113.6 reduce-scatter.4

commit v11 on v10

--- a/solution.py
+++ b/solution.py
@@ -92,8 +92,8 @@
     member = lax.axis_index("mem")
     group = lax.axis_index("grp")
     per_row = NB // ACT
-    sizes = (2, 6)
-    starts = (0, 2)
+    sizes = (1, 2, 5)
+    starts = (0, 1, 3)
     row_count = design.shape[0]
     divisor = jnp.float32(row_count * n_grp * n_mem // 16)
     eye = jnp.eye(BLK, dtype=jnp.float32)

time: 217 us -> 210 us (0.968)
  waiting for transfers between devices: 124 us -> 115 us
  starting transfers between devices: 19.2 us -> 22.4 us
  other arithmetic: 26.7 us -> 29.8 us
  local copies, waits for them, and re-layouts: 19 us -> 16.3 us
    all_to_all x1, waiting for transfers between devices: 13.3 us -> 6.77 us  [on_device_fast(): lax.all_to_all(spread, 'grp', split_axis=0, concat_axis=0, tiled=True)]
    reduce_scatter x2 -> x3, waiting for transfers between devices: 42.8 us -> 36.8 us  [on_device_fast(): got = lax.psum_scatter(send, 'grp', scatter_dimension=0, tiled=True)]
    all_to_all x2 -> x3, starting transfers between devices: 9.61 us -> 13.1 us  [on_device_fast(): lax.all_to_all(piece, 'mem', split_axis=0, concat_axis=0, tiled=True)]
    dot_general x1 -> x2, local copies, waits for them, and re-layouts: 1.88 us -> 5.25 us  [on_device_fast(): jnp.dot(sel.reshape(n_grp * width, n_mem * per_chunk).astype(jnp.float32)...]
    all_to_all x2 -> x3, waiting for transfers between devices: 53.3 us -> 56.6 us  [on_device_fast(): lax.all_to_all(piece, 'mem', split_axis=0, concat_axis=0, tiled=True)]
    broadcast_in_dim x2 -> x1, local copies, waits for them, and re-layouts: 3.15 us -> 0.01 us  [on_device_fast(): id_rows = jnp.broadcast_to(id_rows[None, None], (n_mem, 1, 8, BLK))]
    broadcast_in_dim x1, other arithmetic: 1.03 us -> 4.03 us  [on_device_fast(): return tiles[None]]
    dot_general x2 -> x3, matrix products: 7.24 us -> 6.09 us  [on_device_fast(): jnp.dot(sel.reshape(n_grp * width, n_mem * per_chunk).astype(jnp.float32)...]
  transfers between devices with their start and end apart: 6 -> 8, of which waited for: 5 -> 6; matrix products, arithmetic and copies ran while one was open for 21% -> 23% of each run, Pallas kernels for 0% -> 0%
where the time goes in v11:
time: 210 us
  waiting for transfers between devices  115 us (55%)
  other arithmetic  29.8 us (14%)
  starting transfers between devices  22.4 us (11%)
  local copies, waits for them, and re-layouts  16.3 us (8%)
  between operations  13.4 us (6%)
  matrix products  12.8 us (6%)
    all_to_all x3, waiting for transfers between devices, on_device_fast(): lax.all_to_all(piece, 'mem', split_axis=0, concat_axis=0, tiled=True)  56.6 us
    reduce_scatter x3, waiting for transfers between devices, on_device_fast(): got = lax.psum_scatter(send, 'grp', scatter_dimension=0, tiled=True)  36.8 us
    all_to_all x1, waiting for transfers between devices, on_device_fast(): pairs = lax.all_to_all(pair, 'mem', split_axis=0, concat_axis=0, tiled=True)  14.6 us
    all_to_all x3, starting transfers between devices, on_device_fast(): lax.all_to_all(piece, 'mem', split_axis=0, concat_axis=0, tiled=True)  13.1 us
    another operation x3, other arithmetic, on_device_fast(): chol = jnp.linalg.cholesky(a00)  12.5 us
    another operation x2, other arithmetic, on_device_fast(): lax.linalg.triangular_solve(chol, eye, left_side=True, lower=True)  10.5 us
    all_to_all x1, waiting for transfers between devices, on_device_fast(): lax.all_to_all(spread, 'grp', split_axis=0, concat_axis=0, tiled=True)  6.77 us
    dot_general x3, matrix products, on_device_fast(): jnp.dot(sel.reshape(n_grp * width, n_mem * per_chunk).astype(jnp.float32)...  6.09 us
  transfers between devices with their start and end apart: 8, of which 6 were waited for; matrix products, arithmetic and copies ran while one was open for 23% of the time, Pallas kernels for 0%

profile of v11, /device:TPU:0, one launch (start us, length us, event | category | flops | bytes accessed | tf_op | source)
XLA Modules:
  0.0 209.8 jit_solution(8545373896436228726)
XLA Ops:
  6.5 0.7 convert_element_type.27
  7.2 1.2 copy.52
  8.4 0.3 convolution_bitcast_fusion.3
  8.8 0.8 maximum_bitcast_fusion
  9.6 5.2 %all-to-all-start = ((f32[8,1,136,128]{3,2,1,0:T(8,128)}), f32[8,1,136,128]{3,2,1,0:T(8,128)S(1)}, u32[]{:S(2)}, u32[]{:S(2)}) async-start(f32[8,1,136,128]{3,2,1,0:T(8,128)} %maximum_bitcast_fusion), calls=%async_computation | async-start | bytes 1114112 | tf_op jit(solution)/shard_map/all_to_all | solution.py:122
  14.8 10.0 %all-to-all-done = f32[8,1,136,128]{3,2,1,0:T(8,128)S(1)} async-done(((f32[8,1,136,128]{3,2,1,0:T(8,128)}), f32[8,1,136,128]{3,2,1,0:T(8,128)S(1)}, u32[]{:S(2)}, u32[]{:S(2)}) %all-to-all-start) | async-done | bytes 557088 | tf_op jit(solution)/shard_map/all_to_all | solution.py:122
  24.9 0.1 slice_reduce_fusion
  25.1 0.1 fusion.22
  25.2 0.2 select_reduce_fusion.1
  25.4 0.1 copy.56
  25.9 0.7 fusion.10
  26.6 1.3 copy.57
  28.0 1.3 convolution_bitcast_fusion.2
  29.3 3.6 %all-to-all-start.1 = ((f32[8,2,128,128]{2,3,1,0:T(8,128)}), f32[8,2,128,128]{2,3,1,0:T(8,128)S(1)}, u32[]{:S(2)}, u32[]{:S(2)}) async-start(f32[8,2,128,128]{2,3,1,0:T(8,128)} %convolution_bitcast_fusion.2), calls=%async_computation.2 | async-start | bytes 2097152 | tf_op jit(solution)/shard_map/all_to_all | solution.py:122
  33.2 0.1 broadcast_and_fusion.1
  33.3 0.1 reshape.514
  33.4 14.8 %all-to-all-done.1 = f32[8,2,128,128]{2,3,1,0:T(8,128)S(1)} async-done(((f32[8,2,128,128]{2,3,1,0:T(8,128)}), f32[8,2,128,128]{2,3,1,0:T(8,128)S(1)}, u32[]{:S(2)}, u32[]{:S(2)}) %all-to-all-start.1) | async-done | bytes 1048608 | tf_op jit(solution)/shard_map/all_to_all | solution.py:122
  48.2 0.3 copy.64
  48.5 2.4 %fusion.7 = f32[32,128,128]{2,0,1:T(8,128)} fusion(pred[32,16,1]{0,1,2:T(8,128)(4,1)S(1)} %reshape.514, f32[2,8,128,128]{3,2,1,0:T(8,128)S(1)} %bitcast.139), kind=kOutput, calls=%fused_computation.19 | convolution fusion | flops 50331648 | bytes 3146240 | tf_op jit(solution)/shard_map/dot_general | solution.py:147
  51.0 2.1 %convolution_bitcast_fusion = f32[8,5,128,128]{2,3,1,0:T(8,128)} fusion(bf16[256,8,128,1]{0,2,3,1:T(8,128)(2,1)S(1)} %bitcast.137, bf16[256,8,128]{0,2,1:T(8,128)(2,1)S(1)} %bitcast.136), kind=kOutput, calls=%fused_computation.11 | convolution fusion | flops 335544320 | bytes 3473408 | tf_op jit(solution)/shard_map/nak,nbl->bakl/dot_general | solution.py:114
  53.1 4.4 %all-to-all-start.2 = ((f32[8,5,128,128]{2,3,1,0:T(8,128)}), f32[8,5,128,128]{2,3,1,0:T(8,128)}, u32[]{:S(2)}, u32[]{:S(2)}) async-start(f32[8,5,128,128]{2,3,1,0:T(8,128)} %convolution_bitcast_fusion), calls=%async_computation.3 | async-start | bytes 5242880 | tf_op jit(solution)/shard_map/all_to_all | solution.py:122
  57.7 0.1 broadcast_and_fusion
  57.8 0.2 and.268
  58.0 31.8 %all-to-all-done.2 = f32[8,5,128,128]{2,3,1,0:T(8,128)} async-done(((f32[8,5,128,128]{2,3,1,0:T(8,128)}), f32[8,5,128,128]{2,3,1,0:T(8,128)}, u32[]{:S(2)}, u32[]{:S(2)}) %all-to-all-start.2) | async-done | bytes 2621472 | tf_op jit(solution)/shard_map/all_to_all | solution.py:122
  89.8 2.1 %copy.66 = f32[8,5,128,128]{3,2,1,0:T(8,128)S(1)} copy(f32[8,5,128,128]{2,3,1,0:T(8,128)} %all-to-all-done.2) | data formatting | bytes 5242880 | tf_op jit(solution)/shard_map/all_to_all | solution.py:122
  91.9 3.0 %fusion = f32[80,128,128]{2,0,1:T(8,128)S(1)} fusion(pred[80,40]{1,0:T(8,128)(4,1)S(1)} %and.268, f32[5,8,128,128]{3,2,1,0:T(8,128)S(1)} %bitcast.138), kind=kOutput, calls=%fused_computation.3 | convolution fusion | flops 314572800 | bytes 7867520 | tf_op jit(solution)/shard_map/dot_general | solution.py:147
  94.9 3.9 %copy.69 = f32[80,128,128]{2,1,0:T(8,128)} copy(f32[80,128,128]{2,0,1:T(8,128)S(1)} %fusion) | data formatting | bytes 10485760 | tf_op jit(solution)/shard_map/dot_general | solution.py:147
  98.9 0.8 slice.99
  99.8 0.7 broadcast_in_dim.85
  100.6 5.0 %all-to-all-start.3 = ((f32[4,128,128]{2,1,0:T(8,128)}), f32[4,128,128]{2,1,0:T(8,128)S(1)}, u32[]{:S(2)}, u32[]{:S(2)}) async-start(f32[4,128,128]{2,1,0:T(8,128)} %broadcast_in_dim.85), calls=%async_computation.4 | async-start | bytes 524288 | tf_op jit(solution)/shard_map/all_to_all | solution.py:161
  105.6 6.8 %all-to-all-done.3 = f32[4,128,128]{2,1,0:T(8,128)S(1)} async-done(((f32[4,128,128]{2,1,0:T(8,128)}), f32[4,128,128]{2,1,0:T(8,128)S(1)}, u32[]{:S(2)}, u32[]{:S(2)}) %all-to-all-start.3) | async-done | bytes 262176 | tf_op jit(solution)/shard_map/all_to_all | solution.py:161
  112.4 1.1 broadcast_in_dim.130
  113.5 4.2 %all-to-all-start.4 = ((f32[8,2,128,128]{3,2,1,0:T(8,128)}), f32[8,2,128,128]{3,2,1,0:T(8,128)S(1)}, u32[]{:S(2)}, u32[]{:S(2)}) async-start(f32[8,2,128,128]{3,2,1,0:T(8,128)} %broadcast_in_dim.130), calls=%async_computation.5 | async-start | bytes 2097152 | tf_op jit(solution)/shard_map/all_to_all | solution.py:163
  117.7 0.6 gather_fusion
  118.4 14.6 %all-to-all-done.4 = f32[8,2,128,128]{3,2,1,0:T(8,128)S(1)} async-done(((f32[8,2,128,128]{3,2,1,0:T(8,128)}), f32[8,2,128,128]{3,2,1,0:T(8,128)S(1)}, u32[]{:S(2)}, u32[]{:S(2)}) %all-to-all-start.4) | async-done | bytes 1048608 | tf_op jit(solution)/shard_map/all_to_all | solution.py:163
  133.2 11.7 %cholesky.23 = f32[128,128]{1,0:T(8,128)S(1)} custom-call(f32[128,128]{1,0:T(8,128)S(1)} %fusion.16), custom_call_target="Cholesky" | custom-call | tf_op jit(solution)/shard_map/jit(cholesky)/cholesky | solution.py:166
  145.0 0.7 compare_reduce_fusion
  145.7 0.7 select_bitcast_fusion
  146.4 9.8 %custom-call.6 = f32[1,128,128]{1,2,0:T(8,128)S(1)} custom-call(f32[1,128,128]{2,1,0:T(8,128)S(1)} %get-tuple-element.34), custom_call_target="InvertDiagBlocksLowerTriangular" | custom-call | tf_op jit(solution)/shard_map/triangular_solve | solution.py:167
  156.2 0.2 convolution_bitcast_fusion.4
  156.5 0.4 convolution_select_fusion.1
  156.9 0.1 copy.62
  157.0 0.6 convolution_select_fusion
  157.6 1.8 convolution_bitcast_fusion.1
  159.4 1.9 copy.71
  161.3 1.2 copy.70
  162.4 36.8 %reduce-scatter.8.cloned.1.call-done = f32[20,128,128]{2,1,0:T(8,128)} async-done(((f32[80,128,128]{2,1,0:T(8,128)}), f32[20,128,128]{2,1,0:T(8,128)}) %reduce-scatter.8.cloned.1.call-update) | async-done | bytes 1310736 | tf_op jit(solution)/shard_map/reduce_scatter | solution.py:153
  199.2 4.0 %fusion.5 = f32[1,32,128,128]{3,2,1,0:T(8,128)} fusion(f32[20,128,128]{2,1,0:T(8,128)} %reduce-scatter.8.cloned.1.call-done, f32[8,128,128]{2,1,0:T(8,128)S(1)} %copy.70, f32[4,128,128]{2,1,0:T(8,128)S(1)} %slice-done, f32[8,4,128,128]{3,2,1,0:T(8,128)} %copy.71, f32[32]{0:T(128)S(1)} %get-tuple-element.36, f32[32,128]{1,0:T(8,128)S(1)} %broadcast_select_fusion, ...), kind=kLoop, calls=%fused_computation.8 | loop fusion | flops 5242880 | bytes 7160032 | tf_op jit(solution)/shard_map/broadcast_in_dim | solution.py:193
  (52 shorter events, 1.5 us)
Async XLA Ops:
  9.6 15.3 %all-to-all-start = ((f32[8,1,136,128]{3,2,1,0:T(8,128)}), f32[8,1,136,128]{3,2,1,0:T(8,128)S(1)}, u32[]{:S(2)}, u32[]{:S(2)}) async-start(f32[8,1,136,128]{3,2,1,0:T(8,128)} %maximum_bitcast_fusion), calls=%async_computation | async-start | bytes 1114112 | tf_op jit(solution)/shard_map/all_to_all | solution.py:122
  14.8 84.1 %reduce-scatter.4.cloned.1.call-start = ((), (), s32[]{:S(2)}) async-start(), calls=%async_computation.8 | async-start | bytes 1638400 | tf_op jit(solution)/shard_map/reduce_scatter | solution.py:153
  29.3 18.9 %all-to-all-start.1 = ((f32[8,2,128,128]{2,3,1,0:T(8,128)}), f32[8,2,128,128]{2,3,1,0:T(8,128)S(1)}, u32[]{:S(2)}, u32[]{:S(2)}) async-start(f32[8,2,128,128]{2,3,1,0:T(8,128)} %convolution_bitcast_fusion.2), calls=%async_computation.2 | async-start | bytes 2097152 | tf_op jit(solution)/shard_map/all_to_all | solution.py:122
  32.9 128.4 %reduce-scatter.6.cloned.1.call-start = ((), (), s32[]{:S(2)}) async-start(), calls=%async_computation.9 | async-start | bytes 2621440 | tf_op jit(solution)/shard_map/reduce_scatter | solution.py:153
  53.1 36.7 %all-to-all-start.2 = ((f32[8,5,128,128]{2,3,1,0:T(8,128)}), f32[8,5,128,128]{2,3,1,0:T(8,128)}, u32[]{:S(2)}, u32[]{:S(2)}) async-start(f32[8,5,128,128]{2,3,1,0:T(8,128)} %convolution_bitcast_fusion), calls=%async_computation.3 | async-start | bytes 5242880 | tf_op jit(solution)/shard_map/all_to_all | solution.py:122
  57.5 141.7 %reduce-scatter.8.cloned.1.call-start = ((), (), s32[]{:S(2)}) async-start(), calls=%async_computation.10 | async-start | bytes 6553600 | tf_op jit(solution)/shard_map/reduce_scatter | solution.py:153
  100.6 17.1 %copy-start = (f32[4096]{0:T(1024)S(1)}, f32[4096]{0:T(1024)}, u32[]{:S(2)}) copy-start(f32[4096]{0:T(1024)} %param.7) | copy-start | bytes 49156
  100.6 11.8 %all-to-all-start.3 = ((f32[4,128,128]{2,1,0:T(8,128)}), f32[4,128,128]{2,1,0:T(8,128)S(1)}, u32[]{:S(2)}, u32[]{:S(2)}) async-start(f32[4,128,128]{2,1,0:T(8,128)} %broadcast_in_dim.85), calls=%async_computation.4 | async-start | bytes 524288 | tf_op jit(solution)/shard_map/all_to_all | solution.py:161
  113.5 19.6 %all-to-all-start.4 = ((f32[8,2,128,128]{3,2,1,0:T(8,128)}), f32[8,2,128,128]{3,2,1,0:T(8,128)S(1)}, u32[]{:S(2)}, u32[]{:S(2)}) async-start(f32[8,2,128,128]{3,2,1,0:T(8,128)} %broadcast_in_dim.130), calls=%async_computation.5 | async-start | bytes 2097152 | tf_op jit(solution)/shard_map/all_to_all | solution.py:163
  159.4 39.8 %slice-start = ((f32[5,128,128]{2,1,0:T(8,128)}), f32[4,128,128]{2,1,0:T(8,128)S(1)}, s32[]{:S(2)}) async-start(f32[5,128,128]{2,1,0:T(8,128)} %reduce-scatter.4.cloned.1.call-done), calls=%async_computation.11 | async-start | bytes 524288 | tf_op jit(solution)/shard_map/slice | solution.py:154
Sparse Core Ops, SparseCore 0:
  28.1 30.5 reduce-scatter.3
  61.0 42.6 reduce-scatter.5
  106.1 93.0 reduce-scatter.7

commit v12 on v7

--- a/solution.py
+++ b/solution.py
@@ -92,9 +92,9 @@
     member = lax.axis_index("mem")
     group = lax.axis_index("grp")
     per_row = NB // ACT
-    sizes = (1, 2, 2, 3)
-    starts = (0, 1, 3, 5)
-    tail = starts[-1]
+    sizes = (1, 3, 4)
+    starts = (0, 1, 4)
+    tail = 5
     row_count = design.shape[0]
     divisor = jnp.float32(row_count * n_grp * n_mem // 16)
     eye = jnp.eye(BLK, dtype=jnp.float32)
@@ -115,13 +115,14 @@
         rows_at = [[(b + lo + dl) % ACT for dl in range(per_chunk)] for b in range(n_mem)]
         left = blocks[:, jnp.array(rows_at, dtype=jnp.int32)]
         piece = jnp.einsum("nbdk,nbl->bdkl", left, blocks, preferred_element_type=jnp.float32)
-        if k == 1:
+        if k == 0:
             row0 = jnp.einsum("nk,nbl->bkl", blocks[:, 0], blocks, preferred_element_type=jnp.float32)
             piece = jnp.concatenate([piece, row0[:, None]], axis=1)
         if prev is not None:
             piece, prev = lax.optimization_barrier((piece, prev))
         else:
-            piece = jnp.concatenate([piece, id_rows], axis=2)
+            ids_here = jnp.broadcast_to(id_rows, (n_mem, piece.shape[1], 8, BLK))
+            piece = jnp.concatenate([piece, ids_here], axis=2)
         got_piece = lax.all_to_all(piece, "mem", split_axis=0, concat_axis=0, tiled=True)
         if prev is None:
             everyone = got_piece[:, 0, BLK, :ACT].astype(jnp.int32)
@@ -129,7 +130,7 @@
             row_grp = everyone // 8
             col_grp = jnp.take(everyone, member, axis=1) // 8
             zero_on = everyone[:, 0] == 0
-        if k == 1:
+        if k == 0:
             row0_got = got_piece[:, per_chunk]
             got_piece = got_piece[:, :per_chunk]
         prev = got_piece
@@ -141,11 +142,13 @@
             & (rg[None, None, None, :, :] == grp_ids[:, None, None, None, None])
             & (col_grp[None, None, None, :, None] == q_ids[None, None, :, None, None])
         )
-        if lo >= tail:
-            sel = jnp.stack([sel[g][:, [q for q in range(per_row) if q != g]] for g in range(n_grp)])
-        kept = sel.shape[2]
-        sel = sel.reshape(n_grp, per_chunk * kept, n_mem * per_chunk)
-        if k == 1:
+        keep = [
+            [(dl, q) for dl in range(per_chunk) for q in range(per_row) if not (lo + dl >= tail and q == g)]
+            for g in range(n_grp)
+        ]
+        sel = jnp.stack([jnp.stack([sel[g, dl, q] for dl, q in keep[g]]) for g in range(n_grp)])
+        kept_rows = sel.shape[1]
+        if k == 0:
             col_sel = (
                 (col_grp[None, :] == grp_ids[:, None]) & zero_on[None, :]
             ).astype(jnp.float32)
@@ -154,23 +157,25 @@
                 preferred_element_type=jnp.float32,
             ).reshape(n_grp, 1, BLK * BLK)
         send = jnp.dot(
-            sel.reshape(n_grp * per_chunk * kept, n_mem * per_chunk).astype(jnp.float32),
+            sel.reshape(n_grp * kept_rows, n_mem * per_chunk).astype(jnp.float32),
             flat,
-            precision=HI,
+            precision=lax.Precision.HIGH,
             preferred_element_type=jnp.float32,
-        ).reshape(n_grp, per_chunk * kept, BLK * BLK)
-        if k == 1:
+        ).reshape(n_grp, kept_rows, BLK * BLK)
+        if k == 0:
             send = jnp.concatenate([send, col_part], axis=1)
         width = send.shape[1]
         got = lax.psum_scatter(
             send.reshape(n_grp * width, BLK, BLK), "grp", scatter_dimension=0, tiled=True
         )
-        if k == 1:
-            col_tile = jnp.transpose(got[per_chunk * kept]) / divisor
-            got = got[: per_chunk * kept]
-        got = got.reshape(per_chunk, kept, BLK, BLK)
+        if k == 0:
+            col_tile = jnp.transpose(got[kept_rows]) / divisor
+            got = got[:kept_rows]
+        pos = 0
         for dl in range(per_chunk):
-            by_d[lo + dl] = got[dl]
+            width_d = per_row - 1 if lo + dl >= tail else per_row
+            by_d[lo + dl] = got[pos:pos + width_d]
+            pos += width_d
 
     for d in range(tail, ACT):
         shift = ACT - d

time: 229 us -> 232 us (1.013)
  other arithmetic: 47.8 us -> 37.1 us
  waiting for transfers between devices: 83.1 us -> 93.6 us
  local copies, waits for them, and re-layouts: 41.1 us -> 46.2 us
    all_to_all x1, waiting for transfers between devices: 0.01 us -> 13.9 us  [on_device_fast(): pairs = lax.all_to_all(pair, 'mem', split_axis=0, concat_axis=0, tiled=True)]
    all_to_all x4 -> x3, waiting for transfers between devices: 53.8 us -> 39.9 us  [on_device_fast(): lax.all_to_all(piece, 'mem', split_axis=0, concat_axis=0, tiled=True)]
    unnamed x40 -> x43, local copies, waits for them, and re-layouts: 7.16 us -> 18.7 us
    reduce_scatter x4 -> x3, waiting for transfers between devices: 18.6 us -> 24.6 us  [on_device_fast(): lax.psum_scatter(send.reshape(n_grp * width, BLK, BLK), 'grp', scatter_di...]
    slice x6 -> x1, local copies, waits for them, and re-layouts: 7.19 us -> 1.3 us  [on_device_fast(): by_d[lo + dl] = got[pos:pos + width_d]]
    all_to_all x1, waiting for transfers between devices: 10.6 us -> 15.2 us  [on_device_fast(): lax.all_to_all(spread, 'grp', split_axis=0, concat_axis=0, tiled=True)]
    all_to_all x4 -> x3, starting transfers between devices: 16 us -> 13.1 us  [on_device_fast(): lax.all_to_all(piece, 'mem', split_axis=0, concat_axis=0, tiled=True)]
    transpose x3, other arithmetic: 2.73 us -> 0.04 us  [on_device_fast(): src_tile = jnp.transpose(jnp.take(by_d[shift], group, axis=0))]
  transfers between devices with their start and end apart: 13 -> 11, of which waited for: 7 -> 6; matrix products, arithmetic and copies ran while one was open for 41% -> 36% of each run, Pallas kernels for 0% -> 0%
where the time goes in v12:
time: 232 us; the launch traced here: 231 us
  waiting for transfers between devices  93.6 us (40%)
  local copies, waits for them, and re-layouts  46.2 us (20%)
  other arithmetic  37.1 us (16%)
  starting transfers between devices  24 us (10%)
  matrix products  16 us (7%)
  between operations  13.8 us (6%)
    all_to_all x3, waiting for transfers between devices, on_device_fast(): lax.all_to_all(piece, 'mem', split_axis=0, concat_axis=0, tiled=True)  39.9 us
    reduce_scatter x3, waiting for transfers between devices, on_device_fast(): lax.psum_scatter(send.reshape(n_grp * width, BLK, BLK), 'grp', scatter_di...  24.6 us
    unnamed x43, local copies, waits for them, and re-layouts  18.7 us
    all_to_all x1, waiting for transfers between devices, on_device_fast(): lax.all_to_all(spread, 'grp', split_axis=0, concat_axis=0, tiled=True)  15.2 us
    all_to_all x1, waiting for transfers between devices, on_device_fast(): pairs = lax.all_to_all(pair, 'mem', split_axis=0, concat_axis=0, tiled=True)  13.9 us
    all_to_all x3, starting transfers between devices, on_device_fast(): lax.all_to_all(piece, 'mem', split_axis=0, concat_axis=0, tiled=True)  13.1 us
    another operation x3, other arithmetic, on_device_fast(): chol = jnp.linalg.cholesky(a00)  12.4 us
    another operation x2, other arithmetic, on_device_fast(): lax.linalg.triangular_solve(chol, eye, left_side=True, lower=True)  10.5 us
  transfers between devices with their start and end apart: 11, of which 6 were waited for; matrix products, arithmetic and copies ran while one was open for 36% of the time, Pallas kernels for 0%

profile of v12, /device:TPU:0, one launch (start us, length us, event | category | flops | bytes accessed | tf_op | source)
XLA Modules:
  0.0 230.8 jit_solution(680188930435642794)
XLA Ops:
  6.5 1.2 copy.52
  9.2 1.1 copy.55
  10.3 5.2 %all-to-all-start = ((f32[8,2,136,128]{3,2,1,0:T(8,128)}), f32[8,2,136,128]{3,2,1,0:T(8,128)S(1)}, u32[]{:S(2)}, u32[]{:S(2)}) async-start(f32[8,2,136,128]{3,2,1,0:T(8,128)} %copy.55), calls=%async_computation | async-start | bytes 2228224 | tf_op jit(solution)/shard_map/all_to_all | solution.py:126
  16.2 1.7 fusion.61
  17.9 13.7 %all-to-all-done = f32[8,2,136,128]{3,2,1,0:T(8,128)S(1)} async-done(((f32[8,2,136,128]{3,2,1,0:T(8,128)}), f32[8,2,136,128]{3,2,1,0:T(8,128)S(1)}, u32[]{:S(2)}, u32[]{:S(2)}) %all-to-all-start) | async-done | bytes 1114144 | tf_op jit(solution)/shard_map/all_to_all | solution.py:126
  32.2 4.3 %all-to-all-start.1 = ((f32[8,3,128,128]{3,2,1,0:T(8,128)}), f32[8,3,128,128]{3,2,1,0:T(8,128)}, u32[]{:S(2)}, u32[]{:S(2)}) async-start(f32[8,3,128,128]{3,2,1,0:T(8,128)} %fusion.61), calls=%async_computation.2 | async-start | bytes 3145728 | tf_op jit(solution)/shard_map/all_to_all | solution.py:126
  39.4 1.7 reshape.651
  41.1 2.8 %copy.77 = f32[20,128,128]{1,2,0:T(8,128)} copy(f32[20,128,128]{2,1,0:T(8,128)} %reshape.651) | data formatting | bytes 2621440 | tf_op jit(solution)/shard_map/reshape | solution.py:169
  49.4 0.7 constant_dynamic-update-slice_fusion.2
  50.8 0.7 constant_dynamic-update-slice_fusion
  51.8 5.7 %all-to-all-done.1 = f32[8,3,128,128]{3,2,1,0:T(8,128)} async-done(((f32[8,3,128,128]{3,2,1,0:T(8,128)}), f32[8,3,128,128]{3,2,1,0:T(8,128)}, u32[]{:S(2)}, u32[]{:S(2)}) %all-to-all-start.1) | async-done | bytes 1572896 | tf_op jit(solution)/shard_map/all_to_all | solution.py:126
  57.5 3.3 %fusion.6 = f32[48,128,128]{2,0,1:T(8,128)S(1)} fusion(pred[48,24,1]{0,1,2:T(8,128)(4,1)S(1)} %reshape.867, f32[3,8,128,128]{3,2,1,0:T(8,128)} %bitcast.267), kind=kOutput, calls=%fused_computation.21 | convolution fusion | flops 113246208 | bytes 4719744 | tf_op jit(solution)/shard_map/dot_general | solution.py:159
  60.9 2.7 %copy.84 = f32[48,128,128]{2,1,0:T(8,128)} copy(f32[48,128,128]{2,0,1:T(8,128)S(1)} %fusion.6) | data formatting | bytes 6291456 | tf_op jit(solution)/shard_map/dot_general | solution.py:159
  65.0 2.0 fusion.60
  68.4 3.6 %all-to-all-start.2 = ((f32[8,4,128,128]{3,2,1,0:T(8,128)}), f32[8,4,128,128]{3,2,1,0:T(8,128)S(1)}, u32[]{:S(2)}, u32[]{:S(2)}) async-start(f32[8,4,128,128]{3,2,1,0:T(8,128)} %fusion.60), calls=%async_computation.3 | async-start | bytes 4194304 | tf_op jit(solution)/shard_map/all_to_all | solution.py:126
  72.3 0.7 constant_dynamic-update-slice_fusion.55
  78.1 20.5 %all-to-all-done.2 = f32[8,4,128,128]{3,2,1,0:T(8,128)S(1)} async-done(((f32[8,4,128,128]{3,2,1,0:T(8,128)}), f32[8,4,128,128]{3,2,1,0:T(8,128)S(1)}, u32[]{:S(2)}, u32[]{:S(2)}) %all-to-all-start.2) | async-done | bytes 2097184 | tf_op jit(solution)/shard_map/all_to_all | solution.py:126
  98.6 4.1 %fusion.3 = f32[52,128,128]{2,0,1:T(8,128)} fusion(pred[52,32,1]{0,1,2:T(32,128)(4,1)S(1)} %reshape.868, f32[4,8,128,128]{3,2,1,0:T(8,128)S(1)} %bitcast.756), kind=kOutput, calls=%fused_computation.15 | convolution fusion | flops 163577856 | bytes 5506688 | tf_op jit(solution)/shard_map/dot_general | solution.py:159
  102.7 4.5 %copy.87 = f32[52,128,128]{1,2,0:T(8,128)} copy(f32[52,128,128]{2,0,1:T(8,128)} %fusion.3) | data formatting | bytes 6815744 | tf_op jit(solution)/shard_map/dot_general | solution.py:159
  107.5 0.8 fusion.22
  108.3 0.7 broadcast_in_dim.190
  109.0 4.9 %all-to-all-start.3 = ((f32[4,128,128]{2,1,0:T(8,128)}), f32[4,128,128]{2,1,0:T(8,128)S(1)}, u32[]{:S(2)}, u32[]{:S(2)}) async-start(f32[4,128,128]{2,1,0:T(8,128)} %broadcast_in_dim.190), calls=%async_computation.4 | async-start | bytes 524288 | tf_op jit(solution)/shard_map/all_to_all | solution.py:197
  114.7 15.2 %all-to-all-done.3 = f32[4,128,128]{2,1,0:T(8,128)S(1)} async-done(((f32[4,128,128]{2,1,0:T(8,128)}), f32[4,128,128]{2,1,0:T(8,128)S(1)}, u32[]{:S(2)}, u32[]{:S(2)}) %all-to-all-start.3) | async-done | bytes 262176 | tf_op jit(solution)/shard_map/all_to_all | solution.py:197
  129.9 1.1 broadcast_in_dim.191
  131.0 3.6 %all-to-all-start.4 = ((f32[8,2,128,128]{3,2,1,0:T(8,128)}), f32[8,2,128,128]{3,2,1,0:T(8,128)S(1)}, u32[]{:S(2)}, u32[]{:S(2)}) async-start(f32[8,2,128,128]{3,2,1,0:T(8,128)} %broadcast_in_dim.191), calls=%async_computation.5 | async-start | bytes 2097152 | tf_op jit(solution)/shard_map/all_to_all | solution.py:199
  135.2 0.7 fusion.16
  135.9 13.9 %all-to-all-done.4 = f32[8,2,128,128]{3,2,1,0:T(8,128)S(1)} async-done(((f32[8,2,128,128]{3,2,1,0:T(8,128)}), f32[8,2,128,128]{3,2,1,0:T(8,128)S(1)}, u32[]{:S(2)}, u32[]{:S(2)}) %all-to-all-start.4) | async-done | bytes 1048608 | tf_op jit(solution)/shard_map/all_to_all | solution.py:199
  150.0 11.7 %cholesky.23 = f32[128,128]{1,0:T(8,128)S(1)} custom-call(f32[128,128]{1,0:T(8,128)S(1)} %fusion.24), custom_call_target="Cholesky" | custom-call | tf_op jit(solution)/shard_map/jit(cholesky)/cholesky | solution.py:202
  163.1 9.8 %custom-call.6 = f32[1,128,128]{1,2,0:T(8,128)S(1)} custom-call(f32[1,128,128]{2,1,0:T(8,128)S(1)} %get-tuple-element.59), custom_call_target="InvertDiagBlocksLowerTriangular" | custom-call | tf_op jit(solution)/shard_map/triangular_solve | solution.py:203
  175.0 1.8 convolution_bitcast_fusion
  176.8 1.8 copy.92
  178.6 1.3 fusion.59
  180.6 1.5 collective-permute-start
  182.5 0.7 constant_dynamic-update-slice_fusion.102
  183.2 0.7 constant_dynamic-update-slice_fusion.101
  184.0 0.7 constant_dynamic-update-slice_fusion.100
  184.7 24.6 %reduce-scatter.8.cloned.1.call-done = f32[13,128,128]{1,2,0:T(8,128)} async-done(((f32[52,128,128]{1,2,0:T(8,128)}), f32[13,128,128]{1,2,0:T(8,128)}) %reduce-scatter.8.cloned.1.call-update) | async-done | bytes 851984 | tf_op jit(solution)/shard_map/reduce_scatter | solution.py:168
  209.3 1.7 fusion.15
  210.9 0.9 select_bitcast_fusion.14
  211.9 0.7 fusion.17
  212.6 0.9 select_bitcast_fusion.10
  213.5 0.7 fusion.18
  214.3 0.9 select_bitcast_fusion.6
  215.2 0.7 fusion.19
  215.9 1.7 broadcast_multiply_fusion
  217.7 1.9 copy.91
  219.5 2.9 %fusion.1 = f32[32,128,128]{2,1,0:T(8,128)S(1)} fusion(f32[8,4,128,128]{3,2,1,0:T(8,128)} %copy.92, f32[32,128,128]{2,1,0:T(8,128)} %copy.91, f32[32]{0:T(128)S(1)} %get-tuple-element.198, f32[32,128]{1,0:T(8,128)S(1)} %broadcast_select_fusion, f32[128,128]{1,0:T(8,128)S(1)} %fusion.25, f32[8,128,128]{2,1,0:T(8,128)S(1)} %select_select_fusion, ...), kind=kLoop, calls=%fused_computation.12 | loop fusion | flops 3670016 | bytes 7160032 | tf_op jit(solution)/shard_map/jit(_where)/select_n | solution.py:230
  222.5 1.7 fusion.2
  (144 shorter events, 26.1 us)
Async XLA Ops:
  7.8 1.2 copy-start.6
  9.1 6.3 %copy-start.5 = (s32[24]{0:T(128)S(1)}, s32[24]{0:T(128)}, u32[]{:S(2)}) copy-start(s32[24]{0:T(128)} %constant.421) | copy-start | bytes 292
  10.3 21.3 %all-to-all-start = ((f32[8,2,136,128]{3,2,1,0:T(8,128)}), f32[8,2,136,128]{3,2,1,0:T(8,128)S(1)}, u32[]{:S(2)}, u32[]{:S(2)}) async-start(f32[8,2,136,128]{3,2,1,0:T(8,128)} %copy.55), calls=%async_computation | async-start | bytes 2228224 | tf_op jit(solution)/shard_map/all_to_all | solution.py:126
  32.2 25.4 %all-to-all-start.1 = ((f32[8,3,128,128]{3,2,1,0:T(8,128)}), f32[8,3,128,128]{3,2,1,0:T(8,128)}, u32[]{:S(2)}, u32[]{:S(2)}) async-start(f32[8,3,128,128]{3,2,1,0:T(8,128)} %fusion.61), calls=%async_computation.2 | async-start | bytes 3145728 | tf_op jit(solution)/shard_map/all_to_all | solution.py:126
  36.5 71.0 %reduce-scatter.4.cloned.1.call-start = ((), (), s32[]{:S(2)}) async-start(), calls=%async_computation.8 | async-start | bytes 1638400 | tf_op jit(solution)/shard_map/reduce_scatter | solution.py:168
  37.3 2.0 copy-start.3
  43.9 134.7 %reduce-scatter.6.cloned.1.call-start = ((), (), s32[]{:S(2)}) async-start(), calls=%async_computation.9 | async-start | bytes 3932160 | tf_op jit(solution)/shard_map/reduce_scatter | solution.py:168
  63.6 0.7 copy-start.4
  67.8 0.6 copy-start.2
  68.4 30.2 %all-to-all-start.2 = ((f32[8,4,128,128]{3,2,1,0:T(8,128)}), f32[8,4,128,128]{3,2,1,0:T(8,128)S(1)}, u32[]{:S(2)}, u32[]{:S(2)}) async-start(f32[8,4,128,128]{3,2,1,0:T(8,128)} %fusion.60), calls=%async_computation.3 | async-start | bytes 4194304 | tf_op jit(solution)/shard_map/all_to_all | solution.py:126
  72.0 137.2 %reduce-scatter.8.cloned.1.call-start = ((), (), s32[]{:S(2)}) async-start(), calls=%async_computation.10 | async-start | bytes 4259840 | tf_op jit(solution)/shard_map/reduce_scatter | solution.py:168
  107.2 6.7 %copy-start = (f32[4096]{0:T(1024)S(1)}, f32[4096]{0:T(1024)}, u32[]{:S(2)}) copy-start(f32[4096]{0:T(1024)} %param.12) | copy-start | bytes 49156
  109.0 20.8 %all-to-all-start.3 = ((f32[4,128,128]{2,1,0:T(8,128)}), f32[4,128,128]{2,1,0:T(8,128)S(1)}, u32[]{:S(2)}, u32[]{:S(2)}) async-start(f32[4,128,128]{2,1,0:T(8,128)} %broadcast_in_dim.190), calls=%async_computation.4 | async-start | bytes 524288 | tf_op jit(solution)/shard_map/all_to_all | solution.py:197
  114.0 21.2 %copy-start.1 = (f32[5,128,128]{1,2,0:T(8,128)S(1)}, f32[5,128,128]{1,2,0:T(8,128)}, u32[]{:S(2)}) copy-start(f32[5,128,128]{1,2,0:T(8,128)} %reduce-scatter.4.cloned.1.call-done) | copy-start | bytes 983044
  131.0 18.9 %all-to-all-start.4 = ((f32[8,2,128,128]{3,2,1,0:T(8,128)}), f32[8,2,128,128]{3,2,1,0:T(8,128)S(1)}, u32[]{:S(2)}, u32[]{:S(2)}) async-start(f32[8,2,128,128]{3,2,1,0:T(8,128)} %broadcast_in_dim.191), calls=%async_computation.5 | async-start | bytes 2097152 | tf_op jit(solution)/shard_map/all_to_all | solution.py:199
  179.9 34.3 %collective-permute-start.2 = (f32[128,128]{0,1:T(8,128)S(1)}, f32[128,128]{0,1:T(8,128)S(1)}, u32[]{:S(2)}, u32[]{:S(2)}) collective-permute-start(f32[128,128]{0,1:T(8,128)S(1)} %select_bitcast_fusion), channel_id=1, source_target_pairs={{0,1},{1,2},{2,3},{3,4},{4,5},{5,6},{6,7},{7,0},{8,9},{9,10},{10,1... | collective-permute-start | bytes 196616 | tf_op jit(solution)/shard_map/ppermute | solution.py:183
  180.0 32.6 %collective-permute-start.1 = (f32[128,128]{0,1:T(8,128)S(1)}, f32[128,128]{0,1:T(8,128)S(1)}, u32[]{:S(2)}, u32[]{:S(2)}) collective-permute-start(f32[128,128]{0,1:T(8,128)S(1)} %select_bitcast_fusion.1), channel_id=1, source_target_pairs={{0,2},{1,3},{2,4},{3,5},{4,6},{5,7},{6,0},{7,1},{8,10},{9,11},{10,... | collective-permute-start | bytes 196616 | tf_op jit(solution)/shard_map/ppermute | solution.py:183
  180.6 30.3 %collective-permute-start = (f32[128,128]{0,1:T(8,128)S(1)}, f32[128,128]{0,1:T(8,128)S(1)}, u32[]{:S(2)}, u32[]{:S(2)}) collective-permute-start(f32[128,128]{0,1:T(8,128)S(1)} %select_bitcast_fusion.2), channel_id=1, source_target_pairs={{0,3},{1,4},{2,5},{3,6},{4,7},{5,0},{6,1},{7,2},{8,11},{9,12},{10,... | collective-permute-start | bytes 196616 | tf_op jit(solution)/shard_map/ppermute | solution.py:183
Sparse Core Ops, SparseCore 0:
  44.0 32.7 reduce-scatter.3
  79.2 63.1 reduce-scatter.5
  144.7 64.5 reduce-scatter.7

commit v13 on v11

--- a/solution.py
+++ b/solution.py
@@ -171,7 +171,6 @@
     tile_cols = (t % per_row) * 8 + member
     same = (tile_rows == tile_cols).astype(jnp.float32)
     diag = eye[None] * jnp.take(ridge_blocks, tile_rows, axis=0)[:, None, :] * same[:, None, None]
-    tiles = owned / divisor + diag
 
     p_rows = jnp.einsum("ipr,qr->ipq", col_rows, chol_inv, precision=HI)
     p_cols = jnp.einsum("ipr,qr->ipq", col_cols, chol_inv, precision=HI)
@@ -187,9 +186,21 @@
     trailing = ((tile_rows > 0) & (tile_cols > 0))[:, None, None]
     on_column = (tile_cols == 0)[:, None, None]
     on_row = ((tile_rows == 0) & (tile_cols > 0))[:, None, None]
-    tiles = jnp.where(trailing, tiles - update, tiles)
-    tiles = jnp.where(on_column, left_tiles, tiles)
-    tiles = jnp.where(on_row, jnp.transpose(right_tiles, (0, 2, 1)), tiles)
+    flipped = jnp.transpose(right_tiles, (0, 2, 1))
+
+    def finish(lo, hi, part):
+        piece = part / divisor + diag[lo:hi]
+        piece = jnp.where(trailing[lo:hi], piece - update[lo:hi], piece)
+        piece = jnp.where(on_column[lo:hi], left_tiles[lo:hi], piece)
+        return jnp.where(on_row[lo:hi], flipped[lo:hi], piece)
+
+    done = []
+    first = 0
+    for part in owned_parts:
+        done.append(finish(first, first + part.shape[0], part))
+        first += part.shape[0]
+    early = lax.optimization_barrier(jnp.concatenate(done[:-1], axis=0))
+    tiles = jnp.concatenate([early, done[-1]], axis=0)
     return tiles[None]
 
 

time: 210 us -> 216 us (1.029)
  waiting for transfers between devices: 115 us -> 78.6 us
  local copies, waits for them, and re-layouts: 16.3 us -> 47.7 us
  other arithmetic: 29.8 us -> 37.5 us
    reduce_scatter x3, waiting for transfers between devices: 36.8 us -> 4.59 us  [on_device_fast(): got = lax.psum_scatter(send, 'grp', scatter_dimension=0, tiled=True)]
    slice x0 -> x18, local copies, waits for them, and re-layouts: none -> 19.1 us  [the longest x8 10.6 us: finish(): piece = jnp.where(trailing[lo:hi], piece - update[lo:hi], piece)]
    select_n x0 -> x3, other arithmetic: none -> 5.91 us  [finish(): return jnp.where(on_row[lo:hi], flipped[lo:hi], piece)]
    all_to_all x1, waiting for transfers between devices: 14.6 us -> 9.45 us  [on_device_fast(): pairs = lax.all_to_all(pair, 'mem', split_axis=0, concat_axis=0, tiled=True)]
    broadcast_in_dim x0 -> x2, local copies, waits for them, and re-layouts: none -> 3.98 us  [the longest x1 2.17 us: on_device_fast(): left_tiles = jnp.repeat(p_rows, per_row, axis=0)]
    unnamed x5 -> x38, local copies, waits for them, and re-layouts: 1.37 us -> 5.2 us
    broadcast_in_dim x1, other arithmetic: 4.03 us -> 0.22 us  [on_device_fast(): return tiles[None]]
    dot_general x2 -> x3, local copies, waits for them, and re-layouts: 5.25 us -> 7.11 us  [on_device_fast(): jnp.dot(sel.reshape(n_grp * width, n_mem * per_chunk).astype(jnp.float32)...]
  transfers between devices with their start and end apart: 8 -> 8, of which waited for: 6 -> 6; matrix products, arithmetic and copies ran while one was open for 23% -> 39% of each run, Pallas kernels for 0% -> 0%
where the time goes in v13:
time: 216 us; the launch traced here: 215 us
  waiting for transfers between devices  78.6 us (36%)
  local copies, waits for them, and re-layouts  47.7 us (22%)
  other arithmetic  37.5 us (17%)
  starting transfers between devices  23 us (11%)
  matrix products  14.1 us (7%)
  between operations  13.6 us (6%)
    all_to_all x3, waiting for transfers between devices, on_device_fast(): lax.all_to_all(piece, 'mem', split_axis=0, concat_axis=0, tiled=True)  56.6 us
    another operation x3, other arithmetic, on_device_fast(): chol = jnp.linalg.cholesky(a00)  13.3 us
    all_to_all x3, starting transfers between devices, on_device_fast(): lax.all_to_all(piece, 'mem', split_axis=0, concat_axis=0, tiled=True)  13.1 us
    another operation x2, other arithmetic, on_device_fast(): lax.linalg.triangular_solve(chol, eye, left_side=True, lower=True)  11.9 us
    slice x8, local copies, waits for them, and re-layouts, finish(): piece = jnp.where(trailing[lo:hi], piece - update[lo:hi], piece)  10.6 us
    all_to_all x1, waiting for transfers between devices, on_device_fast(): pairs = lax.all_to_all(pair, 'mem', split_axis=0, concat_axis=0, tiled=True)  9.45 us
    all_to_all x1, waiting for transfers between devices, on_device_fast(): lax.all_to_all(spread, 'grp', split_axis=0, concat_axis=0, tiled=True)  7.86 us
    slice x8, local copies, waits for them, and re-layouts, finish(): piece = jnp.where(on_column[lo:hi], left_tiles[lo:hi], piece)  7.24 us
  transfers between devices with their start and end apart: 8, of which 6 were waited for; matrix products, arithmetic and copies ran while one was open for 39% of the time, Pallas kernels for 0%

profile of v13, /device:TPU:0, one launch (start us, length us, event | category | flops | bytes accessed | tf_op | source)
XLA Modules:
  0.0 214.6 jit_solution(5708457532335783526)
XLA Ops:
  7.2 1.2 copy.67
  8.8 0.8 maximum_bitcast_fusion.1
  9.6 5.2 %all-to-all-start = ((f32[8,1,136,128]{3,2,1,0:T(8,128)}), f32[8,1,136,128]{3,2,1,0:T(8,128)S(1)}, u32[]{:S(2)}, u32[]{:S(2)}) async-start(f32[8,1,136,128]{3,2,1,0:T(8,128)} %maximum_bitcast_fusion.1), calls=%async_computation | async-start | bytes 1114112 | tf_op jit(solution)/shard_map/all_to_all | solution.py:122
  14.8 10.0 %all-to-all-done = f32[8,1,136,128]{3,2,1,0:T(8,128)S(1)} async-done(((f32[8,1,136,128]{3,2,1,0:T(8,128)}), f32[8,1,136,128]{3,2,1,0:T(8,128)S(1)}, u32[]{:S(2)}, u32[]{:S(2)}) %all-to-all-start) | async-done | bytes 557088 | tf_op jit(solution)/shard_map/all_to_all | solution.py:122
  26.6 1.3 copy.72
  27.9 1.3 convolution_bitcast_fusion.2
  29.2 3.6 %all-to-all-start.1 = ((f32[8,2,128,128]{2,3,1,0:T(8,128)}), f32[8,2,128,128]{2,3,1,0:T(8,128)S(1)}, u32[]{:S(2)}, u32[]{:S(2)}) async-start(f32[8,2,128,128]{2,3,1,0:T(8,128)} %convolution_bitcast_fusion.2), calls=%async_computation.2 | async-start | bytes 2097152 | tf_op jit(solution)/shard_map/all_to_all | solution.py:122
  33.4 14.8 %all-to-all-done.1 = f32[8,2,128,128]{2,3,1,0:T(8,128)S(1)} async-done(((f32[8,2,128,128]{2,3,1,0:T(8,128)}), f32[8,2,128,128]{2,3,1,0:T(8,128)S(1)}, u32[]{:S(2)}, u32[]{:S(2)}) %all-to-all-start.1) | async-done | bytes 1048608 | tf_op jit(solution)/shard_map/all_to_all | solution.py:122
  48.2 1.3 copy.82
  49.5 2.3 %fusion.5 = f32[32,128,128]{2,0,1:T(8,128)S(1)} fusion(pred[32,16,1]{0,1,2:T(8,128)(4,1)S(1)} %reshape.523, f32[2,8,128,128]{3,2,1,0:T(8,128)} %bitcast.153), kind=kOutput, calls=%fused_computation.19 | convolution fusion | flops 50331648 | bytes 3146240 | tf_op jit(solution)/shard_map/dot_general | solution.py:147
  51.8 1.9 copy.84
  53.7 2.1 convolution_bitcast_fusion
  55.9 4.4 %all-to-all-start.2 = ((f32[8,5,128,128]{2,3,1,0:T(8,128)}), f32[8,5,128,128]{2,3,1,0:T(8,128)}, u32[]{:S(2)}, u32[]{:S(2)}) async-start(f32[8,5,128,128]{2,3,1,0:T(8,128)} %convolution_bitcast_fusion), calls=%async_computation.3 | async-start | bytes 5242880 | tf_op jit(solution)/shard_map/all_to_all | solution.py:122
  60.7 31.8 %all-to-all-done.2 = f32[8,5,128,128]{2,3,1,0:T(8,128)} async-done(((f32[8,5,128,128]{2,3,1,0:T(8,128)}), f32[8,5,128,128]{2,3,1,0:T(8,128)}, u32[]{:S(2)}, u32[]{:S(2)}) %all-to-all-start.2) | async-done | bytes 2621472 | tf_op jit(solution)/shard_map/all_to_all | solution.py:122
  92.5 2.1 %copy.87 = f32[8,5,128,128]{3,2,1,0:T(8,128)S(1)} copy(f32[8,5,128,128]{2,3,1,0:T(8,128)} %all-to-all-done.2) | data formatting | bytes 5242880 | tf_op jit(solution)/shard_map/all_to_all | solution.py:122
  94.7 3.0 %fusion = f32[80,128,128]{2,0,1:T(8,128)S(1)} fusion(pred[80,40]{1,0:T(8,128)(4,1)S(1)} %and.236, f32[5,8,128,128]{3,2,1,0:T(8,128)S(1)} %bitcast.147), kind=kOutput, calls=%fused_computation.2 | convolution fusion | flops 314572800 | bytes 7867520 | tf_op jit(solution)/shard_map/dot_general | solution.py:147
  97.7 3.9 %copy.90 = f32[80,128,128]{2,1,0:T(8,128)} copy(f32[80,128,128]{2,0,1:T(8,128)S(1)} %fusion) | data formatting | bytes 10485760 | tf_op jit(solution)/shard_map/dot_general | solution.py:147
  101.7 0.8 slice.222
  103.3 4.9 %all-to-all-start.3 = ((f32[4,128,128]{2,1,0:T(8,128)}), f32[4,128,128]{2,1,0:T(8,128)S(1)}, u32[]{:S(2)}, u32[]{:S(2)}) async-start(f32[4,128,128]{2,1,0:T(8,128)} %broadcast_in_dim.167), calls=%async_computation.4 | async-start | bytes 524288 | tf_op jit(solution)/shard_map/all_to_all | solution.py:161
  112.1 7.9 %all-to-all-done.3 = f32[4,128,128]{2,1,0:T(8,128)S(1)} async-done(((f32[4,128,128]{2,1,0:T(8,128)}), f32[4,128,128]{2,1,0:T(8,128)S(1)}, u32[]{:S(2)}, u32[]{:S(2)}) %all-to-all-start.3) | async-done | bytes 262176 | tf_op jit(solution)/shard_map/all_to_all | solution.py:161
  120.0 1.1 broadcast_in_dim.168
  121.0 4.9 %all-to-all-start.4 = ((f32[8,2,128,128]{3,2,1,0:T(8,128)}), f32[8,2,128,128]{3,2,1,0:T(8,128)S(1)}, u32[]{:S(2)}, u32[]{:S(2)}) async-start(f32[8,2,128,128]{3,2,1,0:T(8,128)} %broadcast_in_dim.168), calls=%async_computation.5 | async-start | bytes 2097152 | tf_op jit(solution)/shard_map/all_to_all | solution.py:163
  128.4 1.7 slice.230
  130.1 1.8 copy.107
  131.9 9.5 %all-to-all-done.4 = f32[8,2,128,128]{3,2,1,0:T(8,128)S(1)} async-done(((f32[8,2,128,128]{3,2,1,0:T(8,128)}), f32[8,2,128,128]{3,2,1,0:T(8,128)S(1)}, u32[]{:S(2)}, u32[]{:S(2)}) %all-to-all-start.4) | async-done | bytes 1048608 | tf_op jit(solution)/shard_map/all_to_all | solution.py:163
  142.1 12.5 %cholesky.23 = f32[128,128]{1,0:T(8,128)S(1)} custom-call(f32[128,128]{1,0:T(8,128)} %fusion.18), custom_call_target="Cholesky" | custom-call | tf_op jit(solution)/shard_map/jit(cholesky)/cholesky | solution.py:166
  155.4 1.3 select_bitcast_fusion
  156.7 10.6 %custom-call.6 = f32[1,128,128]{1,2,0:T(8,128)S(1)} custom-call(f32[1,128,128]{2,1,0:T(8,128)} %get-tuple-element.34), custom_call_target="InvertDiagBlocksLowerTriangular" | custom-call | tf_op jit(solution)/shard_map/triangular_solve | solution.py:167
  167.6 1.3 convolution_select_fusion
  169.5 0.7 slice.238
  170.2 1.0 convolution_select_fusion.1
  171.3 1.8 convolution_bitcast_fusion.1
  173.1 0.9 slice.236
  175.5 1.0 copy.80
  176.5 2.2 %broadcast_in_dim.182 = f32[5,4,128,128]{3,2,1,0:T(8,128)} broadcast(f32[5,128,128]{2,1,0:T(8,128)} %slice.238), dimensions={0,2,3} | broadcast | bytes 1638400 | tf_op jit(solution)/shard_map/broadcast_in_dim | solution.py:184
  178.7 2.9 %copy.94 = f32[20,128,128]{1,2,0:T(8,128)} copy(f32[20,128,128]{2,1,0:T(8,128)} %bitcast.151) | data formatting | bytes 2621440 | tf_op jit(solution)/shard_map/slice | solution.py:194
  181.6 2.0 copy.85
  183.7 2.0 copy.86
  185.7 1.5 copy.92
  187.2 2.8 %copy.93 = f32[20,128,128]{1,2,0:T(8,128)} copy(f32[20,128,128]{2,1,0:T(8,128)} %bitcast.152) | data formatting | bytes 2621440 | tf_op jit(solution)/shard_map/slice | solution.py:193
  190.3 1.3 copy-done
  191.6 1.8 fusion.14
  193.4 1.5 fusion.9
  195.0 1.0 pad_maximum_fusion
  196.0 4.6 %reduce-scatter.8.cloned.1.call-done = f32[20,128,128]{2,1,0:T(8,128)} async-done(((f32[80,128,128]{2,1,0:T(8,128)}), f32[20,128,128]{2,1,0:T(8,128)}) %reduce-scatter.8.cloned.1.call-update) | async-done | bytes 1310736 | tf_op jit(solution)/shard_map/reduce_scatter | solution.py:153
  200.6 2.8 %copy.91 = f32[20,128,128]{1,2,0:T(8,128)} copy(f32[20,128,128]{2,1,0:T(8,128)} %reduce-scatter.8.cloned.1.call-done) | data formatting | bytes 2621440 | tf_op jit(solution)/shard_map/reduce_scatter | solution.py:153
  203.4 2.6 %fusion.4 = f32[20,128,128]{1,2,0:T(8,128)S(1)} fusion(f32[20,128,128]{1,2,0:T(8,128)S(1)} %copy-done.2, f32[20,128,128]{1,2,0:T(8,128)} %copy.93, f32[32,128,128]{1,2,0:T(8,128)S(1)} %multiply_multiply_fusion, f32[32,128,128]{1,2,0:T(8,128)} %bitcast.150, f32[20,128,128]{1,2,0:T(8,128)} %copy.91, pred[20]{0:T(512)(128)(4,1)S(1)} %copy-done.13, ...), kind=kLoop, calls=%fused_computation.12 | loop fusion | flops 1966080 | bytes 7864380 | tf_op jit(solution)/shard_map/jit(_where)/select_n | solution.py:195
  206.2 1.8 copy.95
  (110 shorter events, 15.3 us)
Async XLA Ops:
  9.6 15.3 %all-to-all-start = ((f32[8,1,136,128]{3,2,1,0:T(8,128)}), f32[8,1,136,128]{3,2,1,0:T(8,128)S(1)}, u32[]{:S(2)}, u32[]{:S(2)}) async-start(f32[8,1,136,128]{3,2,1,0:T(8,128)} %maximum_bitcast_fusion.1), calls=%async_computation | async-start | bytes 1114112 | tf_op jit(solution)/shard_map/all_to_all | solution.py:122
  14.8 86.9 %reduce-scatter.4.cloned.1.call-start = ((), (), s32[]{:S(2)}) async-start(), calls=%async_computation.8 | async-start | bytes 1638400 | tf_op jit(solution)/shard_map/reduce_scatter | solution.py:153
  29.2 18.9 %all-to-all-start.1 = ((f32[8,2,128,128]{2,3,1,0:T(8,128)}), f32[8,2,128,128]{2,3,1,0:T(8,128)S(1)}, u32[]{:S(2)}, u32[]{:S(2)}) async-start(f32[8,2,128,128]{2,3,1,0:T(8,128)} %convolution_bitcast_fusion.2), calls=%async_computation.2 | async-start | bytes 2097152 | tf_op jit(solution)/shard_map/all_to_all | solution.py:122
  32.8 160.6 %reduce-scatter.6.cloned.1.call-start = ((), (), s32[]{:S(2)}) async-start(), calls=%async_computation.9 | async-start | bytes 2621440 | tf_op jit(solution)/shard_map/reduce_scatter | solution.py:153
  55.9 36.7 %all-to-all-start.2 = ((f32[8,5,128,128]{2,3,1,0:T(8,128)}), f32[8,5,128,128]{2,3,1,0:T(8,128)}, u32[]{:S(2)}, u32[]{:S(2)}) async-start(f32[8,5,128,128]{2,3,1,0:T(8,128)} %convolution_bitcast_fusion), calls=%async_computation.3 | async-start | bytes 5242880 | tf_op jit(solution)/shard_map/all_to_all | solution.py:122
  60.3 140.3 %reduce-scatter.8.cloned.1.call-start = ((), (), s32[]{:S(2)}) async-start(), calls=%async_computation.10 | async-start | bytes 6553600 | tf_op jit(solution)/shard_map/reduce_scatter | solution.py:153
  101.6 10.4 %copy-start.7 = (f32[4096]{0:T(1024)S(1)}, f32[4096]{0:T(1024)}, u32[]{:S(2)}) copy-start(f32[4096]{0:T(1024)} %param.7) | copy-start | bytes 49156
  103.3 16.6 %all-to-all-start.3 = ((f32[4,128,128]{2,1,0:T(8,128)}), f32[4,128,128]{2,1,0:T(8,128)S(1)}, u32[]{:S(2)}, u32[]{:S(2)}) async-start(f32[4,128,128]{2,1,0:T(8,128)} %broadcast_in_dim.167), calls=%async_computation.4 | async-start | bytes 524288 | tf_op jit(solution)/shard_map/all_to_all | solution.py:161
  121.0 20.3 %all-to-all-start.4 = ((f32[8,2,128,128]{3,2,1,0:T(8,128)}), f32[8,2,128,128]{3,2,1,0:T(8,128)S(1)}, u32[]{:S(2)}, u32[]{:S(2)}) async-start(f32[8,2,128,128]{3,2,1,0:T(8,128)} %broadcast_in_dim.168), calls=%async_computation.5 | async-start | bytes 2097152 | tf_op jit(solution)/shard_map/all_to_all | solution.py:163
  171.3 1.8 copy-start.4
  173.1 1.6 copy-start.1
  187.2 2.9 %copy-start.5 = (f32[4,128,128]{2,1,0:T(8,128)S(1)}, f32[4,128,128]{2,1,0:T(8,128)}, u32[]{:S(2)}) copy-start(f32[4,128,128]{2,1,0:T(8,128)} %copy-done.4) | copy-start | bytes 786436
  187.2 4.4 %copy-start.8 = (f32[4,128,128]{1,2,0:T(8,128)S(1)}, f32[4,128,128]{1,2,0:T(8,128)}, u32[]{:S(2)}) copy-start(f32[4,128,128]{1,2,0:T(8,128)} %copy.107) | copy-start | bytes 786436
  187.2 4.4 %copy-start.10 = (f32[128,128]{0,1:T(8,128)S(1)}, f32[128,128]{0,1:T(8,128)}, u32[]{:S(2)}) copy-start(f32[128,128]{0,1:T(8,128)} %copy.77) | copy-start | bytes 196612
  190.0 3.4 %copy-start.6 = (f32[8,128,128]{1,2,0:T(8,128)S(1)}, f32[8,128,128]{1,2,0:T(8,128)}, u32[]{:S(2)}) copy-start(f32[8,128,128]{1,2,0:T(8,128)} %copy.86) | copy-start | bytes 1572868
  190.0 3.4 %copy-start.14 = (pred[8]{0:T(512)(128)(4,1)S(1)}, pred[8]{0:T(512)(128)(4,1)}, u32[]{:S(2)}) copy-start(pred[8]{0:T(512)(128)(4,1)} %slice.190) | copy-start | bytes 28
  190.0 3.4 %copy-start.15 = (pred[8]{0:T(512)(128)(4,1)S(1)}, pred[8]{0:T(512)(128)(4,1)}, u32[]{:S(2)}) copy-start(pred[8]{0:T(512)(128)(4,1)} %slice.192) | copy-start | bytes 28
  190.0 3.4 %copy-start.16 = (pred[8]{0:T(512)(128)(4,1)S(1)}, pred[8]{0:T(512)(128)(4,1)}, u32[]{:S(2)}) copy-start(pred[8]{0:T(512)(128)(4,1)} %slice.195) | copy-start | bytes 28
  190.3 1.3 copy-start
  193.4 1.6 copy-start.9
  195.0 8.4 %copy-start.2 = (f32[20,128,128]{1,2,0:T(8,128)S(1)}, f32[20,128,128]{1,2,0:T(8,128)}, u32[]{:S(2)}) copy-start(f32[20,128,128]{1,2,0:T(8,128)} %copy.94) | copy-start | bytes 3932164
  195.0 8.4 %copy-start.11 = (pred[20]{0:T(512)(128)(4,1)S(1)}, pred[20]{0:T(512)(128)(4,1)}, u32[]{:S(2)}) copy-start(pred[20]{0:T(512)(128)(4,1)} %slice.200) | copy-start | bytes 64
  195.0 8.4 %copy-start.12 = (pred[20]{0:T(512)(128)(4,1)S(1)}, pred[20]{0:T(512)(128)(4,1)}, u32[]{:S(2)}) copy-start(pred[20]{0:T(512)(128)(4,1)} %slice.202) | copy-start | bytes 64
  195.0 8.4 %copy-start.13 = (pred[20]{0:T(512)(128)(4,1)S(1)}, pred[20]{0:T(512)(128)(4,1)}, u32[]{:S(2)}) copy-start(pred[20]{0:T(512)(128)(4,1)} %slice.205) | copy-start | bytes 64
  203.4 2.6 %copy-start.3 = (f32[12,128,128]{1,2,0:T(8,128)S(1)}, f32[12,128,128]{1,2,0:T(8,128)}, u32[]{:S(2)}) copy-start(f32[12,128,128]{1,2,0:T(8,128)} %pad_maximum_fusion) | copy-start | bytes 2359300
Sparse Core Ops, SparseCore 0:
  28.1 30.5 reduce-scatter.3
  61.0 42.6 reduce-scatter.5
  106.1 94.4 reduce-scatter.7

commit v14 on v11

--- a/solution.py
+++ b/solution.py
@@ -171,7 +171,6 @@
     tile_cols = (t % per_row) * 8 + member
     same = (tile_rows == tile_cols).astype(jnp.float32)
     diag = eye[None] * jnp.take(ridge_blocks, tile_rows, axis=0)[:, None, :] * same[:, None, None]
-    tiles = owned / divisor + diag
 
     p_rows = jnp.einsum("ipr,qr->ipq", col_rows, chol_inv, precision=HI)
     p_cols = jnp.einsum("ipr,qr->ipq", col_cols, chol_inv, precision=HI)
@@ -187,9 +186,11 @@
     trailing = ((tile_rows > 0) & (tile_cols > 0))[:, None, None]
     on_column = (tile_cols == 0)[:, None, None]
     on_row = ((tile_rows == 0) & (tile_cols > 0))[:, None, None]
-    tiles = jnp.where(trailing, tiles - update, tiles)
-    tiles = jnp.where(on_column, left_tiles, tiles)
-    tiles = jnp.where(on_row, jnp.transpose(right_tiles, (0, 2, 1)), tiles)
+    addend = jnp.where(trailing, diag - update, diag)
+    replaced = on_column | on_row
+    override = jnp.where(on_column, left_tiles, jnp.transpose(right_tiles, (0, 2, 1)))
+    addend, override = lax.optimization_barrier((addend, override))
+    tiles = jnp.where(replaced, override, owned / divisor + addend)
     return tiles[None]
 
 

time: 210 us -> 211 us (level)
  waiting for transfers between devices: 115 us -> 110 us
  other arithmetic: 29.8 us -> 33.2 us
    reduce_scatter x3, waiting for transfers between devices: 36.8 us -> 32.2 us  [on_device_fast(): got = lax.psum_scatter(send, 'grp', scatter_dimension=0, tiled=True)]
    select_n x0 -> x2, other arithmetic: none -> 3.32 us  [the longest x1 1.77 us: on_device_fast(): addend = jnp.where(trailing, diag - update, diag)]
  transfers between devices with their start and end apart: 8 -> 8, of which waited for: 6 -> 6; matrix products, arithmetic and copies ran while one was open for 23% -> 25% of each run, Pallas kernels for 0% -> 0%
where the time goes in v14:
time: 211 us; the launch traced here: 210 us
  waiting for transfers between devices  110 us (52%)
  other arithmetic  33.2 us (16%)
  starting transfers between devices  22.4 us (11%)
  local copies, waits for them, and re-layouts  16.3 us (8%)
  matrix products  14.2 us (7%)
  between operations  13.4 us (6%)
    all_to_all x3, waiting for transfers between devices, on_device_fast(): lax.all_to_all(piece, 'mem', split_axis=0, concat_axis=0, tiled=True)  56.6 us
    reduce_scatter x3, waiting for transfers between devices, on_device_fast(): got = lax.psum_scatter(send, 'grp', scatter_dimension=0, tiled=True)  32.2 us
    all_to_all x1, waiting for transfers between devices, on_device_fast(): pairs = lax.all_to_all(pair, 'mem', split_axis=0, concat_axis=0, tiled=True)  14.6 us
    all_to_all x3, starting transfers between devices, on_device_fast(): lax.all_to_all(piece, 'mem', split_axis=0, concat_axis=0, tiled=True)  13.1 us
    another operation x3, other arithmetic, on_device_fast(): chol = jnp.linalg.cholesky(a00)  12.4 us
    another operation x2, other arithmetic, on_device_fast(): lax.linalg.triangular_solve(chol, eye, left_side=True, lower=True)  10.5 us
    all_to_all x1, waiting for transfers between devices, on_device_fast(): lax.all_to_all(spread, 'grp', split_axis=0, concat_axis=0, tiled=True)  6.75 us
    dot_general x3, matrix products, on_device_fast(): jnp.dot(sel.reshape(n_grp * width, n_mem * per_chunk).astype(jnp.float32)...  6.13 us
  transfers between devices with their start and end apart: 8, of which 6 were waited for; matrix products, arithmetic and copies ran while one was open for 25% of the time, Pallas kernels for 0%

profile of v14, /device:TPU:0, one launch (start us, length us, event | category | flops | bytes accessed | tf_op | source)
XLA Modules:
  0.0 209.9 jit_solution(11555679260462697949)
XLA Ops:
  6.5 0.7 convert_element_type.29
  7.2 1.2 copy.33
  8.4 0.3 convolution_bitcast_fusion.3
  8.8 0.8 maximum_bitcast_fusion
  9.6 5.2 %all-to-all-start = ((f32[8,1,136,128]{3,2,1,0:T(8,128)}), f32[8,1,136,128]{3,2,1,0:T(8,128)S(1)}, u32[]{:S(2)}, u32[]{:S(2)}) async-start(f32[8,1,136,128]{3,2,1,0:T(8,128)} %maximum_bitcast_fusion), calls=%async_computation | async-start | bytes 1114112 | tf_op jit(solution)/shard_map/all_to_all | solution.py:122
  14.8 10.0 %all-to-all-done = f32[8,1,136,128]{3,2,1,0:T(8,128)S(1)} async-done(((f32[8,1,136,128]{3,2,1,0:T(8,128)}), f32[8,1,136,128]{3,2,1,0:T(8,128)S(1)}, u32[]{:S(2)}, u32[]{:S(2)}) %all-to-all-start) | async-done | bytes 557088 | tf_op jit(solution)/shard_map/all_to_all | solution.py:122
  24.9 0.1 slice_reduce_fusion
  25.1 0.1 fusion.21
  25.2 0.2 select_reduce_fusion.1
  25.9 0.7 fusion.9
  26.6 1.3 copy.38
  27.9 1.3 convolution_bitcast_fusion.2
  29.3 3.6 %all-to-all-start.1 = ((f32[8,2,128,128]{2,3,1,0:T(8,128)}), f32[8,2,128,128]{2,3,1,0:T(8,128)S(1)}, u32[]{:S(2)}, u32[]{:S(2)}) async-start(f32[8,2,128,128]{2,3,1,0:T(8,128)} %convolution_bitcast_fusion.2), calls=%async_computation.2 | async-start | bytes 2097152 | tf_op jit(solution)/shard_map/all_to_all | solution.py:122
  33.1 0.1 broadcast_and_fusion.1
  33.4 14.8 %all-to-all-done.1 = f32[8,2,128,128]{2,3,1,0:T(8,128)S(1)} async-done(((f32[8,2,128,128]{2,3,1,0:T(8,128)}), f32[8,2,128,128]{2,3,1,0:T(8,128)S(1)}, u32[]{:S(2)}, u32[]{:S(2)}) %all-to-all-start.1) | async-done | bytes 1048608 | tf_op jit(solution)/shard_map/all_to_all | solution.py:122
  48.2 0.3 copy.46
  48.5 2.5 %fusion.6 = f32[32,128,128]{2,0,1:T(8,128)} fusion(pred[32,16,1]{0,1,2:T(8,128)(4,1)S(1)} %reshape.518, f32[2,8,128,128]{3,2,1,0:T(8,128)S(1)} %bitcast.139), kind=kOutput, calls=%fused_computation.19 | convolution fusion | flops 50331648 | bytes 3146240 | tf_op jit(solution)/shard_map/dot_general | solution.py:147
  51.0 2.1 %convolution_bitcast_fusion = f32[8,5,128,128]{2,3,1,0:T(8,128)} fusion(bf16[256,8,128,1]{0,2,3,1:T(8,128)(2,1)S(1)} %bitcast.137, bf16[256,8,128]{0,2,1:T(8,128)(2,1)S(1)} %bitcast.136), kind=kOutput, calls=%fused_computation.11 | convolution fusion | flops 335544320 | bytes 3473408 | tf_op jit(solution)/shard_map/nak,nbl->bakl/dot_general | solution.py:114
  53.1 4.4 %all-to-all-start.2 = ((f32[8,5,128,128]{2,3,1,0:T(8,128)}), f32[8,5,128,128]{2,3,1,0:T(8,128)}, u32[]{:S(2)}, u32[]{:S(2)}) async-start(f32[8,5,128,128]{2,3,1,0:T(8,128)} %convolution_bitcast_fusion), calls=%async_computation.3 | async-start | bytes 5242880 | tf_op jit(solution)/shard_map/all_to_all | solution.py:122
  57.7 0.1 broadcast_and_fusion
  57.8 0.2 and.270
  58.0 31.8 %all-to-all-done.2 = f32[8,5,128,128]{2,3,1,0:T(8,128)} async-done(((f32[8,5,128,128]{2,3,1,0:T(8,128)}), f32[8,5,128,128]{2,3,1,0:T(8,128)}, u32[]{:S(2)}, u32[]{:S(2)}) %all-to-all-start.2) | async-done | bytes 2621472 | tf_op jit(solution)/shard_map/all_to_all | solution.py:122
  89.8 2.1 %copy.48 = f32[8,5,128,128]{3,2,1,0:T(8,128)S(1)} copy(f32[8,5,128,128]{2,3,1,0:T(8,128)} %all-to-all-done.2) | data formatting | bytes 5242880 | tf_op jit(solution)/shard_map/all_to_all | solution.py:122
  91.9 3.0 %fusion = f32[80,128,128]{2,0,1:T(8,128)S(1)} fusion(pred[80,40]{1,0:T(8,128)(4,1)S(1)} %and.270, f32[5,8,128,128]{3,2,1,0:T(8,128)S(1)} %bitcast.138), kind=kOutput, calls=%fused_computation.3 | convolution fusion | flops 314572800 | bytes 7867520 | tf_op jit(solution)/shard_map/dot_general | solution.py:147
  94.9 3.9 %copy.51 = f32[80,128,128]{2,1,0:T(8,128)} copy(f32[80,128,128]{2,0,1:T(8,128)S(1)} %fusion) | data formatting | bytes 10485760 | tf_op jit(solution)/shard_map/dot_general | solution.py:147
  98.9 0.8 slice.99
  99.9 0.7 broadcast_in_dim.132
  100.6 5.0 %all-to-all-start.3 = ((f32[4,128,128]{2,1,0:T(8,128)}), f32[4,128,128]{2,1,0:T(8,128)S(1)}, u32[]{:S(2)}, u32[]{:S(2)}) async-start(f32[4,128,128]{2,1,0:T(8,128)} %broadcast_in_dim.132), calls=%async_computation.4 | async-start | bytes 524288 | tf_op jit(solution)/shard_map/all_to_all | solution.py:161
  105.6 6.8 %all-to-all-done.3 = f32[4,128,128]{2,1,0:T(8,128)S(1)} async-done(((f32[4,128,128]{2,1,0:T(8,128)}), f32[4,128,128]{2,1,0:T(8,128)S(1)}, u32[]{:S(2)}, u32[]{:S(2)}) %all-to-all-start.3) | async-done | bytes 262176 | tf_op jit(solution)/shard_map/all_to_all | solution.py:161
  112.4 1.1 broadcast_in_dim.133
  113.4 4.2 %all-to-all-start.4 = ((f32[8,2,128,128]{3,2,1,0:T(8,128)}), f32[8,2,128,128]{3,2,1,0:T(8,128)S(1)}, u32[]{:S(2)}, u32[]{:S(2)}) async-start(f32[8,2,128,128]{3,2,1,0:T(8,128)} %broadcast_in_dim.133), calls=%async_computation.5 | async-start | bytes 2097152 | tf_op jit(solution)/shard_map/all_to_all | solution.py:163
  117.7 0.6 gather_fusion
  118.4 14.6 %all-to-all-done.4 = f32[8,2,128,128]{3,2,1,0:T(8,128)S(1)} async-done(((f32[8,2,128,128]{3,2,1,0:T(8,128)}), f32[8,2,128,128]{3,2,1,0:T(8,128)S(1)}, u32[]{:S(2)}, u32[]{:S(2)}) %all-to-all-start.4) | async-done | bytes 1048608 | tf_op jit(solution)/shard_map/all_to_all | solution.py:163
  133.2 11.7 %cholesky.13 = f32[128,128]{1,0:T(8,128)S(1)} custom-call(f32[128,128]{1,0:T(8,128)S(1)} %fusion.15), custom_call_target="Cholesky" | custom-call | tf_op jit(solution)/shard_map/jit(cholesky)/cholesky | solution.py:166
  145.0 0.6 compare_reduce_fusion
  145.6 0.7 select_bitcast_fusion
  146.3 9.8 %custom-call.6 = f32[1,128,128]{1,2,0:T(8,128)S(1)} custom-call(f32[1,128,128]{2,1,0:T(8,128)S(1)} %get-tuple-element.38), custom_call_target="InvertDiagBlocksLowerTriangular" | custom-call | tf_op jit(solution)/shard_map/triangular_solve | solution.py:167
  156.1 0.2 convolution_bitcast_fusion.4
  156.3 0.4 convolution_select_fusion.1
  156.7 0.1 copy.44
  156.8 0.6 convolution_select_fusion
  157.4 3.1 %convolution_bitcast_fusion.1 = f32[8,4,128,128]{2,3,0,1:T(8,128)} fusion(f32[8,128,128]{2,1,0:T(8,128)S(1)} %convolution_select_fusion, f32[4,128,128]{2,1,0:T(8,128)S(1)} %convolution_select_fusion.1), kind=kOutput, calls=%fused_computation.12 | convolution fusion | flops 805306368 | bytes 2883584 | tf_op jit(solution)/shard_map/apr,qsr->aqps/dot_general | solution.py:182
  160.6 2.0 copy.43
  162.5 1.5 bitcast_select_fusion
  164.1 1.8 subtract_select_fusion
  165.9 1.1 copy.52
  167.0 32.2 %reduce-scatter.8.cloned.1.call-done = f32[20,128,128]{2,1,0:T(8,128)} async-done(((f32[80,128,128]{2,1,0:T(8,128)}), f32[20,128,128]{2,1,0:T(8,128)}) %reduce-scatter.8.cloned.1.call-update) | async-done | bytes 1310736 | tf_op jit(solution)/shard_map/reduce_scatter | solution.py:153
  199.2 4.2 %fusion.5 = f32[1,32,128,128]{3,2,1,0:T(8,128)} fusion(f32[32,128,128]{2,1,0:T(8,128)} %bitcast_select_fusion, f32[32,128,128]{2,1,0:T(8,128)} %subtract_select_fusion, f32[20,128,128]{2,1,0:T(8,128)} %reduce-scatter.8.cloned.1.call-done, f32[8,128,128]{2,1,0:T(8,128)S(1)} %copy.52, f32[4,128,128]{2,1,0:T(8,128)S(1)} %slice-done, pred[32]{0:T(512)(128)(4,1)S(1)} %and_or_fusion), kind=kLoop, calls=%fused_computation.9 | loop fusion | flops 2621440 | bytes 8388640 | tf_op jit(solution)/shard_map/broadcast_in_dim | solution.py:194
  (55 shorter events, 1.7 us)
Async XLA Ops:
  9.6 15.3 %all-to-all-start = ((f32[8,1,136,128]{3,2,1,0:T(8,128)}), f32[8,1,136,128]{3,2,1,0:T(8,128)S(1)}, u32[]{:S(2)}, u32[]{:S(2)}) async-start(f32[8,1,136,128]{3,2,1,0:T(8,128)} %maximum_bitcast_fusion), calls=%async_computation | async-start | bytes 1114112 | tf_op jit(solution)/shard_map/all_to_all | solution.py:122
  14.8 84.1 %reduce-scatter.4.cloned.1.call-start = ((), (), s32[]{:S(2)}) async-start(), calls=%async_computation.8 | async-start | bytes 1638400 | tf_op jit(solution)/shard_map/reduce_scatter | solution.py:153
  29.3 18.9 %all-to-all-start.1 = ((f32[8,2,128,128]{2,3,1,0:T(8,128)}), f32[8,2,128,128]{2,3,1,0:T(8,128)S(1)}, u32[]{:S(2)}, u32[]{:S(2)}) async-start(f32[8,2,128,128]{2,3,1,0:T(8,128)} %convolution_bitcast_fusion.2), calls=%async_computation.2 | async-start | bytes 2097152 | tf_op jit(solution)/shard_map/all_to_all | solution.py:122
  32.8 133.0 %reduce-scatter.6.cloned.1.call-start = ((), (), s32[]{:S(2)}) async-start(), calls=%async_computation.9 | async-start | bytes 2621440 | tf_op jit(solution)/shard_map/reduce_scatter | solution.py:153
  53.1 36.7 %all-to-all-start.2 = ((f32[8,5,128,128]{2,3,1,0:T(8,128)}), f32[8,5,128,128]{2,3,1,0:T(8,128)}, u32[]{:S(2)}, u32[]{:S(2)}) async-start(f32[8,5,128,128]{2,3,1,0:T(8,128)} %convolution_bitcast_fusion), calls=%async_computation.3 | async-start | bytes 5242880 | tf_op jit(solution)/shard_map/all_to_all | solution.py:122
  57.5 141.6 %reduce-scatter.8.cloned.1.call-start = ((), (), s32[]{:S(2)}) async-start(), calls=%async_computation.10 | async-start | bytes 6553600 | tf_op jit(solution)/shard_map/reduce_scatter | solution.py:153
  100.6 17.1 %copy-start = (f32[4096]{0:T(1024)S(1)}, f32[4096]{0:T(1024)}, u32[]{:S(2)}) copy-start(f32[4096]{0:T(1024)} %param.7) | copy-start | bytes 49156
  100.6 11.8 %all-to-all-start.3 = ((f32[4,128,128]{2,1,0:T(8,128)}), f32[4,128,128]{2,1,0:T(8,128)S(1)}, u32[]{:S(2)}, u32[]{:S(2)}) async-start(f32[4,128,128]{2,1,0:T(8,128)} %broadcast_in_dim.132), calls=%async_computation.4 | async-start | bytes 524288 | tf_op jit(solution)/shard_map/all_to_all | solution.py:161
  113.4 19.6 %all-to-all-start.4 = ((f32[8,2,128,128]{3,2,1,0:T(8,128)}), f32[8,2,128,128]{3,2,1,0:T(8,128)S(1)}, u32[]{:S(2)}, u32[]{:S(2)}) async-start(f32[8,2,128,128]{3,2,1,0:T(8,128)} %broadcast_in_dim.133), calls=%async_computation.5 | async-start | bytes 2097152 | tf_op jit(solution)/shard_map/all_to_all | solution.py:163
  164.1 35.1 %slice-start = ((f32[5,128,128]{2,1,0:T(8,128)}), f32[4,128,128]{2,1,0:T(8,128)S(1)}, s32[]{:S(2)}) async-start(f32[5,128,128]{2,1,0:T(8,128)} %reduce-scatter.4.cloned.1.call-done), calls=%async_computation.11 | async-start | bytes 524288 | tf_op jit(solution)/shard_map/slice | solution.py:154
Sparse Core Ops, SparseCore 0:
  28.1 30.6 reduce-scatter.3
  61.0 42.6 reduce-scatter.5
  106.1 93.0 reduce-scatter.7

commit v15 on v14

--- a/solution.py
+++ b/solution.py
@@ -144,12 +144,13 @@
             ).reshape(n_grp, 1, n_mem * per_chunk)
             sel = jnp.concatenate([sel, col_sel], axis=1)
         width = sel.shape[1]
-        send = jnp.dot(
+        send = jnp.einsum(
+            "rs,skl->rkl",
             sel.reshape(n_grp * width, n_mem * per_chunk).astype(jnp.float32),
-            got_piece.reshape(n_mem * per_chunk, BLK * BLK),
+            got_piece.reshape(n_mem * per_chunk, BLK, BLK),
             precision=lax.Precision.HIGH,
             preferred_element_type=jnp.float32,
-        ).reshape(n_grp * width, BLK, BLK)
+        )
         got = lax.psum_scatter(send, "grp", scatter_dimension=0, tiled=True)
         owned_parts.append(got[: per_chunk * per_row])
         if k == 0:

time: 211 us -> 211 us (level)
    reshape x0 -> x2, local copies, waits for them, and re-layouts: none -> 3.06 us  [on_device_fast(): got_piece.reshape(n_mem * per_chunk, BLK, BLK)]
    all_to_all x2 -> x0, local copies, waits for them, and re-layouts: 2.48 us -> none  [on_device_fast(): lax.all_to_all(piece, 'mem', split_axis=0, concat_axis=0, tiled=True)]
where the time goes in v15:
time: 211 us; the launch traced here: 210 us
  waiting for transfers between devices  111 us (53%)
  other arithmetic  33.2 us (16%)
  starting transfers between devices  21.7 us (10%)
  local copies, waits for them, and re-layouts  18.4 us (9%)
  between operations  13.4 us (6%)
  matrix products  12.5 us (6%)
    all_to_all x3, waiting for transfers between devices, on_device_fast(): lax.all_to_all(piece, 'mem', split_axis=0, concat_axis=0, tiled=True)  56.6 us
    reduce_scatter x3, waiting for transfers between devices, on_device_fast(): got = lax.psum_scatter(send, 'grp', scatter_dimension=0, tiled=True)  32.7 us
    all_to_all x1, waiting for transfers between devices, on_device_fast(): pairs = lax.all_to_all(pair, 'mem', split_axis=0, concat_axis=0, tiled=True)  14.6 us
    another operation x3, other arithmetic, on_device_fast(): chol = jnp.linalg.cholesky(a00)  12.4 us
    all_to_all x3, starting transfers between devices, on_device_fast(): lax.all_to_all(piece, 'mem', split_axis=0, concat_axis=0, tiled=True)  12.4 us
    another operation x2, other arithmetic, on_device_fast(): lax.linalg.triangular_solve(chol, eye, left_side=True, lower=True)  10.5 us
    all_to_all x1, waiting for transfers between devices, on_device_fast(): lax.all_to_all(spread, 'grp', split_axis=0, concat_axis=0, tiled=True)  6.75 us
    dot_general x2, local copies, waits for them, and re-layouts, on_device_fast(): jnp.einsum('rs,skl->rkl', sel.reshape(n_grp * width, n_mem * per_chunk).a...  5.2 us
  transfers between devices with their start and end apart: 8, of which 6 were waited for; matrix products, arithmetic and copies ran while one was open for 25% of the time, Pallas kernels for 0%

profile of v15, /device:TPU:0, one launch (start us, length us, event | category | flops | bytes accessed | tf_op | source)
XLA Modules:
  0.0 209.9 jit_solution(11500473714339276290)
XLA Ops:
  6.5 0.7 convert_element_type.29
  7.2 1.2 copy.35
  8.4 0.3 convolution_bitcast_fusion.3
  8.8 0.8 maximum_bitcast_fusion
  9.6 5.2 %all-to-all-start = ((f32[8,1,136,128]{3,2,1,0:T(8,128)}), f32[8,1,136,128]{3,2,1,0:T(8,128)S(1)}, u32[]{:S(2)}, u32[]{:S(2)}) async-start(f32[8,1,136,128]{3,2,1,0:T(8,128)} %maximum_bitcast_fusion), calls=%async_computation | async-start | bytes 1114112 | tf_op jit(solution)/shard_map/all_to_all | solution.py:122
  14.8 10.0 %all-to-all-done = f32[8,1,136,128]{3,2,1,0:T(8,128)S(1)} async-done(((f32[8,1,136,128]{3,2,1,0:T(8,128)}), f32[8,1,136,128]{3,2,1,0:T(8,128)S(1)}, u32[]{:S(2)}, u32[]{:S(2)}) %all-to-all-start) | async-done | bytes 557088 | tf_op jit(solution)/shard_map/all_to_all | solution.py:122
  24.9 0.1 slice_reduce_fusion
  25.1 0.1 fusion.16
  25.2 0.2 select_reduce_fusion.1
  25.9 0.7 fusion.4
  26.6 1.3 copy.41
  27.9 1.3 convolution_bitcast_fusion.2
  29.2 3.6 %all-to-all-start.1 = ((f32[8,2,128,128]{2,3,1,0:T(8,128)}), f32[8,2,128,128]{2,3,1,0:T(8,128)S(1)}, u32[]{:S(2)}, u32[]{:S(2)}) async-start(f32[8,2,128,128]{2,3,1,0:T(8,128)} %convolution_bitcast_fusion.2), calls=%async_computation.2 | async-start | bytes 2097152 | tf_op jit(solution)/shard_map/all_to_all | solution.py:122
  33.1 0.1 broadcast_and_fusion.1
  33.4 14.8 %all-to-all-done.1 = f32[8,2,128,128]{2,3,1,0:T(8,128)S(1)} async-done(((f32[8,2,128,128]{2,3,1,0:T(8,128)}), f32[8,2,128,128]{2,3,1,0:T(8,128)S(1)}, u32[]{:S(2)}, u32[]{:S(2)}) %all-to-all-start.1) | async-done | bytes 1048608 | tf_op jit(solution)/shard_map/all_to_all | solution.py:122
  48.2 0.5 copy.49
  48.7 2.1 %fusion.23 = f32[32,128,128]{2,0,1:T(8,128)} fusion(pred[32,16,1]{0,1,2:T(8,128)(4,1)S(1)} %reshape.512, f32[16,128,128]{2,0,1:T(8,128)S(1)} %copy.49), kind=kOutput, calls=%fused_computation.95 | convolution fusion | flops 50331648 | bytes 3146240 | tf_op jit(solution)/shard_map/rs,skl->rkl/dot_general | solution.py:147
  50.8 2.1 %convolution_bitcast_fusion = f32[8,5,128,128]{2,3,1,0:T(8,128)} fusion(bf16[256,8,128,1]{0,2,3,1:T(8,128)(2,1)S(1)} %bitcast.105, bf16[256,8,128]{0,2,1:T(8,128)(2,1)S(1)} %bitcast.104), kind=kOutput, calls=%fused_computation.7 | convolution fusion | flops 335544320 | bytes 3473408 | tf_op jit(solution)/shard_map/nak,nbl->bakl/dot_general | solution.py:114
  52.9 3.6 %all-to-all-start.2 = ((f32[8,5,128,128]{2,3,1,0:T(8,128)}), f32[8,5,128,128]{2,3,1,0:T(8,128)S(1)}, u32[]{:S(2)}, u32[]{:S(2)}) async-start(f32[8,5,128,128]{2,3,1,0:T(8,128)} %convolution_bitcast_fusion), calls=%async_computation.3 | async-start | bytes 5242880 | tf_op jit(solution)/shard_map/all_to_all | solution.py:122
  56.9 0.2 and.270
  57.0 31.7 %all-to-all-done.2 = f32[8,5,128,128]{2,3,1,0:T(8,128)S(1)} async-done(((f32[8,5,128,128]{2,3,1,0:T(8,128)}), f32[8,5,128,128]{2,3,1,0:T(8,128)S(1)}, u32[]{:S(2)}, u32[]{:S(2)}) %all-to-all-start.2) | async-done | bytes 2621472 | tf_op jit(solution)/shard_map/all_to_all | solution.py:122
  88.8 1.5 copy-done
  90.3 2.6 %copy.51 = f32[40,128,128]{2,0,1:T(8,128)S(1)} copy(f32[40,128,128]{1,2,0:T(8,128)} %bitcast.106) | data formatting | bytes 5242880 | tf_op jit(solution)/shard_map/reshape | solution.py:150
  92.9 1.6 fusion.11
  94.4 3.9 %copy.52 = f32[80,128,128]{2,1,0:T(8,128)} copy(f32[80,128,128]{2,0,1:T(8,128)S(1)} %fusion.11) | data formatting | bytes 10485760 | tf_op jit(solution)/shard_map/rs,skl->rkl/dot_general | solution.py:147
  98.4 0.8 slice.99
  99.3 0.7 broadcast_in_dim.132
  100.1 5.0 %all-to-all-start.3 = ((f32[4,128,128]{2,1,0:T(8,128)}), f32[4,128,128]{2,1,0:T(8,128)S(1)}, u32[]{:S(2)}, u32[]{:S(2)}) async-start(f32[4,128,128]{2,1,0:T(8,128)} %broadcast_in_dim.132), calls=%async_computation.4 | async-start | bytes 524288 | tf_op jit(solution)/shard_map/all_to_all | solution.py:162
  105.1 6.8 %all-to-all-done.3 = f32[4,128,128]{2,1,0:T(8,128)S(1)} async-done(((f32[4,128,128]{2,1,0:T(8,128)}), f32[4,128,128]{2,1,0:T(8,128)S(1)}, u32[]{:S(2)}, u32[]{:S(2)}) %all-to-all-start.3) | async-done | bytes 262176 | tf_op jit(solution)/shard_map/all_to_all | solution.py:162
  111.9 1.1 broadcast_in_dim.133
  112.9 4.3 %all-to-all-start.4 = ((f32[8,2,128,128]{3,2,1,0:T(8,128)}), f32[8,2,128,128]{3,2,1,0:T(8,128)S(1)}, u32[]{:S(2)}, u32[]{:S(2)}) async-start(f32[8,2,128,128]{3,2,1,0:T(8,128)} %broadcast_in_dim.133), calls=%async_computation.5 | async-start | bytes 2097152 | tf_op jit(solution)/shard_map/all_to_all | solution.py:164
  117.2 0.6 gather_fusion
  117.9 14.6 %all-to-all-done.4 = f32[8,2,128,128]{3,2,1,0:T(8,128)S(1)} async-done(((f32[8,2,128,128]{3,2,1,0:T(8,128)}), f32[8,2,128,128]{3,2,1,0:T(8,128)S(1)}, u32[]{:S(2)}, u32[]{:S(2)}) %all-to-all-start.4) | async-done | bytes 1048608 | tf_op jit(solution)/shard_map/all_to_all | solution.py:164
  132.7 11.7 %cholesky.13 = f32[128,128]{1,0:T(8,128)S(1)} custom-call(f32[128,128]{1,0:T(8,128)S(1)} %fusion.9), custom_call_target="Cholesky" | custom-call | tf_op jit(solution)/shard_map/jit(cholesky)/cholesky | solution.py:167
  144.5 0.6 compare_reduce_fusion
  145.1 0.7 select_bitcast_fusion
  145.8 9.8 %custom-call.6 = f32[1,128,128]{1,2,0:T(8,128)S(1)} custom-call(f32[1,128,128]{2,1,0:T(8,128)S(1)} %get-tuple-element.38), custom_call_target="InvertDiagBlocksLowerTriangular" | custom-call | tf_op jit(solution)/shard_map/triangular_solve | solution.py:168
  155.6 0.2 convolution_bitcast_fusion.4
  155.9 0.4 convolution_select_fusion.1
  156.2 0.1 copy.47
  156.4 0.6 convolution_select_fusion
  157.0 3.1 %convolution_bitcast_fusion.1 = f32[8,4,128,128]{2,3,0,1:T(8,128)} fusion(f32[8,128,128]{2,1,0:T(8,128)S(1)} %convolution_select_fusion, f32[4,128,128]{2,1,0:T(8,128)S(1)} %convolution_select_fusion.1), kind=kOutput, calls=%fused_computation.8 | convolution fusion | flops 805306368 | bytes 2883584 | tf_op jit(solution)/shard_map/apr,qsr->aqps/dot_general | solution.py:183
  160.1 1.9 copy.46
  162.0 1.5 bitcast_select_fusion
  163.6 1.8 subtract_select_fusion
  165.3 1.1 copy.53
  166.5 32.7 %reduce-scatter.8.cloned.1.call-done = f32[20,128,128]{2,1,0:T(8,128)} async-done(((f32[80,128,128]{2,1,0:T(8,128)}), f32[20,128,128]{2,1,0:T(8,128)}) %reduce-scatter.8.cloned.1.call-update) | async-done | bytes 1310736 | tf_op jit(solution)/shard_map/reduce_scatter | solution.py:154
  199.2 4.2 %fusion.2 = f32[1,32,128,128]{3,2,1,0:T(8,128)} fusion(f32[32,128,128]{2,1,0:T(8,128)} %bitcast_select_fusion, f32[32,128,128]{2,1,0:T(8,128)} %subtract_select_fusion, f32[20,128,128]{2,1,0:T(8,128)} %reduce-scatter.8.cloned.1.call-done, f32[8,128,128]{2,1,0:T(8,128)S(1)} %copy.53, f32[4,128,128]{2,1,0:T(8,128)S(1)} %slice-done, pred[32]{0:T(512)(128)(4,1)S(1)} %and_or_fusion), kind=kLoop, calls=%fused_computation.5 | loop fusion | flops 2621440 | bytes 8388640 | tf_op jit(solution)/shard_map/broadcast_in_dim | solution.py:195
  (57 shorter events, 1.8 us)
Async XLA Ops:
  9.6 15.3 %all-to-all-start = ((f32[8,1,136,128]{3,2,1,0:T(8,128)}), f32[8,1,136,128]{3,2,1,0:T(8,128)S(1)}, u32[]{:S(2)}, u32[]{:S(2)}) async-start(f32[8,1,136,128]{3,2,1,0:T(8,128)} %maximum_bitcast_fusion), calls=%async_computation | async-start | bytes 1114112 | tf_op jit(solution)/shard_map/all_to_all | solution.py:122
  14.8 83.6 %reduce-scatter.4.cloned.1.call-start = ((), (), s32[]{:S(2)}) async-start(), calls=%async_computation.8 | async-start | bytes 1638400 | tf_op jit(solution)/shard_map/reduce_scatter | solution.py:154
  29.2 18.9 %all-to-all-start.1 = ((f32[8,2,128,128]{2,3,1,0:T(8,128)}), f32[8,2,128,128]{2,3,1,0:T(8,128)S(1)}, u32[]{:S(2)}, u32[]{:S(2)}) async-start(f32[8,2,128,128]{2,3,1,0:T(8,128)} %convolution_bitcast_fusion.2), calls=%async_computation.2 | async-start | bytes 2097152 | tf_op jit(solution)/shard_map/all_to_all | solution.py:122
  32.8 132.5 %reduce-scatter.6.cloned.1.call-start = ((), (), s32[]{:S(2)}) async-start(), calls=%async_computation.9 | async-start | bytes 2621440 | tf_op jit(solution)/shard_map/reduce_scatter | solution.py:154
  52.9 35.8 %all-to-all-start.2 = ((f32[8,5,128,128]{2,3,1,0:T(8,128)}), f32[8,5,128,128]{2,3,1,0:T(8,128)S(1)}, u32[]{:S(2)}, u32[]{:S(2)}) async-start(f32[8,5,128,128]{2,3,1,0:T(8,128)} %convolution_bitcast_fusion), calls=%async_computation.3 | async-start | bytes 5242880 | tf_op jit(solution)/shard_map/all_to_all | solution.py:122
  56.6 142.6 %reduce-scatter.8.cloned.1.call-start = ((), (), s32[]{:S(2)}) async-start(), calls=%async_computation.10 | async-start | bytes 6553600 | tf_op jit(solution)/shard_map/reduce_scatter | solution.py:154
  88.8 1.5 copy-start
  100.1 17.1 %copy-start.1 = (f32[4096]{0:T(1024)S(1)}, f32[4096]{0:T(1024)}, u32[]{:S(2)}) copy-start(f32[4096]{0:T(1024)} %param.7) | copy-start | bytes 49156
  100.1 11.8 %all-to-all-start.3 = ((f32[4,128,128]{2,1,0:T(8,128)}), f32[4,128,128]{2,1,0:T(8,128)S(1)}, u32[]{:S(2)}, u32[]{:S(2)}) async-start(f32[4,128,128]{2,1,0:T(8,128)} %broadcast_in_dim.132), calls=%async_computation.4 | async-start | bytes 524288 | tf_op jit(solution)/shard_map/all_to_all | solution.py:162
  112.9 19.7 %all-to-all-start.4 = ((f32[8,2,128,128]{3,2,1,0:T(8,128)}), f32[8,2,128,128]{3,2,1,0:T(8,128)S(1)}, u32[]{:S(2)}, u32[]{:S(2)}) async-start(f32[8,2,128,128]{3,2,1,0:T(8,128)} %broadcast_in_dim.133), calls=%async_computation.5 | async-start | bytes 2097152 | tf_op jit(solution)/shard_map/all_to_all | solution.py:164
  163.6 35.6 %slice-start = ((f32[5,128,128]{2,1,0:T(8,128)}), f32[4,128,128]{2,1,0:T(8,128)S(1)}, s32[]{:S(2)}) async-start(f32[5,128,128]{2,1,0:T(8,128)} %reduce-scatter.4.cloned.1.call-done), calls=%async_computation.11 | async-start | bytes 524288 | tf_op jit(solution)/shard_map/slice | solution.py:155
Sparse Core Ops, SparseCore 0:
  28.1 30.5 reduce-scatter.3
  61.0 42.6 reduce-scatter.5
  106.1 93.0 reduce-scatter.7
